TPU v7x, 512 devices: a whole 4x4x16 slice. The times are simulated.
512 devices in a mesh: rep: 8 (over y, core), expert: 64 (over x, z).
Axes of the slice: x: 4, y: 4, z: 16, core: 2. Of those that a mesh axis runs over, the one named last changes fastest.
Arguments:
- tokens: bfloat16 [8192, 4096], P('expert', 'rep')
- norm_gain: float32 [4096], P('rep'), may hold values from 0.25 to 1.75
- gate_weights: float32 [8192, 8], P('expert'), may hold values from 0.1 to 0.6
- exit_flags: int32 [8192], P('expert'), may hold values from 0 to 1, as said below
- routes: int32 [8192, 8], P('expert'), may hold values from 0 to 127, as said below
- next_device: int32 [8192], P('expert'), may hold values from 0 to 63, as said below
- up_weight: bfloat16 [128, 4096, 1024], P('expert', 'rep'), may hold values from -0.09375 to 0.09375
- down_weight: bfloat16 [128, 1024, 4096], P('expert', None, 'rep'), may hold values from -0.1875 to 0.1875
Outputs:
- handed: float32 [4096, 4096], P('expert', 'rep')
Inputs may be any that keep to these rules, and one draw needn't show every extreme that they name: `exit_flags`: one block of 128 rows holds at most 64 live rows; some block holds exactly 64. `routes`: each row names 8 different experts. Among the live rows of one block, every expert is named the same number of times up to one, so at most 4 times; a block with 64 live rows names every expert exactly 4 times. `next_device`: among the live rows of one block, every value is named the same number of times up to one, so at most 1 times.
All inputs are finite; a program needn't handle non-finite values.
Results may differ from a plain program's by a relative error of at most 0.0017.
Values may be sent and summed in bfloat16 or wider, within the bound.
No kernel may reach another device: no remote copies, remote signals or barrier semaphores. Data moves between devices by JAX's collectives and lax.ppermute only.
A program may use at most 64 MiB of HBM per device.

v0:
```python
import jax
import jax.numpy as jnp
from jax import lax
from jax.sharding import PartitionSpec as P


def per_device(
    tokens, norm_gain, gate_weights, exit_flags, routes, next_device, up_weight, down_weight
):
    row_count, feat_width = tokens.shape
    owner_count = lax.axis_size("expert")
    rep_count = lax.axis_size("rep")
    local_experts = up_weight.shape[0]
    route_count = routes.shape[1]
    experts_all = local_experts * owner_count
    most_live = row_count // 2
    capacity = route_count * most_live // experts_all
    hand_cap = (most_live + owner_count - 1) // owner_count
    slot_total = local_experts * owner_count * capacity
    widened = tokens.astype(jnp.float32)
    squares = lax.psum(jnp.sum(widened * widened, axis=1), "rep")
    rinv_rows = lax.rsqrt(squares / (feat_width * rep_count) + 1e-06)
    normed = (widened * rinv_rows[:, None] * norm_gain[None, :]).astype(jnp.bfloat16)
    survive = 1 - exit_flags
    pair_live = jnp.repeat(survive, route_count)
    route_flat = routes.reshape(-1)
    one_hot = (route_flat[:, None] == jnp.arange(experts_all, dtype=jnp.int32)[None, :]).astype(
        jnp.int32
    ) * pair_live[:, None]
    earlier = jnp.cumsum(one_hot, axis=0) - one_hot
    position = jnp.sum(earlier * one_hot, axis=1)
    owner_id = route_flat // local_experts
    local_id = route_flat % local_experts
    slot_index = (local_id * owner_count + owner_id) * capacity + position
    slot_index = jnp.where(pair_live > 0, slot_index, slot_total)
    pair_row = jnp.arange(row_count * route_count, dtype=jnp.int32) // route_count
    source_row = jnp.zeros((slot_total,), jnp.int32).at[slot_index].set(pair_row + 1, mode="drop")
    padded = jnp.concatenate([jnp.zeros((1, feat_width), jnp.bfloat16), normed], axis=0)
    outbound = padded[source_row].reshape(local_experts, owner_count, capacity, feat_width)
    received = lax.all_to_all(outbound, "expert", split_axis=1, concat_axis=1, tiled=True)
    item_count = received.shape[2]
    flattened = received.reshape(local_experts, owner_count * item_count, feat_width)
    partial_value = jnp.einsum(
        "erd,edh->erh", flattened, up_weight, preferred_element_type=jnp.float32
    )
    summed = lax.psum(partial_value, "rep")
    activated = jax.nn.silu(summed).astype(jnp.bfloat16)
    expert_out = jnp.einsum(
        "erh,ehd->erd", activated, down_weight, preferred_element_type=jnp.float32
    )
    expert_out = expert_out.astype(jnp.bfloat16).reshape(
        local_experts, owner_count, item_count, feat_width
    )
    returned = lax.all_to_all(expert_out, "expert", split_axis=1, concat_axis=1, tiled=True)
    flat_back = returned.reshape(slot_total, feat_width)
    picked = flat_back[jnp.minimum(slot_index, slot_total - 1)].reshape(
        row_count, route_count, feat_width
    )
    mixture = jnp.einsum("rk,rkd->rd", gate_weights, picked, preferred_element_type=jnp.float32)
    updated = widened + mixture
    dest_hot = (next_device[:, None] == jnp.arange(owner_count, dtype=jnp.int32)[None, :]).astype(
        jnp.int32
    ) * survive[:, None]
    dest_before = jnp.cumsum(dest_hot, axis=0) - dest_hot
    handoff_pos = jnp.sum(dest_before * dest_hot, axis=1)
    hand_slot = jnp.where(survive > 0, next_device * hand_cap + handoff_pos, owner_count * hand_cap)
    row_plus = jnp.arange(row_count, dtype=jnp.int32) + 1
    target = (
        jnp.zeros((owner_count * hand_cap,), jnp.int32).at[hand_slot].set(row_plus, mode="drop")
    )
    stacked = jnp.concatenate([jnp.zeros((1, feat_width), jnp.float32), updated], axis=0)
    leaving = stacked[target].reshape(owner_count, hand_cap, feat_width)
    arrived = lax.all_to_all(leaving, "expert", split_axis=0, concat_axis=0, tiled=True)
    return arrived.reshape(owner_count * hand_cap, feat_width)


def solution(mesh):
    in_specs = (
        P("expert", "rep"),
        P("rep"),
        P("expert", None),
        P("expert"),
        P("expert", None),
        P("expert"),
        P("expert", "rep", None),
        P("expert", None, "rep"),
    )
    out_specs = P("expert", "rep")
    return jax.shard_map(
        per_device, mesh=mesh, in_specs=in_specs, out_specs=out_specs, check_vma=False
    )
```

profile of v0, /device:TPU:6, one launch (start us, length us, event | category | flops | bytes accessed | tf_op | source)
XLA Modules:
  0.0 241.3 jit_solution(2612807899074196465)
XLA Ops:
  6.5 0.9 copy.16
  7.8 0.7 broadcast_subtract_fusion
  8.4 0.7 broadcast_compare_fusion
  9.4 0.3 fusion.3
  10.3 0.5 fusion.2
  10.8 4.3 %scatter_custom_fusion = s32[512]{0:T(512)S(1)} fusion(s32[1024]{0:T(1024)S(1)} %bitcast.29, s32[1024]{0:T(1024)S(1)} %fusion.13, s32[]{:T(128)} %constant.69.clone.1), kind=kCustom, calls=%fused_computation.56 | custom fusion | bytes 2052 | tf_op jit(solution)/shard_map/scatter | solution.py:37
  15.3 14.9 %psum.14 = f32[128]{0:T(128)S(1)} all-reduce(f32[128]{0:T(128)S(1)} %fusion.5), channel_id=1, replica_groups=mesh['rep'=8,'expert'=64] {'rep'}, use_global_device_ids=true, to_apply=%region_1.0 | all-reduce | flops 128 | bytes 1024 | tf_op jit(solution)/shard_map/psum | solution.py:21
  30.3 2.0 gather_fusion
  32.4 0.2 copy.22
  32.6 47.7 %all_to_all.15 = bf16[2,64,4,512]{3,2,0,1:T(4,128)(2,1)S(1)} all-to-all(bf16[2,64,4,512]{3,2,0,1:T(4,128)(2,1)S(1)} %copy.22), channel_id=1, replica_groups=mesh['rep'=8,'expert'=64] {'expert'}, dimensions={1} | all-to-all | bytes 1048576 | tf_op jit(solution)/shard_map/all_to_all | solution.py:40
  80.3 0.2 copy.23
  80.6 2.0 fusion.25
  82.7 72.8 %all-reduce.4.cloned.1.call-done = f32[2,256,1024]{2,1,0:T(8,128)} async-done(((f32[2,256,1024]{2,1,0:T(8,128)}), f32[2,256,1024]{2,1,0:T(8,128)}) %all-reduce.4.cloned.1.call-update) | async-done | bytes 2097168 | tf_op jit(solution)/shard_map/psum | solution.py:46
  155.4 3.0 %convolution_convert_fusion = bf16[2,256,512]{2,1,0:T(8,128)(2,1)S(1)} fusion(bf16[2,1024,512]{2,1,0:T(8,128)(2,1)} %param.15, f32[2,256,1024]{2,1,0:T(8,128)} %all-reduce.4.cloned.1.call-done), kind=kOutput, calls=%fused_computation.6 | convolution fusion | flops 539754496 | bytes 4718592 | tf_op jit(solution)/shard_map/erh,ehd->erd/dot_general | solution.py:48
  158.6 1.0 copy.24
  159.5 15.9 %all-to-all-start.1 = ((bf16[2,64,4,512]{3,2,0,1:T(4,128)(2,1)}), bf16[2,64,4,512]{3,2,0,1:T(4,128)(2,1)S(1)}, u32[]{:S(2)}, u32[]{:S(2)}) async-start(bf16[2,64,4,512]{3,2,0,1:T(4,128)(2,1)} %copy.24), calls=%async_computation.1 | async-start | bytes 1048576 | tf_op jit(solution)/shard_map/all_to_all | solution.py:54
  176.1 1.0 scatter_custom_fusion.1
  177.1 27.7 %all-to-all-done.1 = bf16[2,64,4,512]{3,2,0,1:T(4,128)(2,1)S(1)} async-done(((bf16[2,64,4,512]{3,2,0,1:T(4,128)(2,1)}), bf16[2,64,4,512]{3,2,0,1:T(4,128)(2,1)S(1)}, u32[]{:S(2)}, u32[]{:S(2)}) %all-to-all-start.1) | async-done | bytes 524320 | tf_op jit(solution)/shard_map/all_to_all | solution.py:54
  204.8 0.2 copy.25
  205.1 5.1 %gather_fusion.1 = bf16[1024,512]{1,0:T(8,128)(2,1)} fusion(bf16[512,512]{1,0:T(8,128)(2,1)S(1)} %reshape.231, s32[1024]{0:T(1024)S(1)} %broadcast_clamp_fusion), kind=kCustom, calls=%fused_computation.1 | custom fusion | bytes 2101248 | tf_op jit(solution)/shard_map/gather | solution.py:56
  210.2 1.6 fusion
  211.9 0.7 gather_fusion.2
  212.7 21.1 %all_to_all.16 = f32[64,1,512]{2,1,0:T(1,128)S(1)} all-to-all(f32[64,1,512]{2,1,0:T(1,128)S(1)} %copy.26), channel_id=1, replica_groups=mesh['rep'=8,'expert'=64] {'expert'}, dimensions={0} | all-to-all | bytes 262144 | tf_op jit(solution)/shard_map/all_to_all | solution.py:73
  233.8 0.7 copy.32
  (54 shorter events, 2.7 us)
Async XLA Ops:
  6.5 74.1 %copy-start = (bf16[2,512,1024]{2,1,0:T(8,128)(2,1)S(1)}, bf16[2,512,1024]{2,1,0:T(8,128)(2,1)}, u32[]{:S(2)}) copy-start(bf16[2,512,1024]{2,1,0:T(8,128)(2,1)} %param.14) | copy-start | bytes 6291460
  6.5 8.6 %copy-start.1 = (bf16[128,512]{1,0:T(8,128)(2,1)S(1)}, bf16[128,512]{1,0:T(8,128)(2,1)}, u32[]{:S(2)}) copy-start(bf16[128,512]{1,0:T(8,128)(2,1)} %param.8) | copy-start | bytes 393220
  6.5 23.6 %copy-start.4 = (f32[512]{0:T(512)S(1)}, f32[512]{0:T(512)}, u32[]{:S(2)}) copy-start(f32[512]{0:T(512)} %param.9) | copy-start | bytes 6148
  6.5 148.9 %all-reduce.4.cloned.1.call-start = ((), (), s32[]{:S(2)}) async-start(), calls=%async_computation.3 | async-start | bytes 4194304 | tf_op jit(solution)/shard_map/psum | solution.py:46
  158.4 17.1 %copy-start.3 = (f32[128,8]{0,1:T(8,128)S(1)}, f32[128,8]{0,1:T(8,128)}, u32[]{:S(2)}) copy-start(f32[128,8]{0,1:T(8,128)} %param.10) | copy-start | bytes 12292
  158.4 17.2 %copy-start.2 = (s32[128]{0:T(128)S(1)}, s32[128]{0:T(128)}, u32[]{:S(2)}) copy-start(s32[128]{0:T(128)} %param.13) | copy-start | bytes 1540
  158.4 17.7 %copy-start.5 = (s32[128]{0:T(128)S(1)}, s32[128]{0:T(128)}, u32[]{:S(2)}) copy-start(s32[128]{0:T(128)} %param.11) | copy-start | bytes 1540
  159.5 45.2 %all-to-all-start.1 = ((bf16[2,64,4,512]{3,2,0,1:T(4,128)(2,1)}), bf16[2,64,4,512]{3,2,0,1:T(4,128)(2,1)S(1)}, u32[]{:S(2)}, u32[]{:S(2)}) async-start(bf16[2,64,4,512]{3,2,0,1:T(4,128)(2,1)} %copy.24), calls=%async_computation.1 | async-start | bytes 1048576 | tf_op jit(solution)/shard_map/all_to_all | solution.py:54
Sparse Core Ops, SparseCore 0:
  82.8 72.6 all-reduce.3
where the time goes:
time: 244 us; the launch traced here: 241 us
  waiting for transfers between devices  100 us (41%)
  blocking collectives  83.6 us (34%)
  local copies, waits for them, and re-layouts  18 us (7%)
  starting transfers between devices  15.9 us (7%)
  between operations  13.7 us (6%)
  matrix products  6.61 us (3%)
  other arithmetic  3.01 us (1%)
    psum x1, waiting for transfers between devices, per_device(): summed = lax.psum(partial_value, 'rep')  72.8 us
    all_to_all x1, blocking collectives, per_device(): lax.all_to_all(outbound, 'expert', split_axis=1, concat_axis=1, tiled=True)  47.7 us
    all_to_all x1, waiting for transfers between devices, per_device(): lax.all_to_all(expert_out, 'expert', split_axis=1, concat_axis=1, tiled=T...  27.7 us
    all_to_all x1, blocking collectives, per_device(): lax.all_to_all(leaving, 'expert', split_axis=0, concat_axis=0, tiled=True)  21.1 us
    all_to_all x1, starting transfers between devices, per_device(): lax.all_to_all(expert_out, 'expert', split_axis=1, concat_axis=1, tiled=T...  15.9 us
    psum x1, blocking collectives, per_device(): squares = lax.psum(jnp.sum(widened * widened, axis=1), 'rep')  14.9 us
    gather x1, local copies, waits for them, and re-layouts, per_device(): flat_back[jnp.minimum(slot_index, slot_total - 1)]  5.07 us
  transfers between devices with their start and end apart: 2, of which 2 were waited for; matrix products, arithmetic and copies ran while one was open for 1% of the time, Pallas kernels for 0%

commit v1 on v0

--- a/solution.py
+++ b/solution.py
@@ -11,16 +11,15 @@
     owner_count = lax.axis_size("expert")
     rep_count = lax.axis_size("rep")
     local_experts = up_weight.shape[0]
+    hid = up_weight.shape[2]
     route_count = routes.shape[1]
     experts_all = local_experts * owner_count
     most_live = row_count // 2
     capacity = route_count * most_live // experts_all
     hand_cap = (most_live + owner_count - 1) // owner_count
     slot_total = local_experts * owner_count * capacity
+    hid_part = hid // rep_count
     widened = tokens.astype(jnp.float32)
-    squares = lax.psum(jnp.sum(widened * widened, axis=1), "rep")
-    rinv_rows = lax.rsqrt(squares / (feat_width * rep_count) + 1e-06)
-    normed = (widened * rinv_rows[:, None] * norm_gain[None, :]).astype(jnp.bfloat16)
     survive = 1 - exit_flags
     pair_live = jnp.repeat(survive, route_count)
     route_flat = routes.reshape(-1)
@@ -35,16 +34,34 @@
     slot_index = jnp.where(pair_live > 0, slot_index, slot_total)
     pair_row = jnp.arange(row_count * route_count, dtype=jnp.int32) // route_count
     source_row = jnp.zeros((slot_total,), jnp.int32).at[slot_index].set(pair_row + 1, mode="drop")
-    padded = jnp.concatenate([jnp.zeros((1, feat_width), jnp.bfloat16), normed], axis=0)
+    padded = jnp.concatenate([jnp.zeros((1, feat_width), jnp.bfloat16), tokens], axis=0)
     outbound = padded[source_row].reshape(local_experts, owner_count, capacity, feat_width)
     received = lax.all_to_all(outbound, "expert", split_axis=1, concat_axis=1, tiled=True)
     item_count = received.shape[2]
-    flattened = received.reshape(local_experts, owner_count * item_count, feat_width)
+    rows_here = owner_count * item_count
+    flattened = received.reshape(local_experts, rows_here, feat_width).astype(jnp.float32)
+    scaled = flattened * norm_gain[None, None, :]
+    high = scaled.astype(jnp.bfloat16)
+    low = (scaled - high.astype(jnp.float32)).astype(jnp.bfloat16)
     partial_value = jnp.einsum(
-        "erd,edh->erh", flattened, up_weight, preferred_element_type=jnp.float32
-    )
-    summed = lax.psum(partial_value, "rep")
-    activated = jax.nn.silu(summed).astype(jnp.bfloat16)
+        "erd,edh->erh", high, up_weight, preferred_element_type=jnp.float32
+    ) + jnp.einsum("erd,edh->erh", low, up_weight, preferred_element_type=jnp.float32)
+    squares = jnp.sum(flattened * flattened, axis=2)
+    pieces = partial_value.reshape(local_experts * rows_here, rep_count, hid_part)
+    pieces = jnp.transpose(pieces, (1, 0, 2))
+    sq_rows = squares.reshape(-1, hid_part)
+    sq_tile = jnp.broadcast_to(sq_rows[None], (rep_count,) + sq_rows.shape)
+    packed = jnp.concatenate([pieces, sq_tile], axis=1)
+    got = lax.all_to_all(packed, "rep", split_axis=0, concat_axis=0, tiled=True)
+    total = jnp.sum(got, axis=0)
+    hidden_part = total[: local_experts * rows_here].reshape(local_experts, rows_here, hid_part)
+    sq_total = total[local_experts * rows_here :].reshape(local_experts, rows_here)
+    rinv = lax.rsqrt(sq_total / (feat_width * rep_count) + 1e-06)
+    hidden_part = hidden_part * rinv[:, :, None]
+    act_part = jax.nn.silu(hidden_part).astype(jnp.bfloat16)
+    act_tile = jnp.broadcast_to(act_part[None], (rep_count,) + act_part.shape)
+    act_all = lax.all_to_all(act_tile, "rep", split_axis=0, concat_axis=0, tiled=True)
+    activated = jnp.transpose(act_all, (1, 2, 0, 3)).reshape(local_experts, rows_here, hid)
     expert_out = jnp.einsum(
         "erh,ehd->erd", activated, down_weight, preferred_element_type=jnp.float32
     )

time: 244 us -> 188 us (0.77)
  waiting for transfers between devices: 100 us -> 29.3 us
  blocking collectives: 83.6 us -> 122 us
  between operations: 13.7 us -> 0.43 us
  starting transfers between devices: 15.9 us -> 6.9 us
  matrix products: 6.61 us -> 3.85 us
    psum x1 -> x0, waiting for transfers between devices: 72.8 us -> none  [per_device(): summed = lax.psum(partial_value, 'rep')]
    all_to_all x0 -> x2, blocking collectives: none -> 50.5 us  [the longest x1 31.9 us: per_device(): got = lax.all_to_all(packed, 'rep', split_axis=0, concat_axis=0, tiled=True)]
    psum x1 -> x0, blocking collectives: 14.9 us -> none  [per_device(): squares = lax.psum(jnp.sum(widened * widened, axis=1), 'rep')]
    all_to_all x1, starting transfers between devices: 15.9 us -> 6.9 us  [per_device(): lax.all_to_all(expert_out, 'expert', split_axis=1, concat_axis=1, tiled=T...]
    all_to_all x1, blocking collectives: 47.7 us -> 50.3 us  [per_device(): lax.all_to_all(outbound, 'expert', split_axis=1, concat_axis=1, tiled=True)]
  transfers between devices with their start and end apart: 2 -> 1, of which waited for: 2 -> 1; matrix products, arithmetic and copies ran while one was open for 1% -> 1% of each run, Pallas kernels for 0% -> 0%
where the time goes in v1:
time: 188 us
  blocking collectives  122 us (65%)
  waiting for transfers between devices  29.3 us (16%)
  local copies, waits for them, and re-layouts  19.3 us (10%)
  starting transfers between devices  6.9 us (4%)
  other arithmetic  5.38 us (3%)
  matrix products  3.85 us (2%)
    all_to_all x1, blocking collectives, per_device(): lax.all_to_all(outbound, 'expert', split_axis=1, concat_axis=1, tiled=True)  50.3 us
    all_to_all x1, blocking collectives, per_device(): got = lax.all_to_all(packed, 'rep', split_axis=0, concat_axis=0, tiled=True)  31.9 us
    all_to_all x1, waiting for transfers between devices, per_device(): lax.all_to_all(expert_out, 'expert', split_axis=1, concat_axis=1, tiled=T...  29.3 us
    all_to_all x1, blocking collectives, per_device(): lax.all_to_all(leaving, 'expert', split_axis=0, concat_axis=0, tiled=True)  21.8 us
    all_to_all x1, blocking collectives, per_device(): lax.all_to_all(act_tile, 'rep', split_axis=0, concat_axis=0, tiled=True)  18.5 us
    all_to_all x1, starting transfers between devices, per_device(): lax.all_to_all(expert_out, 'expert', split_axis=1, concat_axis=1, tiled=T...  6.9 us
    gather x1, local copies, waits for them, and re-layouts, per_device(): flat_back[jnp.minimum(slot_index, slot_total - 1)]  5.07 us
    scatter x1, local copies, waits for them, and re-layouts, per_device(): jnp.zeros((slot_total,), jnp.int32).at[slot_index]  4.3 us
  transfers between devices with their start and end apart: 1, of which 1 were waited for; matrix products, arithmetic and copies ran while one was open for 1% of the time, Pallas kernels for 0%

profile of v1, /device:TPU:6, one launch (start us, length us, event | category | flops | bytes accessed | tf_op | source)
XLA Modules:
  0.0 187.6 jit_solution(9312158936113711577)
XLA Ops:
  0.0 0.8 broadcast_compare_fusion
  0.8 0.7 broadcast_subtract_fusion
  1.5 0.8 copy.59
  3.7 0.5 fusion.7
  4.3 4.3 %scatter_custom_fusion = s32[512]{0:T(512)S(1)} fusion(s32[1024]{0:T(1024)S(1)} %bitcast.51, s32[1024]{0:T(1024)S(1)} %fusion.17, s32[]{:T(128)} %constant.66.clone.1), kind=kCustom, calls=%fused_computation.66 | custom fusion | bytes 2052 | tf_op jit(solution)/shard_map/scatter | solution.py:36
  8.7 2.0 %gather_fusion = bf16[512,512]{1,0:T(8,128)(2,1)S(1)} fusion(bf16[129,512]{1,0:T(8,128)(2,1)S(1)} %concatenate.9, s32[1024]{0:T(1024)S(1)} %pad_clamp_fusion.1), kind=kCustom, calls=%fused_computation | custom fusion | bytes 1050624 | tf_op jit(solution)/shard_map/gather | solution.py:38
  11.0 50.3 %all_to_all.25 = bf16[2,64,4,512]{3,2,0,1:T(4,128)(2,1)S(1)} all-to-all(bf16[2,64,4,512]{3,2,0,1:T(4,128)(2,1)S(1)} %copy.65), channel_id=1, replica_groups=mesh['rep'=8,'expert'=64] {'expert'}, dimensions={1} | all-to-all | bytes 1048576 | tf_op jit(solution)/shard_map/all_to_all | solution.py:39
  62.2 0.7 fusion.5
  63.0 0.8 convolution_add_fusion
  63.7 0.5 copy.78
  64.2 0.4 copy.95
  64.8 31.9 %all_to_all.26 = f32[8,516,128]{2,1,0:T(8,128)} all-to-all(f32[8,516,128]{2,1,0:T(8,128)S(1)} %pad_maximum_fusion), channel_id=1, replica_groups=mesh['rep'=8,'expert'=64] {'rep'}, dimensions={0} | all-to-all | bytes 4227072 | tf_op jit(solution)/shard_map/all_to_all | solution.py:55
  96.7 1.7 reduce_sum.41
  98.9 18.5 %all_to_all.27 = bf16[8,2,256,128]{3,2,1,0:T(8,128)(2,1)S(1)} all-to-all(bf16[8,2,256,128]{3,2,1,0:T(8,128)(2,1)S(1)} %broadcast_in_dim.60), channel_id=1, replica_groups=mesh['rep'=8,'expert'=64] {'rep'}, dimensions={0} | all-to-all | bytes 2097152 | tf_op jit(solution)/shard_map/all_to_all | solution.py:63
  117.4 0.7 convolution_convert_fusion
  118.3 1.0 copy.71
  119.3 6.9 %all-to-all-start.3 = ((bf16[2,64,4,512]{3,2,0,1:T(4,128)(2,1)}), bf16[2,64,4,512]{3,2,0,1:T(4,128)(2,1)S(1)}, u32[]{:S(2)}, u32[]{:S(2)}) async-start(bf16[2,64,4,512]{3,2,0,1:T(4,128)(2,1)} %copy.71), calls=%async_computation.3 | async-start | bytes 1048576 | tf_op jit(solution)/shard_map/all_to_all | solution.py:71
  126.8 1.2 scatter_custom_fusion.1
  128.0 29.3 %all-to-all-done.3 = bf16[2,64,4,512]{3,2,0,1:T(4,128)(2,1)S(1)} async-done(((bf16[2,64,4,512]{3,2,0,1:T(4,128)(2,1)}), bf16[2,64,4,512]{3,2,0,1:T(4,128)(2,1)S(1)}, u32[]{:S(2)}, u32[]{:S(2)}) %all-to-all-start.3) | async-done | bytes 524320 | tf_op jit(solution)/shard_map/all_to_all | solution.py:71
  157.6 5.1 %gather_fusion.1 = bf16[1024,512]{1,0:T(8,128)(2,1)} fusion(bf16[512,512]{1,0:T(8,128)(2,1)S(1)} %reshape.268, s32[1024]{0:T(1024)S(1)} %broadcast_clamp_fusion), kind=kCustom, calls=%fused_computation.1 | custom fusion | bytes 2101248 | tf_op jit(solution)/shard_map/gather | solution.py:73
  162.7 1.6 fusion.2
  164.4 0.7 gather_fusion.2
  165.2 21.8 %all_to_all.28 = f32[64,1,512]{2,1,0:T(1,128)S(1)} all-to-all(f32[64,1,512]{2,1,0:T(1,128)S(1)} %copy.73), channel_id=1, replica_groups=mesh['rep'=8,'expert'=64] {'expert'}, dimensions={0} | all-to-all | bytes 262144 | tf_op jit(solution)/shard_map/all_to_all | solution.py:90
  186.9 0.7 copy.96
  (64 shorter events, 4.5 us)
Async XLA Ops:
  0.0 62.2 %copy-start = (bf16[2,512,1024]{2,1,0:T(8,128)(2,1)S(1)}, bf16[2,512,1024]{2,1,0:T(8,128)(2,1)}, u32[]{:S(2)}) copy-start(bf16[2,512,1024]{2,1,0:T(8,128)(2,1)} %param.14) | copy-start | bytes 6291460
  0.0 8.6 %copy-start.1 = (bf16[128,512]{1,0:T(8,128)(2,1)S(1)}, bf16[128,512]{1,0:T(8,128)(2,1)}, u32[]{:S(2)}) copy-start(bf16[128,512]{1,0:T(8,128)(2,1)} %param.8) | copy-start | bytes 393220
  10.8 51.4 %copy-start.2 = (f32[512]{0:T(512)S(1)}, f32[512]{0:T(512)}, u32[]{:S(2)}) copy-start(f32[512]{0:T(512)} %param.9) | copy-start | bytes 6148
  98.5 18.9 %copy-start.6 = (bf16[2,1024,512]{2,1,0:T(8,128)(2,1)S(1)}, bf16[2,1024,512]{2,1,0:T(8,128)(2,1)}, u32[]{:S(2)}) copy-start(bf16[2,1024,512]{2,1,0:T(8,128)(2,1)} %param.15) | copy-start | bytes 6291460
  118.1 8.0 %copy-start.4 = (f32[128,8]{0,1:T(8,128)S(1)}, f32[128,8]{0,1:T(8,128)}, u32[]{:S(2)}) copy-start(f32[128,8]{0,1:T(8,128)} %param.10) | copy-start | bytes 12292
  118.1 8.2 %copy-start.3 = (s32[128]{0:T(128)S(1)}, s32[128]{0:T(128)}, u32[]{:S(2)}) copy-start(s32[128]{0:T(128)} %param.13) | copy-start | bytes 1540
  118.2 8.6 %copy-start.5 = (s32[128]{0:T(128)S(1)}, s32[128]{0:T(128)}, u32[]{:S(2)}) copy-start(s32[128]{0:T(128)} %param.11) | copy-start | bytes 1540
  119.3 38.0 %all-to-all-start.3 = ((bf16[2,64,4,512]{3,2,0,1:T(4,128)(2,1)}), bf16[2,64,4,512]{3,2,0,1:T(4,128)(2,1)S(1)}, u32[]{:S(2)}, u32[]{:S(2)}) async-start(bf16[2,64,4,512]{3,2,0,1:T(4,128)(2,1)} %copy.71), calls=%async_computation.3 | async-start | bytes 1048576 | tf_op jit(solution)/shard_map/all_to_all | solution.py:71

commit v2 on v0

--- a/solution.py
+++ b/solution.py
@@ -11,16 +11,15 @@
     owner_count = lax.axis_size("expert")
     rep_count = lax.axis_size("rep")
     local_experts = up_weight.shape[0]
+    hid = up_weight.shape[2]
     route_count = routes.shape[1]
     experts_all = local_experts * owner_count
     most_live = row_count // 2
     capacity = route_count * most_live // experts_all
     hand_cap = (most_live + owner_count - 1) // owner_count
     slot_total = local_experts * owner_count * capacity
+    hid_part = hid // rep_count
     widened = tokens.astype(jnp.float32)
-    squares = lax.psum(jnp.sum(widened * widened, axis=1), "rep")
-    rinv_rows = lax.rsqrt(squares / (feat_width * rep_count) + 1e-06)
-    normed = (widened * rinv_rows[:, None] * norm_gain[None, :]).astype(jnp.bfloat16)
     survive = 1 - exit_flags
     pair_live = jnp.repeat(survive, route_count)
     route_flat = routes.reshape(-1)
@@ -35,16 +34,26 @@
     slot_index = jnp.where(pair_live > 0, slot_index, slot_total)
     pair_row = jnp.arange(row_count * route_count, dtype=jnp.int32) // route_count
     source_row = jnp.zeros((slot_total,), jnp.int32).at[slot_index].set(pair_row + 1, mode="drop")
+    squares = lax.psum(jnp.sum(widened * widened, axis=1), "rep")
+    rinv_rows = lax.rsqrt(squares / (feat_width * rep_count) + 1e-06)
+    normed = (widened * rinv_rows[:, None] * norm_gain[None, :]).astype(jnp.bfloat16)
     padded = jnp.concatenate([jnp.zeros((1, feat_width), jnp.bfloat16), normed], axis=0)
     outbound = padded[source_row].reshape(local_experts, owner_count, capacity, feat_width)
     received = lax.all_to_all(outbound, "expert", split_axis=1, concat_axis=1, tiled=True)
     item_count = received.shape[2]
-    flattened = received.reshape(local_experts, owner_count * item_count, feat_width)
+    rows_here = owner_count * item_count
+    flattened = received.reshape(local_experts, rows_here, feat_width)
     partial_value = jnp.einsum(
         "erd,edh->erh", flattened, up_weight, preferred_element_type=jnp.float32
     )
-    summed = lax.psum(partial_value, "rep")
-    activated = jax.nn.silu(summed).astype(jnp.bfloat16)
+    pieces = partial_value.reshape(local_experts * rows_here, rep_count, hid_part)
+    pieces = jnp.transpose(pieces, (1, 0, 2))
+    got = lax.all_to_all(pieces, "rep", split_axis=0, concat_axis=0, tiled=True)
+    hidden_part = jnp.sum(got, axis=0).reshape(local_experts, rows_here, hid_part)
+    act_part = jax.nn.silu(hidden_part).astype(jnp.bfloat16)
+    act_tile = jnp.broadcast_to(act_part[None], (rep_count,) + act_part.shape)
+    act_all = lax.all_to_all(act_tile, "rep", split_axis=0, concat_axis=0, tiled=True)
+    activated = jnp.transpose(act_all, (1, 2, 0, 3)).reshape(local_experts, rows_here, hid)
     expert_out = jnp.einsum(
         "erh,ehd->erd", activated, down_weight, preferred_element_type=jnp.float32
     )

time: 244 us -> 198 us (0.81)
  waiting for transfers between devices: 100 us -> 29.4 us
  blocking collectives: 83.6 us -> 133 us
  between operations: 13.7 us -> 0.38 us
  starting transfers between devices: 15.9 us -> 7.22 us
  matrix products: 6.61 us -> 3.05 us
    psum x1 -> x0, waiting for transfers between devices: 72.8 us -> none  [per_device(): summed = lax.psum(partial_value, 'rep')]
    all_to_all x0 -> x2, blocking collectives: none -> 48.9 us  [the longest x1 30.4 us: per_device(): got = lax.all_to_all(pieces, 'rep', split_axis=0, concat_axis=0, tiled=True)]
    all_to_all x1, starting transfers between devices: 15.9 us -> 7.22 us  [per_device(): lax.all_to_all(expert_out, 'expert', split_axis=1, concat_axis=1, tiled=T...]
  transfers between devices with their start and end apart: 2 -> 1, of which waited for: 2 -> 1; matrix products, arithmetic and copies ran while one was open for 1% -> 1% of each run, Pallas kernels for 0% -> 0%
where the time goes in v2:
time: 198 us; the launch traced here: 197 us
  blocking collectives  133 us (67%)
  waiting for transfers between devices  29.4 us (15%)
  local copies, waits for them, and re-layouts  19 us (10%)
  starting transfers between devices  7.22 us (4%)
  other arithmetic  4.8 us (2%)
  matrix products  3.05 us (2%)
    all_to_all x1, blocking collectives, per_device(): lax.all_to_all(outbound, 'expert', split_axis=1, concat_axis=1, tiled=True)  47.7 us
    all_to_all x1, blocking collectives, per_device(): got = lax.all_to_all(pieces, 'rep', split_axis=0, concat_axis=0, tiled=True)  30.4 us
    all_to_all x1, waiting for transfers between devices, per_device(): lax.all_to_all(expert_out, 'expert', split_axis=1, concat_axis=1, tiled=T...  29.4 us
    all_to_all x1, blocking collectives, per_device(): lax.all_to_all(leaving, 'expert', split_axis=0, concat_axis=0, tiled=True)  21.8 us
    all_to_all x1, blocking collectives, per_device(): lax.all_to_all(act_tile, 'rep', split_axis=0, concat_axis=0, tiled=True)  18.5 us
    psum x1, blocking collectives, per_device(): squares = lax.psum(jnp.sum(widened * widened, axis=1), 'rep')  14.9 us
    all_to_all x1, starting transfers between devices, per_device(): lax.all_to_all(expert_out, 'expert', split_axis=1, concat_axis=1, tiled=T...  7.22 us
    gather x1, local copies, waits for them, and re-layouts, per_device(): flat_back[jnp.minimum(slot_index, slot_total - 1)]  5.07 us
  transfers between devices with their start and end apart: 1, of which 1 were waited for; matrix products, arithmetic and copies ran while one was open for 1% of the time, Pallas kernels for 0%

profile of v2, /device:TPU:6, one launch (start us, length us, event | category | flops | bytes accessed | tf_op | source)
XLA Modules:
  0.0 197.1 jit_solution(15183966785628295892)
XLA Ops:
  0.0 0.9 copy.16
  1.2 0.7 broadcast_subtract_fusion
  1.9 0.7 broadcast_compare_fusion
  3.7 0.5 fusion.4
  4.3 4.3 %scatter_custom_fusion = s32[512]{0:T(512)S(1)} fusion(s32[1024]{0:T(1024)S(1)} %bitcast.48, s32[1024]{0:T(1024)S(1)} %fusion.15, s32[]{:T(128)} %constant.69.clone.1), kind=kCustom, calls=%fused_computation.59 | custom fusion | bytes 2052 | tf_op jit(solution)/shard_map/scatter | solution.py:36
  8.8 14.9 %psum.7 = f32[128]{0:T(128)S(1)} all-reduce(f32[128]{0:T(128)S(1)} %fusion.7), channel_id=1, replica_groups=mesh['rep'=8,'expert'=64] {'rep'}, use_global_device_ids=true, to_apply=%region_1.2 | all-reduce | flops 128 | bytes 1024 | tf_op jit(solution)/shard_map/psum | solution.py:37
  23.8 2.0 %gather_fusion = bf16[512,512]{1,0:T(8,128)(2,1)S(1)} fusion(bf16[129,512]{1,0:T(8,128)(2,1)S(1)} %concatenate.6, s32[1024]{0:T(1024)S(1)} %pad_clamp_fusion.1), kind=kCustom, calls=%fused_computation | custom fusion | bytes 1050624 | tf_op jit(solution)/shard_map/gather | solution.py:41
  26.1 47.7 %all_to_all.25 = bf16[2,64,4,512]{3,2,0,1:T(4,128)(2,1)S(1)} all-to-all(bf16[2,64,4,512]{3,2,0,1:T(4,128)(2,1)S(1)} %copy.22), channel_id=1, replica_groups=mesh['rep'=8,'expert'=64] {'expert'}, dimensions={1} | all-to-all | bytes 1048576 | tf_op jit(solution)/shard_map/all_to_all | solution.py:42
  74.1 0.7 fusion.26
  74.8 0.5 copy.33
  75.3 0.4 copy.41
  75.7 30.4 %all_to_all.26 = f32[8,512,128]{2,1,0:T(8,128)} all-to-all(f32[8,512,128]{2,1,0:T(8,128)S(1)} %bitcast.42), channel_id=1, replica_groups=mesh['rep'=8,'expert'=64] {'rep'}, dimensions={0} | all-to-all | bytes 4194304 | tf_op jit(solution)/shard_map/all_to_all | solution.py:51
  106.0 1.7 reduce_sum.41
  108.1 18.5 %all_to_all.27 = bf16[8,2,256,128]{3,2,1,0:T(8,128)(2,1)S(1)} all-to-all(bf16[8,2,256,128]{3,2,1,0:T(8,128)(2,1)S(1)} %broadcast_in_dim.51), channel_id=1, replica_groups=mesh['rep'=8,'expert'=64] {'rep'}, dimensions={0} | all-to-all | bytes 2097152 | tf_op jit(solution)/shard_map/all_to_all | solution.py:55
  126.6 0.7 convolution_convert_fusion
  127.5 1.0 copy.26
  128.4 7.2 %all-to-all-start.3 = ((bf16[2,64,4,512]{3,2,0,1:T(4,128)(2,1)}), bf16[2,64,4,512]{3,2,0,1:T(4,128)(2,1)S(1)}, u32[]{:S(2)}, u32[]{:S(2)}) async-start(bf16[2,64,4,512]{3,2,0,1:T(4,128)(2,1)} %copy.26), calls=%async_computation.3 | async-start | bytes 1048576 | tf_op jit(solution)/shard_map/all_to_all | solution.py:63
  136.3 1.0 scatter_custom_fusion.1
  137.3 29.4 %all-to-all-done.3 = bf16[2,64,4,512]{3,2,0,1:T(4,128)(2,1)S(1)} async-done(((bf16[2,64,4,512]{3,2,0,1:T(4,128)(2,1)}), bf16[2,64,4,512]{3,2,0,1:T(4,128)(2,1)S(1)}, u32[]{:S(2)}, u32[]{:S(2)}) %all-to-all-start.3) | async-done | bytes 524320 | tf_op jit(solution)/shard_map/all_to_all | solution.py:63
  167.1 5.1 %gather_fusion.1 = bf16[1024,512]{1,0:T(8,128)(2,1)} fusion(bf16[512,512]{1,0:T(8,128)(2,1)S(1)} %reshape.256, s32[1024]{0:T(1024)S(1)} %broadcast_clamp_fusion), kind=kCustom, calls=%fused_computation.1 | custom fusion | bytes 2101248 | tf_op jit(solution)/shard_map/gather | solution.py:65
  172.2 1.6 fusion.2
  173.9 0.7 gather_fusion.2
  174.7 21.8 %all_to_all.28 = f32[64,1,512]{2,1,0:T(1,128)S(1)} all-to-all(f32[64,1,512]{2,1,0:T(1,128)S(1)} %copy.28), channel_id=1, replica_groups=mesh['rep'=8,'expert'=64] {'expert'}, dimensions={0} | all-to-all | bytes 262144 | tf_op jit(solution)/shard_map/all_to_all | solution.py:82
  196.4 0.7 copy.42
  (60 shorter events, 3.9 us)
Async XLA Ops:
  0.0 74.1 %copy-start = (bf16[2,512,1024]{2,1,0:T(8,128)(2,1)S(1)}, bf16[2,512,1024]{2,1,0:T(8,128)(2,1)}, u32[]{:S(2)}) copy-start(bf16[2,512,1024]{2,1,0:T(8,128)(2,1)} %param.14) | copy-start | bytes 6291460
  0.0 8.6 %copy-start.1 = (bf16[128,512]{1,0:T(8,128)(2,1)S(1)}, bf16[128,512]{1,0:T(8,128)(2,1)}, u32[]{:S(2)}) copy-start(bf16[128,512]{1,0:T(8,128)(2,1)} %param.8) | copy-start | bytes 393220
  0.0 23.6 %copy-start.4 = (f32[512]{0:T(512)S(1)}, f32[512]{0:T(512)}, u32[]{:S(2)}) copy-start(f32[512]{0:T(512)} %param.9) | copy-start | bytes 6148
  107.8 18.8 %copy-start.6 = (bf16[2,1024,512]{2,1,0:T(8,128)(2,1)S(1)}, bf16[2,1024,512]{2,1,0:T(8,128)(2,1)}, u32[]{:S(2)}) copy-start(bf16[2,1024,512]{2,1,0:T(8,128)(2,1)} %param.15) | copy-start | bytes 6291460
  127.3 8.4 %copy-start.3 = (f32[128,8]{0,1:T(8,128)S(1)}, f32[128,8]{0,1:T(8,128)}, u32[]{:S(2)}) copy-start(f32[128,8]{0,1:T(8,128)} %param.10) | copy-start | bytes 12292
  127.3 8.5 %copy-start.2 = (s32[128]{0:T(128)S(1)}, s32[128]{0:T(128)}, u32[]{:S(2)}) copy-start(s32[128]{0:T(128)} %param.13) | copy-start | bytes 1540
  127.3 9.0 %copy-start.5 = (s32[128]{0:T(128)S(1)}, s32[128]{0:T(128)}, u32[]{:S(2)}) copy-start(s32[128]{0:T(128)} %param.11) | copy-start | bytes 1540
  128.4 38.3 %all-to-all-start.3 = ((bf16[2,64,4,512]{3,2,0,1:T(4,128)(2,1)}), bf16[2,64,4,512]{3,2,0,1:T(4,128)(2,1)S(1)}, u32[]{:S(2)}, u32[]{:S(2)}) async-start(bf16[2,64,4,512]{3,2,0,1:T(4,128)(2,1)} %copy.26), calls=%async_computation.3 | async-start | bytes 1048576 | tf_op jit(solution)/shard_map/all_to_all | solution.py:63

commit v3 on v2

--- a/solution.py
+++ b/solution.py
@@ -32,13 +32,16 @@
     local_id = route_flat % local_experts
     slot_index = (local_id * owner_count + owner_id) * capacity + position
     slot_index = jnp.where(pair_live > 0, slot_index, slot_total)
-    pair_row = jnp.arange(row_count * route_count, dtype=jnp.int32) // route_count
-    source_row = jnp.zeros((slot_total,), jnp.int32).at[slot_index].set(pair_row + 1, mode="drop")
     squares = lax.psum(jnp.sum(widened * widened, axis=1), "rep")
     rinv_rows = lax.rsqrt(squares / (feat_width * rep_count) + 1e-06)
     normed = (widened * rinv_rows[:, None] * norm_gain[None, :]).astype(jnp.bfloat16)
-    padded = jnp.concatenate([jnp.zeros((1, feat_width), jnp.bfloat16), normed], axis=0)
-    outbound = padded[source_row].reshape(local_experts, owner_count, capacity, feat_width)
+    slot_ids = jnp.arange(slot_total, dtype=jnp.int32)
+    slot_of = slot_index.reshape(row_count, route_count)
+    pick = jnp.sum(
+        (slot_of[None, :, :] == slot_ids[:, None, None]).astype(jnp.float32), axis=2
+    ).astype(jnp.bfloat16)
+    outbound = jnp.dot(pick, normed, preferred_element_type=jnp.float32).astype(jnp.bfloat16)
+    outbound = outbound.reshape(local_experts, owner_count, capacity, feat_width)
     received = lax.all_to_all(outbound, "expert", split_axis=1, concat_axis=1, tiled=True)
     item_count = received.shape[2]
     rows_here = owner_count * item_count
@@ -62,10 +65,18 @@
     )
     returned = lax.all_to_all(expert_out, "expert", split_axis=1, concat_axis=1, tiled=True)
     flat_back = returned.reshape(slot_total, feat_width)
-    picked = flat_back[jnp.minimum(slot_index, slot_total - 1)].reshape(
-        row_count, route_count, feat_width
+    combine = jnp.sum(
+        jnp.where(
+            slot_of[:, :, None] == slot_ids[None, None, :], gate_weights[:, :, None], 0.0
+        ),
+        axis=1,
     )
-    mixture = jnp.einsum("rk,rkd->rd", gate_weights, picked, preferred_element_type=jnp.float32)
+    mixture = jnp.dot(
+        combine,
+        flat_back.astype(jnp.float32),
+        precision=lax.Precision.HIGHEST,
+        preferred_element_type=jnp.float32,
+    )
     updated = widened + mixture
     dest_hot = (next_device[:, None] == jnp.arange(owner_count, dtype=jnp.int32)[None, :]).astype(
         jnp.int32

time: 198 us -> 188 us (0.949)
  local copies, waits for them, and re-layouts: 19 us -> 8.57 us
    gather x2 -> x0, local copies, waits for them, and re-layouts: 7.04 us -> none  [the longest x1 5.07 us: per_device(): flat_back[jnp.minimum(slot_index, slot_total - 1)]]
    scatter x1 -> x0, local copies, waits for them, and re-layouts: 4.3 us -> none  [per_device(): jnp.zeros((slot_total,), jnp.int32).at[slot_index]]
where the time goes in v3:
time: 188 us; the launch traced here: 187 us
  blocking collectives  133 us (71%)
  waiting for transfers between devices  28.8 us (15%)
  local copies, waits for them, and re-layouts  8.57 us (5%)
  starting transfers between devices  7.21 us (4%)
  other arithmetic  6.28 us (3%)
  matrix products  2.95 us (2%)
    all_to_all x1, blocking collectives, per_device(): lax.all_to_all(outbound, 'expert', split_axis=1, concat_axis=1, tiled=True)  47.7 us
    all_to_all x1, blocking collectives, per_device(): got = lax.all_to_all(pieces, 'rep', split_axis=0, concat_axis=0, tiled=True)  30.4 us
    all_to_all x1, waiting for transfers between devices, per_device(): lax.all_to_all(expert_out, 'expert', split_axis=1, concat_axis=1, tiled=T...  28.8 us
    all_to_all x1, blocking collectives, per_device(): lax.all_to_all(leaving, 'expert', split_axis=0, concat_axis=0, tiled=True)  21.8 us
    all_to_all x1, blocking collectives, per_device(): lax.all_to_all(act_tile, 'rep', split_axis=0, concat_axis=0, tiled=True)  18.5 us
    psum x1, blocking collectives, per_device(): squares = lax.psum(jnp.sum(widened * widened, axis=1), 'rep')  14.9 us
    all_to_all x1, starting transfers between devices, per_device(): lax.all_to_all(expert_out, 'expert', split_axis=1, concat_axis=1, tiled=T...  7.21 us
  transfers between devices with their start and end apart: 1, of which 1 were waited for; matrix products, arithmetic and copies ran while one was open for 1% of the time, Pallas kernels for 0%

profile of v3, /device:TPU:6, one launch (start us, length us, event | category | flops | bytes accessed | tf_op | source)
XLA Modules:
  0.0 187.3 jit_solution(8721273738957620084)
XLA Ops:
  0.0 0.9 copy.56
  1.1 0.7 broadcast_subtract_fusion
  1.8 0.7 broadcast_compare_fusion
  3.4 0.5 fusion.2
  4.2 0.9 convert_reduce_fusion
  5.2 14.9 %psum.7 = f32[128]{0:T(128)S(1)} all-reduce(f32[128]{0:T(128)S(1)} %fusion.5), channel_id=1, replica_groups=mesh['rep'=8,'expert'=64] {'rep'}, use_global_device_ids=true, to_apply=%region_6.7 | all-reduce | flops 128 | bytes 1024 | tf_op jit(solution)/shard_map/psum | solution.py:35
  20.8 47.7 %all_to_all.25 = bf16[2,64,4,512]{3,2,0,1:T(4,128)(2,1)S(1)} all-to-all(bf16[2,64,4,512]{3,2,0,1:T(4,128)(2,1)S(1)} %copy.67), channel_id=1, replica_groups=mesh['rep'=8,'expert'=64] {'expert'}, dimensions={1} | all-to-all | bytes 1048576 | tf_op jit(solution)/shard_map/all_to_all | solution.py:45
  68.8 0.7 fusion.29
  69.5 0.5 copy.76
  70.0 0.4 copy.83
  70.4 30.4 %all_to_all.26 = f32[8,512,128]{2,1,0:T(8,128)} all-to-all(f32[8,512,128]{2,1,0:T(8,128)S(1)} %bitcast.35), channel_id=1, replica_groups=mesh['rep'=8,'expert'=64] {'rep'}, dimensions={0} | all-to-all | bytes 4194304 | tf_op jit(solution)/shard_map/all_to_all | solution.py:54
  100.7 1.7 reduce_sum.61
  102.8 18.5 %all_to_all.27 = bf16[8,2,256,128]{3,2,1,0:T(8,128)(2,1)S(1)} all-to-all(bf16[8,2,256,128]{3,2,1,0:T(8,128)(2,1)S(1)} %broadcast_in_dim.61), channel_id=1, replica_groups=mesh['rep'=8,'expert'=64] {'rep'}, dimensions={0} | all-to-all | bytes 2097152 | tf_op jit(solution)/shard_map/all_to_all | solution.py:58
  121.3 1.5 convolution_convert_fusion
  122.8 1.2 reshape.156
  124.0 1.0 copy.71
  125.0 7.2 %all-to-all-start.3 = ((bf16[2,64,4,512]{3,2,0,1:T(4,128)(2,1)}), bf16[2,64,4,512]{3,2,0,1:T(4,128)(2,1)S(1)}, u32[]{:S(2)}, u32[]{:S(2)}) async-start(bf16[2,64,4,512]{3,2,0,1:T(4,128)(2,1)} %copy.71), calls=%async_computation.3 | async-start | bytes 1048576 | tf_op jit(solution)/shard_map/all_to_all | solution.py:66
  132.8 1.0 scatter_custom_fusion
  133.8 0.7 select_reduce_fusion
  134.5 28.8 %all-to-all-done.3 = bf16[2,64,4,512]{3,2,0,1:T(4,128)(2,1)S(1)} async-done(((bf16[2,64,4,512]{3,2,0,1:T(4,128)(2,1)}), bf16[2,64,4,512]{3,2,0,1:T(4,128)(2,1)S(1)}, u32[]{:S(2)}, u32[]{:S(2)}) %all-to-all-start.3) | async-done | bytes 524320 | tf_op jit(solution)/shard_map/all_to_all | solution.py:66
  163.6 0.4 convolution_add_fusion
  164.1 0.7 gather_fusion
  164.9 21.8 %all_to_all.28 = f32[64,1,512]{2,1,0:T(1,128)S(1)} all-to-all(f32[64,1,512]{2,1,0:T(1,128)S(1)} %copy.73), channel_id=1, replica_groups=mesh['rep'=8,'expert'=64] {'expert'}, dimensions={0} | all-to-all | bytes 262144 | tf_op jit(solution)/shard_map/all_to_all | solution.py:93
  186.6 0.7 copy.84
  (55 shorter events, 3.8 us)
Async XLA Ops:
  0.0 68.8 %copy-start = (bf16[2,512,1024]{2,1,0:T(8,128)(2,1)S(1)}, bf16[2,512,1024]{2,1,0:T(8,128)(2,1)}, u32[]{:S(2)}) copy-start(bf16[2,512,1024]{2,1,0:T(8,128)(2,1)} %param.14) | copy-start | bytes 6291460
  1.0 4.1 %copy-start.1 = (bf16[128,512]{1,0:T(8,128)(2,1)S(1)}, bf16[128,512]{1,0:T(8,128)(2,1)}, u32[]{:S(2)}) copy-start(bf16[128,512]{1,0:T(8,128)(2,1)} %param.8) | copy-start | bytes 393220
  2.6 17.5 %copy-start.6 = (f32[512]{0:T(512)S(1)}, f32[512]{0:T(512)}, u32[]{:S(2)}) copy-start(f32[512]{0:T(512)} %param.9) | copy-start | bytes 6148
  4.1 16.0 %copy-start.2 = (s32[128,8]{1,0:T(8,128)}, s32[128,8]{1,0:T(8,128)S(1)}, u32[]{:S(2)}) copy-start(s32[128,8]{1,0:T(8,128)S(1)} %fusion.19) | copy-start | bytes 12292
  102.5 18.8 %copy-start.8 = (bf16[2,1024,512]{2,1,0:T(8,128)(2,1)S(1)}, bf16[2,1024,512]{2,1,0:T(8,128)(2,1)}, u32[]{:S(2)}) copy-start(bf16[2,1024,512]{2,1,0:T(8,128)(2,1)} %param.15) | copy-start | bytes 6291460
  122.8 9.4 %copy-start.5 = (f32[128,8]{0,1:T(8,128)S(1)}, f32[128,8]{0,1:T(8,128)}, u32[]{:S(2)}) copy-start(f32[128,8]{0,1:T(8,128)} %param.10) | copy-start | bytes 12292
  122.8 9.5 %copy-start.4 = (s32[128]{0:T(128)S(1)}, s32[128]{0:T(128)}, u32[]{:S(2)}) copy-start(s32[128]{0:T(128)} %param.13) | copy-start | bytes 1540
  122.8 10.0 %copy-start.7 = (s32[128]{0:T(128)S(1)}, s32[128]{0:T(128)}, u32[]{:S(2)}) copy-start(s32[128]{0:T(128)} %param.11) | copy-start | bytes 1540
  122.8 11.0 %copy-start.3 = (s32[128,8]{1,0:T(8,128)S(1)}, s32[128,8]{1,0:T(8,128)}, u32[]{:S(2)}) copy-start(s32[128,8]{1,0:T(8,128)} %copy-done.2) | copy-start | bytes 12292
  125.0 38.3 %all-to-all-start.3 = ((bf16[2,64,4,512]{3,2,0,1:T(4,128)(2,1)}), bf16[2,64,4,512]{3,2,0,1:T(4,128)(2,1)S(1)}, u32[]{:S(2)}, u32[]{:S(2)}) async-start(bf16[2,64,4,512]{3,2,0,1:T(4,128)(2,1)} %copy.71), calls=%async_computation.3 | async-start | bytes 1048576 | tf_op jit(solution)/shard_map/all_to_all | solution.py:66

commit v4 on v3

--- a/solution.py
+++ b/solution.py
@@ -1,7 +1,7 @@
 import jax
 import jax.numpy as jnp
 from jax import lax
-from jax.sharding import PartitionSpec as P
+from jax.sharding import Mesh, PartitionSpec as P
 
 
 def per_device(
@@ -9,7 +9,7 @@
 ):
     row_count, feat_width = tokens.shape
     owner_count = lax.axis_size("expert")
-    rep_count = lax.axis_size("rep")
+    rep_count = lax.axis_size("ry") * lax.axis_size("rc")
     local_experts = up_weight.shape[0]
     hid = up_weight.shape[2]
     route_count = routes.shape[1]
@@ -32,7 +32,7 @@
     local_id = route_flat % local_experts
     slot_index = (local_id * owner_count + owner_id) * capacity + position
     slot_index = jnp.where(pair_live > 0, slot_index, slot_total)
-    squares = lax.psum(jnp.sum(widened * widened, axis=1), "rep")
+    squares = lax.psum(jnp.sum(widened * widened, axis=1), ("ry", "rc"))
     rinv_rows = lax.rsqrt(squares / (feat_width * rep_count) + 1e-06)
     normed = (widened * rinv_rows[:, None] * norm_gain[None, :]).astype(jnp.bfloat16)
     slot_ids = jnp.arange(slot_total, dtype=jnp.int32)
@@ -49,14 +49,29 @@
     partial_value = jnp.einsum(
         "erd,edh->erh", flattened, up_weight, preferred_element_type=jnp.float32
     )
-    pieces = partial_value.reshape(local_experts * rows_here, rep_count, hid_part)
+    core = lax.axis_index("rc")
+    sibling = [(i, 1 - i) for i in range(2)]
+    chips = lax.axis_size("ry")
+    half = hid // 2
+    quarter = half // chips
+    halves = partial_value.reshape(local_experts, rows_here, 2, half)
+    mine = jnp.where(core == 0, halves[:, :, 0], halves[:, :, 1])
+    theirs = jnp.where(core == 0, halves[:, :, 1], halves[:, :, 0])
+    half_sum = mine + lax.ppermute(theirs, "rc", sibling)
+    pieces = half_sum.reshape(local_experts * rows_here, chips, quarter)
     pieces = jnp.transpose(pieces, (1, 0, 2))
-    got = lax.all_to_all(pieces, "rep", split_axis=0, concat_axis=0, tiled=True)
-    hidden_part = jnp.sum(got, axis=0).reshape(local_experts, rows_here, hid_part)
+    got = lax.all_to_all(pieces, "ry", split_axis=0, concat_axis=0, tiled=True)
+    hidden_part = jnp.sum(got, axis=0).reshape(local_experts, rows_here, quarter)
     act_part = jax.nn.silu(hidden_part).astype(jnp.bfloat16)
-    act_tile = jnp.broadcast_to(act_part[None], (rep_count,) + act_part.shape)
-    act_all = lax.all_to_all(act_tile, "rep", split_axis=0, concat_axis=0, tiled=True)
-    activated = jnp.transpose(act_all, (1, 2, 0, 3)).reshape(local_experts, rows_here, hid)
+    act_tile = jnp.broadcast_to(act_part[None], (chips,) + act_part.shape)
+    act_got = lax.all_to_all(act_tile, "ry", split_axis=0, concat_axis=0, tiled=True)
+    act_half = jnp.transpose(act_got, (1, 2, 0, 3)).reshape(local_experts, rows_here, half)
+    act_other = lax.ppermute(act_half, "rc", sibling)
+    activated = jnp.where(
+        core == 0,
+        jnp.concatenate([act_half, act_other], axis=2),
+        jnp.concatenate([act_other, act_half], axis=2),
+    )
     expert_out = jnp.einsum(
         "erh,ehd->erd", activated, down_weight, preferred_element_type=jnp.float32
     )
@@ -95,17 +110,22 @@
 
 
 def solution(mesh):
+    chips = mesh.shape["rep"] // 2
+    split = Mesh(
+        mesh.devices.reshape(chips, 2, mesh.shape["expert"]), ("ry", "rc", "expert")
+    )
+    rep = ("ry", "rc")
     in_specs = (
-        P("expert", "rep"),
-        P("rep"),
+        P("expert", rep),
+        P(rep),
         P("expert", None),
         P("expert"),
         P("expert", None),
         P("expert"),
-        P("expert", "rep", None),
-        P("expert", None, "rep"),
+        P("expert", rep, None),
+        P("expert", None, rep),
     )
-    out_specs = P("expert", "rep")
+    out_specs = P("expert", rep)
     return jax.shard_map(
-        per_device, mesh=mesh, in_specs=in_specs, out_specs=out_specs, check_vma=False
+        per_device, mesh=split, in_specs=in_specs, out_specs=out_specs, check_vma=False
     )

time: 188 us -> 191 us (1.016)
  blocking collectives: 133 us -> 66.2 us
  waiting for transfers between devices: 28.8 us -> 63.2 us
  starting transfers between devices: 7.21 us -> 29.9 us
  local copies, waits for them, and re-layouts: 8.57 us -> 19.2 us
  matrix products: 2.95 us -> 5.96 us
    all_to_all x3 -> x2, blocking collectives: 96.5 us -> 29.7 us  [the longest x1 18.1 us: per_device(): got = lax.all_to_all(pieces, 'ry', split_axis=0, concat_axis=0, tiled=True)]
    all_to_all x0 -> x1, waiting for transfers between devices: none -> 29.1 us  [per_device(): lax.all_to_all(outbound, 'expert', split_axis=1, concat_axis=1, tiled=True)]
    all_to_all x0 -> x1, starting transfers between devices: none -> 18.8 us  [per_device(): lax.all_to_all(outbound, 'expert', split_axis=1, concat_axis=1, tiled=True)]
    reshape x1 -> x2, local copies, waits for them, and re-layouts: 0.41 us -> 5.32 us  [the longest x1 3.99 us: per_device(): halves = partial_value.reshape(local_experts, rows_here, 2, half)]
    ppermute x0 -> x2, waiting for transfers between devices: none -> 4.5 us  [the longest x1 2.63 us: per_device(): half_sum = mine + lax.ppermute(theirs, 'rc', sibling)]
    slice x0 -> x1, local copies, waits for them, and re-layouts: none -> 4.02 us  [per_device(): mine = jnp.where(core == 0, halves[:, :, 0], halves[:, :, 1])]
    ppermute x0 -> x2, starting transfers between devices: none -> 3.84 us  [the longest x1 1.92 us: per_device(): act_other = lax.ppermute(act_half, 'rc', sibling)]
  transfers between devices with their start and end apart: 1 -> 4, of which waited for: 1 -> 4; matrix products, arithmetic and copies ran while one was open for 1% -> 1% of each run, Pallas kernels for 0% -> 0%
where the time goes in v4:
time: 191 us; the launch traced here: 190 us
  blocking collectives  66.2 us (35%)
  waiting for transfers between devices  63.2 us (33%)
  starting transfers between devices  29.9 us (16%)
  local copies, waits for them, and re-layouts  19.2 us (10%)
  matrix products  5.96 us (3%)
  other arithmetic  5.19 us (3%)
    all_to_all x1, waiting for transfers between devices, per_device(): lax.all_to_all(expert_out, 'expert', split_axis=1, concat_axis=1, tiled=T...  29.7 us
    all_to_all x1, waiting for transfers between devices, per_device(): lax.all_to_all(outbound, 'expert', split_axis=1, concat_axis=1, tiled=True)  29.1 us
    all_to_all x1, blocking collectives, per_device(): lax.all_to_all(leaving, 'expert', split_axis=0, concat_axis=0, tiled=True)  21.6 us
    all_to_all x1, starting transfers between devices, per_device(): lax.all_to_all(outbound, 'expert', split_axis=1, concat_axis=1, tiled=True)  18.8 us
    all_to_all x1, blocking collectives, per_device(): got = lax.all_to_all(pieces, 'ry', split_axis=0, concat_axis=0, tiled=True)  18.1 us
    psum x1, blocking collectives, per_device(): squares = lax.psum(jnp.sum(widened * widened, axis=1), ('ry', 'rc'))  14.9 us
    all_to_all x1, blocking collectives, per_device(): lax.all_to_all(act_tile, 'ry', split_axis=0, concat_axis=0, tiled=True)  11.6 us
    all_to_all x1, starting transfers between devices, per_device(): lax.all_to_all(expert_out, 'expert', split_axis=1, concat_axis=1, tiled=T...  7.23 us
  transfers between devices with their start and end apart: 4, of which 4 were waited for; matrix products, arithmetic and copies ran while one was open for 1% of the time, Pallas kernels for 0%

profile of v4, /device:TPU:6, one launch (start us, length us, event | category | flops | bytes accessed | tf_op | source)
XLA Modules:
  0.0 189.9 jit_solution(11392412334655403800)
XLA Ops:
  0.0 0.9 copy.69
  4.2 0.9 convert_reduce_fusion
  5.2 14.9 %psum.7 = f32[128]{0:T(128)S(1)} all-reduce(f32[128]{0:T(128)S(1)} %fusion.9), channel_id=1, replica_groups=mesh['ry'=4,'rc'=2,'expert'=64] {'ry','rc'}, use_global_device_ids=true, to_apply=%region_6.7 | all-reduce | flops 128 | bytes 1024 | tf_op jit(solution)/shard_map/psum | solution.py:35
  20.6 1.0 copy.80
  21.6 18.8 %all-to-all-start = ((bf16[2,64,4,512]{3,2,0,1:T(4,128)(2,1)}), bf16[2,64,4,512]{3,2,0,1:T(4,128)(2,1)S(1)}, u32[]{:S(2)}, u32[]{:S(2)}) async-start(bf16[2,64,4,512]{3,2,0,1:T(4,128)(2,1)} %copy.80), calls=%async_computation | async-start | bytes 1048576 | tf_op jit(solution)/shard_map/all_to_all | solution.py:45
  40.4 29.1 %all-to-all-done = bf16[2,64,4,512]{3,2,0,1:T(4,128)(2,1)S(1)} async-done(((bf16[2,64,4,512]{3,2,0,1:T(4,128)(2,1)}), bf16[2,64,4,512]{3,2,0,1:T(4,128)(2,1)S(1)}, u32[]{:S(2)}, u32[]{:S(2)}) %all-to-all-start) | async-done | bytes 524320 | tf_op jit(solution)/shard_map/all_to_all | solution.py:45
  69.8 2.1 %fusion.35 = f32[2,256,1024]{2,1,0:T(8,128)} fusion(bf16[2,256,512]{2,1,0:T(8,128)(2,1)S(1)} %reshape.159, bf16[2,512,1024]{2,1,0:T(8,128)(2,1)S(1)} %copy-done), kind=kOutput, calls=%fused_computation.71 | convolution fusion | flops 536870912 | bytes 4718592 | tf_op jit(solution)/shard_map/erd,edh->erh/dot_general | solution.py:49
  71.8 4.0 %reshape.160 = f32[2,256,2,512]{3,2,1,0:T(2,128)} reshape(f32[2,256,1024]{2,1,0:T(8,128)} %fusion.35) | data formatting | bytes 4194304 | tf_op jit(solution)/shard_map/reshape | solution.py:57
  75.8 4.0 %fusion.34 = (f32[2,256,1,512]{3,2,1,0:T(1,128)S(1)}, f32[2,256,1,512]{3,2,1,0:T(1,128)S(1)}) fusion(f32[2,256,2,512]{3,2,1,0:T(2,128)} %reshape.160), kind=kLoop, calls=%fused_computation.70 | loop fusion | bytes 4194304 | tf_op jit(solution)/shard_map/slice | solution.py:58
  80.1 1.9 %collective-permute-start = (f32[2,256,512]{2,1,0:T(8,128)S(1)}, f32[2,256,512]{2,1,0:T(8,128)S(1)}, u32[]{:S(2)}, u32[]{:S(2)}) collective-permute-start(f32[2,256,512]{2,1,0:T(8,128)S(1)} %select_bitcast_fusion), channel_id=1, source_target_pairs={{0,64},{64,0},{1,65},{65,1},{2,66},{66,2},{3,67},{67,3},{4,68},{68... | collective-permute-start | bytes 3145736 | tf_op jit(solution)/shard_map/ppermute | solution.py:60
  82.0 2.6 %collective-permute-done = f32[2,256,512]{2,1,0:T(8,128)S(1)} collective-permute-done((f32[2,256,512]{2,1,0:T(8,128)S(1)}, f32[2,256,512]{2,1,0:T(8,128)S(1)}, u32[]{:S(2)}, u32[]{:S(2)}) %collective-permute-start) | collective-permute-done | bytes 1048608 | tf_op jit(solution)/shard_map/ppermute | solution.py:60
  85.0 1.3 reshape.161
  86.3 1.3 copy.84
  87.6 18.1 %all_to_all.25 = f32[4,512,128]{2,1,0:T(8,128)S(1)} all-to-all(f32[4,512,128]{2,1,0:T(8,128)S(1)} %copy.84), channel_id=1, replica_groups=mesh['ry'=4,'rc'=2,'expert'=64] {'ry'}, dimensions={0} | all-to-all | bytes 2097152 | tf_op jit(solution)/shard_map/all_to_all | solution.py:63
  105.9 11.6 %all_to_all.26 = bf16[4,2,256,128]{3,2,1,0:T(8,128)(2,1)S(1)} all-to-all(bf16[4,2,256,128]{3,2,1,0:T(8,128)(2,1)S(1)} %broadcast_in_dim.61), channel_id=1, replica_groups=mesh['ry'=4,'rc'=2,'expert'=64] {'ry'}, dimensions={0} | all-to-all | bytes 1048576 | tf_op jit(solution)/shard_map/all_to_all | solution.py:67
  117.7 1.9 %collective-permute-start.1 = (bf16[2,256,512]{1,2,0:T(8,128)(2,1)S(1)}, bf16[2,256,512]{1,2,0:T(8,128)(2,1)S(1)}, u32[]{:S(2)}, u32[]{:S(2)}) collective-permute-start(bf16[2,256,512]{1,2,0:T(8,128)(2,1)S(1)} %bitcast.30), channel_id=1, source_target_pairs={{0,64},{64,0},{1,65},{65,1},{2,66},{66,2},{3,67},{67,3},{4,68},{68... | collective-permute-start | bytes 1572872 | tf_op jit(solution)/shard_map/ppermute | solution.py:69
  119.7 1.9 collective-permute-done.1
  121.6 3.1 %convolution_convert_fusion = bf16[2,256,512]{2,1,0:T(8,128)(2,1)} fusion(bf16[2,1024,512]{2,1,0:T(8,128)(2,1)} %param.15, bf16[2,256,512]{1,2,0:T(8,128)(2,1)S(1)} %collective-permute-done.1, bf16[2,256,512]{1,2,0:T(8,128)(2,1)S(1)} %bitcast.31, pred[]{:T(512)S(6)} %eq.82), kind=kOutput, calls=%fused_computation.6 | convolution fusion | flops 541851648 | bytes 3670017 | tf_op jit(solution)/shard_map/erh,ehd->erd/dot_general | solution.py:75
  124.7 1.2 reshape.164
  125.9 1.0 copy.87
  126.9 7.2 %all-to-all-start.3 = ((bf16[2,64,4,512]{3,2,0,1:T(4,128)(2,1)}), bf16[2,64,4,512]{3,2,0,1:T(4,128)(2,1)S(1)}, u32[]{:S(2)}, u32[]{:S(2)}) async-start(bf16[2,64,4,512]{3,2,0,1:T(4,128)(2,1)} %copy.87), calls=%async_computation.3 | async-start | bytes 1048576 | tf_op jit(solution)/shard_map/all_to_all | solution.py:81
  134.7 1.0 scatter_custom_fusion
  136.5 29.7 %all-to-all-done.3 = bf16[2,64,4,512]{3,2,0,1:T(4,128)(2,1)S(1)} async-done(((bf16[2,64,4,512]{3,2,0,1:T(4,128)(2,1)}), bf16[2,64,4,512]{3,2,0,1:T(4,128)(2,1)S(1)}, u32[]{:S(2)}, u32[]{:S(2)}) %all-to-all-start.3) | async-done | bytes 524320 | tf_op jit(solution)/shard_map/all_to_all | solution.py:81
  167.6 21.6 %all_to_all.27 = f32[64,1,512]{2,1,0:T(1,128)S(1)} all-to-all(f32[64,1,512]{2,1,0:T(1,128)S(1)} %copy.89), channel_id=1, replica_groups=mesh['ry'=4,'rc'=2,'expert'=64] {'expert'}, dimensions={0} | all-to-all | bytes 262144 | tf_op jit(solution)/shard_map/all_to_all | solution.py:108
  (63 shorter events, 8.5 us)
Async XLA Ops:
  0.0 69.7 %copy-start = (bf16[2,512,1024]{2,1,0:T(8,128)(2,1)S(1)}, bf16[2,512,1024]{2,1,0:T(8,128)(2,1)}, u32[]{:S(2)}) copy-start(bf16[2,512,1024]{2,1,0:T(8,128)(2,1)} %param.14) | copy-start | bytes 6291460
  1.0 4.1 %copy-start.1 = (bf16[128,512]{1,0:T(8,128)(2,1)S(1)}, bf16[128,512]{1,0:T(8,128)(2,1)}, u32[]{:S(2)}) copy-start(bf16[128,512]{1,0:T(8,128)(2,1)} %param.8) | copy-start | bytes 393220
  2.6 17.5 %copy-start.6 = (f32[512]{0:T(512)S(1)}, f32[512]{0:T(512)}, u32[]{:S(2)}) copy-start(f32[512]{0:T(512)} %param.9) | copy-start | bytes 6148
  4.1 16.0 %copy-start.2 = (s32[128,8]{1,0:T(8,128)}, s32[128,8]{1,0:T(8,128)S(1)}, u32[]{:S(2)}) copy-start(s32[128,8]{1,0:T(8,128)S(1)} %fusion.23) | copy-start | bytes 12292
  21.6 47.9 %all-to-all-start = ((bf16[2,64,4,512]{3,2,0,1:T(4,128)(2,1)}), bf16[2,64,4,512]{3,2,0,1:T(4,128)(2,1)S(1)}, u32[]{:S(2)}, u32[]{:S(2)}) async-start(bf16[2,64,4,512]{3,2,0,1:T(4,128)(2,1)} %copy.80), calls=%async_computation | async-start | bytes 1048576 | tf_op jit(solution)/shard_map/all_to_all | solution.py:45
  80.1 4.6 %collective-permute-start = (f32[2,256,512]{2,1,0:T(8,128)S(1)}, f32[2,256,512]{2,1,0:T(8,128)S(1)}, u32[]{:S(2)}, u32[]{:S(2)}) collective-permute-start(f32[2,256,512]{2,1,0:T(8,128)S(1)} %select_bitcast_fusion), channel_id=1, source_target_pairs={{0,64},{64,0},{1,65},{65,1},{2,66},{66,2},{3,67},{67,3},{4,68},{68... | collective-permute-start | bytes 3145736 | tf_op jit(solution)/shard_map/ppermute | solution.py:60
  117.7 3.8 %collective-permute-start.1 = (bf16[2,256,512]{1,2,0:T(8,128)(2,1)S(1)}, bf16[2,256,512]{1,2,0:T(8,128)(2,1)S(1)}, u32[]{:S(2)}, u32[]{:S(2)}) collective-permute-start(bf16[2,256,512]{1,2,0:T(8,128)(2,1)S(1)} %bitcast.30), channel_id=1, source_target_pairs={{0,64},{64,0},{1,65},{65,1},{2,66},{66,2},{3,67},{67,3},{4,68},{68... | collective-permute-start | bytes 1572872 | tf_op jit(solution)/shard_map/ppermute | solution.py:69
  124.7 9.4 %copy-start.5 = (f32[128,8]{0,1:T(8,128)S(1)}, f32[128,8]{0,1:T(8,128)}, u32[]{:S(2)}) copy-start(f32[128,8]{0,1:T(8,128)} %param.10) | copy-start | bytes 12292
  124.7 9.5 %copy-start.4 = (s32[128]{0:T(128)S(1)}, s32[128]{0:T(128)}, u32[]{:S(2)}) copy-start(s32[128]{0:T(128)} %param.13) | copy-start | bytes 1540
  124.7 10.0 %copy-start.7 = (s32[128]{0:T(128)S(1)}, s32[128]{0:T(128)}, u32[]{:S(2)}) copy-start(s32[128]{0:T(128)} %param.11) | copy-start | bytes 1540
  124.7 11.0 %copy-start.3 = (s32[128,8]{1,0:T(8,128)S(1)}, s32[128,8]{1,0:T(8,128)}, u32[]{:S(2)}) copy-start(s32[128,8]{1,0:T(8,128)} %copy-done.2) | copy-start | bytes 12292
  126.9 39.2 %all-to-all-start.3 = ((bf16[2,64,4,512]{3,2,0,1:T(4,128)(2,1)}), bf16[2,64,4,512]{3,2,0,1:T(4,128)(2,1)S(1)}, u32[]{:S(2)}, u32[]{:S(2)}) async-start(bf16[2,64,4,512]{3,2,0,1:T(4,128)(2,1)} %copy.87), calls=%async_computation.3 | async-start | bytes 1048576 | tf_op jit(solution)/shard_map/all_to_all | solution.py:81

commit v5 on v4

--- a/solution.py
+++ b/solution.py
@@ -52,29 +52,26 @@
     core = lax.axis_index("rc")
     sibling = [(i, 1 - i) for i in range(2)]
     chips = lax.axis_size("ry")
-    half = hid // 2
-    quarter = half // chips
-    halves = partial_value.reshape(local_experts, rows_here, 2, half)
-    mine = jnp.where(core == 0, halves[:, :, 0], halves[:, :, 1])
-    theirs = jnp.where(core == 0, halves[:, :, 1], halves[:, :, 0])
+    quarter = hid // (2 * chips)
+    pieces = partial_value.reshape(local_experts * rows_here, 2 * chips, quarter)
+    pieces = jnp.transpose(pieces, (1, 0, 2)).reshape(2, chips, local_experts * rows_here, quarter)
+    mine = lax.dynamic_index_in_dim(pieces, core, axis=0, keepdims=False)
+    theirs = lax.dynamic_index_in_dim(pieces, 1 - core, axis=0, keepdims=False)
     half_sum = mine + lax.ppermute(theirs, "rc", sibling)
-    pieces = half_sum.reshape(local_experts * rows_here, chips, quarter)
-    pieces = jnp.transpose(pieces, (1, 0, 2))
-    got = lax.all_to_all(pieces, "ry", split_axis=0, concat_axis=0, tiled=True)
-    hidden_part = jnp.sum(got, axis=0).reshape(local_experts, rows_here, quarter)
+    got = lax.all_to_all(half_sum, "ry", split_axis=0, concat_axis=0, tiled=True)
+    hidden_part = jnp.sum(got, axis=0)
     act_part = jax.nn.silu(hidden_part).astype(jnp.bfloat16)
     act_tile = jnp.broadcast_to(act_part[None], (chips,) + act_part.shape)
-    act_got = lax.all_to_all(act_tile, "ry", split_axis=0, concat_axis=0, tiled=True)
-    act_half = jnp.transpose(act_got, (1, 2, 0, 3)).reshape(local_experts, rows_here, half)
+    act_half = lax.all_to_all(act_tile, "ry", split_axis=0, concat_axis=0, tiled=True)
     act_other = lax.ppermute(act_half, "rc", sibling)
-    activated = jnp.where(
-        core == 0,
-        jnp.concatenate([act_half, act_other], axis=2),
-        jnp.concatenate([act_other, act_half], axis=2),
-    )
+    down_q = down_weight.reshape(local_experts, 2, chips, quarter, feat_width)
+    down_mine = lax.dynamic_index_in_dim(down_q, core, axis=1, keepdims=False)
+    down_other = lax.dynamic_index_in_dim(down_q, 1 - core, axis=1, keepdims=False)
+    act_half = act_half.reshape(chips, local_experts, rows_here, quarter)
+    act_other = act_other.reshape(chips, local_experts, rows_here, quarter)
     expert_out = jnp.einsum(
-        "erh,ehd->erd", activated, down_weight, preferred_element_type=jnp.float32
-    )
+        "qerj,eqjd->erd", act_half, down_mine, preferred_element_type=jnp.float32
+    ) + jnp.einsum("qerj,eqjd->erd", act_other, down_other, preferred_element_type=jnp.float32)
     expert_out = expert_out.astype(jnp.bfloat16).reshape(
         local_experts, owner_count, item_count, feat_width
     )

time: 191 us -> 175 us (0.916)
  local copies, waits for them, and re-layouts: 19.2 us -> 8.37 us
  matrix products: 5.96 us -> 2.32 us
    reshape x2 -> x0, local copies, waits for them, and re-layouts: 5.32 us -> none  [the longest x1 3.99 us: per_device(): halves = partial_value.reshape(local_experts, rows_here, 2, half)]
    slice x1 -> x0, local copies, waits for them, and re-layouts: 4.02 us -> none  [per_device(): mine = jnp.where(core == 0, halves[:, :, 0], halves[:, :, 1])]
    dot_general x1 -> x2, matrix products: 3.15 us -> 0.87 us  [the longest x1 0.44 us: per_device(): jnp.einsum('qerj,eqjd->erd', act_other, down_other, preferred_element_typ...]
  transfers between devices with their start and end apart: 4 -> 4, of which waited for: 4 -> 4; matrix products, arithmetic and copies ran while one was open for 1% -> 2% of each run, Pallas kernels for 0% -> 0%
where the time goes in v5:
time: 175 us
  blocking collectives  66.3 us (38%)
  waiting for transfers between devices  62.6 us (36%)
  starting transfers between devices  29.8 us (17%)
  local copies, waits for them, and re-layouts  8.37 us (5%)
  other arithmetic  4.74 us (3%)
  matrix products  2.32 us (1%)
    all_to_all x1, waiting for transfers between devices, per_device(): lax.all_to_all(expert_out, 'expert', split_axis=1, concat_axis=1, tiled=T...  29.7 us
    all_to_all x1, waiting for transfers between devices, per_device(): lax.all_to_all(outbound, 'expert', split_axis=1, concat_axis=1, tiled=True)  29.1 us
    all_to_all x1, blocking collectives, per_device(): lax.all_to_all(leaving, 'expert', split_axis=0, concat_axis=0, tiled=True)  21.6 us
    all_to_all x1, starting transfers between devices, per_device(): lax.all_to_all(outbound, 'expert', split_axis=1, concat_axis=1, tiled=True)  18.8 us
    all_to_all x1, blocking collectives, per_device(): lax.all_to_all(half_sum, 'ry', split_axis=0, concat_axis=0, tiled=True)  18.1 us
    psum x1, blocking collectives, per_device(): squares = lax.psum(jnp.sum(widened * widened, axis=1), ('ry', 'rc'))  14.9 us
    all_to_all x1, blocking collectives, per_device(): lax.all_to_all(act_tile, 'ry', split_axis=0, concat_axis=0, tiled=True)  11.7 us
    all_to_all x1, starting transfers between devices, per_device(): lax.all_to_all(expert_out, 'expert', split_axis=1, concat_axis=1, tiled=T...  7.21 us
  transfers between devices with their start and end apart: 4, of which 4 were waited for; matrix products, arithmetic and copies ran while one was open for 2% of the time, Pallas kernels for 0%

profile of v5, /device:TPU:6, one launch (start us, length us, event | category | flops | bytes accessed | tf_op | source)
XLA Modules:
  0.0 174.6 jit_solution(12517477609156436996)
XLA Ops:
  0.0 0.9 copy.66
  1.1 0.7 broadcast_subtract_fusion
  1.8 0.7 broadcast_compare_fusion
  3.4 0.5 fusion.3
  4.2 0.9 convert_reduce_fusion
  5.2 14.9 %psum.7 = f32[128]{0:T(128)S(1)} all-reduce(f32[128]{0:T(128)S(1)} %fusion.6), channel_id=1, replica_groups=mesh['ry'=4,'rc'=2,'expert'=64] {'ry','rc'}, use_global_device_ids=true, to_apply=%region_6.7 | all-reduce | flops 128 | bytes 1024 | tf_op jit(solution)/shard_map/psum | solution.py:35
  20.6 1.0 copy.77
  21.6 18.8 %all-to-all-start = ((bf16[2,64,4,512]{3,2,0,1:T(4,128)(2,1)}), bf16[2,64,4,512]{3,2,0,1:T(4,128)(2,1)S(1)}, u32[]{:S(2)}, u32[]{:S(2)}) async-start(bf16[2,64,4,512]{3,2,0,1:T(4,128)(2,1)} %copy.77), calls=%async_computation | async-start | bytes 1048576 | tf_op jit(solution)/shard_map/all_to_all | solution.py:45
  40.4 29.1 %all-to-all-done = bf16[2,64,4,512]{3,2,0,1:T(4,128)(2,1)S(1)} async-done(((bf16[2,64,4,512]{3,2,0,1:T(4,128)(2,1)}), bf16[2,64,4,512]{3,2,0,1:T(4,128)(2,1)S(1)}, u32[]{:S(2)}, u32[]{:S(2)}) %all-to-all-start) | async-done | bytes 524320 | tf_op jit(solution)/shard_map/all_to_all | solution.py:45
  69.8 0.7 fusion.30
  71.4 1.9 %collective-permute-start = (f32[4,512,128]{2,1,0:T(8,128)S(1)}, f32[4,512,128]{2,1,0:T(8,128)S(1)}, u32[]{:S(2)}, u32[]{:S(2)}) collective-permute-start(f32[4,512,128]{2,1,0:T(8,128)S(1)} %bitcast.54), channel_id=1, source_target_pairs={{0,64},{64,0},{1,65},{65,1},{2,66},{66,2},{3,67},{67,3},{4,68},{68... | collective-permute-start | bytes 3145736 | tf_op jit(solution)/shard_map/ppermute | solution.py:60
  73.3 2.6 %collective-permute-done = f32[4,512,128]{2,1,0:T(8,128)S(1)} collective-permute-done((f32[4,512,128]{2,1,0:T(8,128)S(1)}, f32[4,512,128]{2,1,0:T(8,128)S(1)}, u32[]{:S(2)}, u32[]{:S(2)}) %collective-permute-start) | collective-permute-done | bytes 1048608 | tf_op jit(solution)/shard_map/ppermute | solution.py:60
  76.1 18.1 %all_to_all.25 = f32[4,512,128]{2,1,0:T(8,128)S(1)} all-to-all(f32[4,512,128]{2,1,0:T(8,128)S(1)} %fusion.2), channel_id=1, replica_groups=mesh['ry'=4,'rc'=2,'expert'=64] {'ry'}, dimensions={0} | all-to-all | bytes 2097152 | tf_op jit(solution)/shard_map/all_to_all | solution.py:61
  94.4 11.7 %all_to_all.26 = bf16[4,512,128]{2,1,0:T(8,128)(2,1)S(1)} all-to-all(bf16[4,512,128]{2,1,0:T(8,128)(2,1)S(1)} %broadcast_in_dim.61), channel_id=1, replica_groups=mesh['ry'=4,'rc'=2,'expert'=64] {'ry'}, dimensions={0} | all-to-all | bytes 1048576 | tf_op jit(solution)/shard_map/all_to_all | solution.py:65
  106.2 1.9 %collective-permute-start.1 = (bf16[4,512,128]{2,1,0:T(8,128)(2,1)S(1)}, bf16[4,512,128]{2,1,0:T(8,128)(2,1)S(1)}, u32[]{:S(2)}, u32[]{:S(2)}) collective-permute-start(bf16[4,512,128]{2,1,0:T(8,128)(2,1)S(1)} %all_to_all.26), channel_id=1, source_target_pairs={{0,64},{64,0},{1,65},{65,1},{2,66},{66,2},{3,67},{67,3},{4,68},{68... | collective-permute-start | bytes 1572872 | tf_op jit(solution)/shard_map/ppermute | solution.py:66
  108.7 1.2 collective-permute-done.1
  110.6 1.0 copy.83
  111.5 7.2 %all-to-all-start.3 = ((bf16[2,64,4,512]{3,2,0,1:T(4,128)(2,1)}), bf16[2,64,4,512]{3,2,0,1:T(4,128)(2,1)S(1)}, u32[]{:S(2)}, u32[]{:S(2)}) async-start(bf16[2,64,4,512]{3,2,0,1:T(4,128)(2,1)} %copy.83), calls=%async_computation.3 | async-start | bytes 1048576 | tf_op jit(solution)/shard_map/all_to_all | solution.py:78
  119.4 1.0 scatter_custom_fusion
  120.4 0.7 select_reduce_fusion
  121.1 29.7 %all-to-all-done.3 = bf16[2,64,4,512]{3,2,0,1:T(4,128)(2,1)S(1)} async-done(((bf16[2,64,4,512]{3,2,0,1:T(4,128)(2,1)}), bf16[2,64,4,512]{3,2,0,1:T(4,128)(2,1)S(1)}, u32[]{:S(2)}, u32[]{:S(2)}) %all-to-all-start.3) | async-done | bytes 524320 | tf_op jit(solution)/shard_map/all_to_all | solution.py:78
  151.5 0.7 gather_fusion
  152.3 21.6 %all_to_all.27 = f32[64,1,512]{2,1,0:T(1,128)S(1)} all-to-all(f32[64,1,512]{2,1,0:T(1,128)S(1)} %copy.85), channel_id=1, replica_groups=mesh['ry'=4,'rc'=2,'expert'=64] {'expert'}, dimensions={0} | all-to-all | bytes 262144 | tf_op jit(solution)/shard_map/all_to_all | solution.py:105
  173.9 0.7 copy.102
  (64 shorter events, 6.1 us)
Async XLA Ops:
  0.0 69.8 %copy-start = (bf16[2,512,1024]{2,1,0:T(8,128)(2,1)S(1)}, bf16[2,512,1024]{2,1,0:T(8,128)(2,1)}, u32[]{:S(2)}) copy-start(bf16[2,512,1024]{2,1,0:T(8,128)(2,1)} %param.14) | copy-start | bytes 6291460
  1.0 4.1 %copy-start.2 = (bf16[128,512]{1,0:T(8,128)(2,1)S(1)}, bf16[128,512]{1,0:T(8,128)(2,1)}, u32[]{:S(2)}) copy-start(bf16[128,512]{1,0:T(8,128)(2,1)} %param.8) | copy-start | bytes 393220
  2.6 17.5 %copy-start.7 = (f32[512]{0:T(512)S(1)}, f32[512]{0:T(512)}, u32[]{:S(2)}) copy-start(f32[512]{0:T(512)} %param.9) | copy-start | bytes 6148
  4.1 16.0 %copy-start.3 = (s32[128,8]{1,0:T(8,128)}, s32[128,8]{1,0:T(8,128)S(1)}, u32[]{:S(2)}) copy-start(s32[128,8]{1,0:T(8,128)S(1)} %fusion.20) | copy-start | bytes 12292
  21.6 47.9 %all-to-all-start = ((bf16[2,64,4,512]{3,2,0,1:T(4,128)(2,1)}), bf16[2,64,4,512]{3,2,0,1:T(4,128)(2,1)S(1)}, u32[]{:S(2)}, u32[]{:S(2)}) async-start(bf16[2,64,4,512]{3,2,0,1:T(4,128)(2,1)} %copy.77), calls=%async_computation | async-start | bytes 1048576 | tf_op jit(solution)/shard_map/all_to_all | solution.py:45
  71.4 4.6 %collective-permute-start = (f32[4,512,128]{2,1,0:T(8,128)S(1)}, f32[4,512,128]{2,1,0:T(8,128)S(1)}, u32[]{:S(2)}, u32[]{:S(2)}) collective-permute-start(f32[4,512,128]{2,1,0:T(8,128)S(1)} %bitcast.54), channel_id=1, source_target_pairs={{0,64},{64,0},{1,65},{65,1},{2,66},{66,2},{3,67},{67,3},{4,68},{68... | collective-permute-start | bytes 3145736 | tf_op jit(solution)/shard_map/ppermute | solution.py:60
  94.3 13.8 %copy-start.1 = (bf16[2,1024,512]{2,1,0:T(8,128)(2,1)S(1)}, bf16[2,1024,512]{2,1,0:T(8,128)(2,1)}, u32[]{:S(2)}) copy-start(bf16[2,1024,512]{2,1,0:T(8,128)(2,1)} %param.15) | copy-start | bytes 6291460
  106.2 3.8 %collective-permute-start.1 = (bf16[4,512,128]{2,1,0:T(8,128)(2,1)S(1)}, bf16[4,512,128]{2,1,0:T(8,128)(2,1)S(1)}, u32[]{:S(2)}, u32[]{:S(2)}) collective-permute-start(bf16[4,512,128]{2,1,0:T(8,128)(2,1)S(1)} %all_to_all.26), channel_id=1, source_target_pairs={{0,64},{64,0},{1,65},{65,1},{2,66},{66,2},{3,67},{67,3},{4,68},{68... | collective-permute-start | bytes 1572872 | tf_op jit(solution)/shard_map/ppermute | solution.py:66
  110.4 8.4 %copy-start.6 = (f32[128,8]{0,1:T(8,128)S(1)}, f32[128,8]{0,1:T(8,128)}, u32[]{:S(2)}) copy-start(f32[128,8]{0,1:T(8,128)} %param.10) | copy-start | bytes 12292
  110.4 8.5 %copy-start.5 = (s32[128]{0:T(128)S(1)}, s32[128]{0:T(128)}, u32[]{:S(2)}) copy-start(s32[128]{0:T(128)} %param.13) | copy-start | bytes 1540
  110.4 8.9 %copy-start.8 = (s32[128]{0:T(128)S(1)}, s32[128]{0:T(128)}, u32[]{:S(2)}) copy-start(s32[128]{0:T(128)} %param.11) | copy-start | bytes 1540
  110.6 9.8 %copy-start.4 = (s32[128,8]{1,0:T(8,128)S(1)}, s32[128,8]{1,0:T(8,128)}, u32[]{:S(2)}) copy-start(s32[128,8]{1,0:T(8,128)} %copy-done.3) | copy-start | bytes 12292
  111.5 39.2 %all-to-all-start.3 = ((bf16[2,64,4,512]{3,2,0,1:T(4,128)(2,1)}), bf16[2,64,4,512]{3,2,0,1:T(4,128)(2,1)S(1)}, u32[]{:S(2)}, u32[]{:S(2)}) async-start(bf16[2,64,4,512]{3,2,0,1:T(4,128)(2,1)} %copy.83), calls=%async_computation.3 | async-start | bytes 1048576 | tf_op jit(solution)/shard_map/all_to_all | solution.py:78

commit v6 on v5

--- a/solution.py
+++ b/solution.py
@@ -32,7 +32,12 @@
     local_id = route_flat % local_experts
     slot_index = (local_id * owner_count + owner_id) * capacity + position
     slot_index = jnp.where(pair_live > 0, slot_index, slot_total)
-    squares = lax.psum(jnp.sum(widened * widened, axis=1), ("ry", "rc"))
+    squares = jnp.sum(widened * widened, axis=1)
+    chip = lax.axis_index("ry")
+    chips = lax.axis_size("ry")
+    for axis, bit in (("rc", 1), ("ry", 1), ("ry", 2)):
+        pairs = [(i, i ^ bit) for i in range(lax.axis_size(axis))]
+        squares = squares + lax.ppermute(squares, axis, pairs)
     rinv_rows = lax.rsqrt(squares / (feat_width * rep_count) + 1e-06)
     normed = (widened * rinv_rows[:, None] * norm_gain[None, :]).astype(jnp.bfloat16)
     slot_ids = jnp.arange(slot_total, dtype=jnp.int32)
@@ -51,22 +56,36 @@
     )
     core = lax.axis_index("rc")
     sibling = [(i, 1 - i) for i in range(2)]
-    chips = lax.axis_size("ry")
     quarter = hid // (2 * chips)
     pieces = partial_value.reshape(local_experts * rows_here, 2 * chips, quarter)
     pieces = jnp.transpose(pieces, (1, 0, 2)).reshape(2, chips, local_experts * rows_here, quarter)
     mine = lax.dynamic_index_in_dim(pieces, core, axis=0, keepdims=False)
     theirs = lax.dynamic_index_in_dim(pieces, 1 - core, axis=0, keepdims=False)
     half_sum = mine + lax.ppermute(theirs, "rc", sibling)
-    got = lax.all_to_all(half_sum, "ry", split_axis=0, concat_axis=0, tiled=True)
-    hidden_part = jnp.sum(got, axis=0)
+    by_bit = half_sum.reshape(2, 2, local_experts * rows_here, quarter)
+    low_bit, high_bit = chip % 2, chip // 2
+    keep = lax.dynamic_index_in_dim(by_bit, low_bit, axis=1, keepdims=False)
+    give = lax.dynamic_index_in_dim(by_bit, 1 - low_bit, axis=1, keepdims=False)
+    keep = keep + lax.ppermute(give, "ry", [(i, i ^ 1) for i in range(chips)])
+    give = lax.dynamic_index_in_dim(keep, 1 - high_bit, axis=0, keepdims=False)
+    keep = lax.dynamic_index_in_dim(keep, high_bit, axis=0, keepdims=False)
+    hidden_part = keep + lax.ppermute(give, "ry", [(i, i ^ 2) for i in range(chips)])
     act_part = jax.nn.silu(hidden_part).astype(jnp.bfloat16)
-    act_tile = jnp.broadcast_to(act_part[None], (chips,) + act_part.shape)
-    act_half = lax.all_to_all(act_tile, "ry", split_axis=0, concat_axis=0, tiled=True)
+    act_two = jnp.stack(
+        [act_part, lax.ppermute(act_part, "ry", [(i, i ^ 2) for i in range(chips)])]
+    )
+    act_half = jnp.concatenate(
+        [act_two, lax.ppermute(act_two, "ry", [(i, i ^ 1) for i in range(chips)])]
+    )
+    order = jnp.array([0, 2, 1, 3], jnp.int32)
     act_other = lax.ppermute(act_half, "rc", sibling)
     down_q = down_weight.reshape(local_experts, 2, chips, quarter, feat_width)
-    down_mine = lax.dynamic_index_in_dim(down_q, core, axis=1, keepdims=False)
-    down_other = lax.dynamic_index_in_dim(down_q, 1 - core, axis=1, keepdims=False)
+    down_mine = jnp.take(
+        lax.dynamic_index_in_dim(down_q, core, axis=1, keepdims=False), chip ^ order, axis=1
+    )
+    down_other = jnp.take(
+        lax.dynamic_index_in_dim(down_q, 1 - core, axis=1, keepdims=False), chip ^ order, axis=1
+    )
     act_half = act_half.reshape(chips, local_experts, rows_here, quarter)
     act_other = act_other.reshape(chips, local_experts, rows_here, quarter)
     expert_out = jnp.einsum(

time: 175 us -> 201 us (1.15)
  blocking collectives: 66.3 us -> 21.5 us
  waiting for transfers between devices: 62.6 us -> 91.4 us
  starting transfers between devices: 29.8 us -> 57.5 us
  local copies, waits for them, and re-layouts: 8.37 us -> 15.8 us
  other arithmetic: 4.74 us -> 8.97 us
    all_to_all x2 -> x0, blocking collectives: 29.8 us -> none  [the longest x1 18.1 us: per_device(): lax.all_to_all(half_sum, 'ry', split_axis=0, concat_axis=0, tiled=True)]
    ppermute x0 -> x7, waiting for transfers between devices: none -> 28.9 us  [the longest x1 12.3 us: per_device(): keep = keep + lax.ppermute(give, 'ry', [(i, i ^ 1) for i in range(chips)])]
    ppermute x0 -> x7, starting transfers between devices: none -> 27.7 us  [the longest x3 10.5 us: per_device(): squares = squares + lax.ppermute(squares, axis, pairs)]
    psum x1 -> x0, blocking collectives: 14.9 us -> none  [per_device(): squares = lax.psum(jnp.sum(widened * widened, axis=1), ('ry', 'rc'))]
    gather x0 -> x2, local copies, waits for them, and re-layouts: none -> 4.44 us  [the longest x1 2.81 us: per_device(): jnp.take(lax.dynamic_index_in_dim(down_q, 1 - core, axis=1, keepdims=Fals...]
    unnamed x23 -> x33, local copies, waits for them, and re-layouts: 2.29 us -> 4.11 us
  transfers between devices with their start and end apart: 4 -> 11, of which waited for: 4 -> 9; matrix products, arithmetic and copies ran while one was open for 2% -> 6% of each run, Pallas kernels for 0% -> 0%
where the time goes in v6:
time: 201 us; the launch traced here: 200 us
  waiting for transfers between devices  91.4 us (45%)
  starting transfers between devices  57.5 us (29%)
  blocking collectives  21.5 us (11%)
  local copies, waits for them, and re-layouts  15.8 us (8%)
  other arithmetic  8.97 us (4%)
  matrix products  3.98 us (2%)
    all_to_all x1, waiting for transfers between devices, per_device(): lax.all_to_all(expert_out, 'expert', split_axis=1, concat_axis=1, tiled=T...  30 us
    all_to_all x1, waiting for transfers between devices, per_device(): lax.all_to_all(outbound, 'expert', split_axis=1, concat_axis=1, tiled=True)  29.6 us
    all_to_all x1, blocking collectives, per_device(): lax.all_to_all(leaving, 'expert', split_axis=0, concat_axis=0, tiled=True)  21.5 us
    all_to_all x1, starting transfers between devices, per_device(): lax.all_to_all(outbound, 'expert', split_axis=1, concat_axis=1, tiled=True)  18.8 us
    ppermute x1, waiting for transfers between devices, per_device(): keep = keep + lax.ppermute(give, 'ry', [(i, i ^ 1) for i in range(chips)])  12.3 us
    ppermute x3, starting transfers between devices, per_device(): squares = squares + lax.ppermute(squares, axis, pairs)  10.5 us
    all_to_all x1, starting transfers between devices, per_device(): lax.all_to_all(expert_out, 'expert', split_axis=1, concat_axis=1, tiled=T...  7.17 us
    ppermute x1, waiting for transfers between devices, per_device(): lax.ppermute(give, 'ry', [(i, i ^ 2) for i in range(chips)])  5.76 us
  transfers between devices with their start and end apart: 11, of which 9 were waited for; matrix products, arithmetic and copies ran while one was open for 6% of the time, Pallas kernels for 0%

profile of v6, /device:TPU:6, one launch (start us, length us, event | category | flops | bytes accessed | tf_op | source)
XLA Modules:
  0.0 199.8 jit_solution(13911214112010775370)
XLA Ops:
  1.2 1.9 collective-permute-start
  7.0 3.5 %collective-permute-start.1 = (f32[128]{0:T(128)S(1)}, f32[128]{0:T(128)S(1)}, u32[]{:S(2)}, u32[]{:S(2)}) collective-permute-start(f32[128]{0:T(128)S(1)} %add.119), channel_id=1, source_target_pairs={{0,128},{128,0},{256,384},{384,256},{1,129},{129,1},{257,385},{385... | collective-permute-start | bytes 1544 | tf_op jit(solution)/shard_map/ppermute | solution.py:40
  10.7 1.8 collective-permute-done.1
  12.5 5.1 %collective-permute-start.2 = (f32[128]{0:T(128)S(1)}, f32[128]{0:T(128)S(1)}, u32[]{:S(2)}, u32[]{:S(2)}) collective-permute-start(f32[128]{0:T(128)S(1)} %add.120), channel_id=1, source_target_pairs={{0,256},{128,384},{256,0},{384,128},{1,257},{129,385},{257,1},{385... | collective-permute-start | bytes 1544 | tf_op jit(solution)/shard_map/ppermute | solution.py:40
  20.9 18.8 %all-to-all-start = ((bf16[2,64,4,512]{3,2,0,1:T(4,128)(2,1)}), bf16[2,64,4,512]{3,2,0,1:T(4,128)(2,1)S(1)}, u32[]{:S(2)}, u32[]{:S(2)}) async-start(bf16[2,64,4,512]{3,2,0,1:T(4,128)(2,1)} %copy.84), calls=%async_computation | async-start | bytes 1048576 | tf_op jit(solution)/shard_map/all_to_all | solution.py:50
  39.7 29.6 %all-to-all-done = bf16[2,64,4,512]{3,2,0,1:T(4,128)(2,1)S(1)} async-done(((bf16[2,64,4,512]{3,2,0,1:T(4,128)(2,1)}), bf16[2,64,4,512]{3,2,0,1:T(4,128)(2,1)S(1)}, u32[]{:S(2)}, u32[]{:S(2)}) %all-to-all-start) | async-done | bytes 524320 | tf_op jit(solution)/shard_map/all_to_all | solution.py:50
  72.2 1.9 collective-permute-start.3
  74.2 2.9 %collective-permute-done.3 = f32[4,512,128]{2,1,0:T(8,128)} collective-permute-done((f32[4,512,128]{2,1,0:T(8,128)}, f32[4,512,128]{2,1,0:T(8,128)}, u32[]{:S(2)}, u32[]{:S(2)}) %collective-permute-start.3) | collective-permute-done | bytes 1048608 | tf_op jit(solution)/shard_map/ppermute | solution.py:64
  77.1 1.3 fusion.2
  79.5 3.5 %collective-permute-start.4 = (f32[2,512,128]{2,1,0:T(8,128)S(1)}, f32[2,512,128]{2,1,0:T(8,128)S(1)}, u32[]{:S(2)}, u32[]{:S(2)}) collective-permute-start(f32[2,512,128]{2,1,0:T(8,128)S(1)} %dynamic-slice_bitcast_fusion.2), channel_id=1, source_target_pairs={{0,128},{128,0},{256,384},{384,256},{1,129},{129,1},{257,385},{385... | collective-permute-start | bytes 1572872 | tf_op jit(solution)/shard_map/ppermute | solution.py:69
  83.0 12.3 %collective-permute-done.4 = f32[2,512,128]{2,1,0:T(8,128)S(1)} collective-permute-done((f32[2,512,128]{2,1,0:T(8,128)S(1)}, f32[2,512,128]{2,1,0:T(8,128)S(1)}, u32[]{:S(2)}, u32[]{:S(2)}) %collective-permute-start.4) | collective-permute-done | bytes 524320 | tf_op jit(solution)/shard_map/ppermute | solution.py:69
  96.5 5.1 %collective-permute-start.5 = (f32[512,128]{1,0:T(8,128)S(1)}, f32[512,128]{1,0:T(8,128)S(1)}, u32[]{:S(2)}, u32[]{:S(2)}) collective-permute-start(f32[512,128]{1,0:T(8,128)S(1)} %dynamic-slice_bitcast_fusion.3), channel_id=1, source_target_pairs={{0,256},{128,384},{256,0},{384,128},{1,257},{129,385},{257,1},{385... | collective-permute-start | bytes 786440 | tf_op jit(solution)/shard_map/ppermute | solution.py:72
  101.6 5.8 %collective-permute-done.5 = f32[512,128]{1,0:T(8,128)S(1)} collective-permute-done((f32[512,128]{1,0:T(8,128)S(1)}, f32[512,128]{1,0:T(8,128)S(1)}, u32[]{:S(2)}, u32[]{:S(2)}) %collective-permute-start.5) | collective-permute-done | bytes 262176 | tf_op jit(solution)/shard_map/ppermute | solution.py:72
  107.5 5.1 %collective-permute-start.6 = (bf16[512,128]{1,0:T(8,128)(2,1)S(1)}, bf16[512,128]{1,0:T(8,128)(2,1)S(1)}, u32[]{:S(2)}, u32[]{:S(2)}) collective-permute-start(bf16[512,128]{1,0:T(8,128)(2,1)S(1)} %multiply_convert_fusion), channel_id=1, source_target_pairs={{0,256},{128,384},{256,0},{384,128},{1,257},{129,385},{257,1},{385... | collective-permute-start | bytes 393224 | tf_op jit(solution)/shard_map/ppermute | solution.py:75
  112.6 3.3 %collective-permute-done.6 = bf16[512,128]{1,0:T(8,128)(2,1)S(1)} collective-permute-done((bf16[512,128]{1,0:T(8,128)(2,1)S(1)}, bf16[512,128]{1,0:T(8,128)(2,1)S(1)}, u32[]{:S(2)}, u32[]{:S(2)}) %collective-permute-start.6) | collective-permute-done | bytes 131104 | tf_op jit(solution)/shard_map/ppermute | solution.py:75
  115.9 3.5 %collective-permute-start.7 = (bf16[2,512,128]{2,1,0:T(8,128)(2,1)S(1)}, bf16[2,512,128]{2,1,0:T(8,128)(2,1)S(1)}, u32[]{:S(2)}, u32[]{:S(2)}) collective-permute-start(bf16[2,512,128]{2,1,0:T(8,128)(2,1)S(1)} %pad_maximum_fusion.1), channel_id=1, source_target_pairs={{0,128},{128,0},{256,384},{384,256},{1,129},{129,1},{257,385},{385... | collective-permute-start | bytes 786440 | tf_op jit(solution)/shard_map/ppermute | solution.py:78
  119.3 4.8 %collective-permute-done.7 = bf16[2,512,128]{2,1,0:T(8,128)(2,1)S(1)} collective-permute-done((bf16[2,512,128]{2,1,0:T(8,128)(2,1)S(1)}, bf16[2,512,128]{2,1,0:T(8,128)(2,1)S(1)}, u32[]{:S(2)}, u32[]{:S(2)}) %collective-permute-start.7) | collective-permute-done | bytes 262176 | tf_op jit(solution)/shard_map/ppermute | solution.py:78
  125.0 1.9 collective-permute-start.8
  128.2 2.8 %gather_fusion.2 = bf16[4,2,128,512]{3,2,1,0:T(8,128)(2,1)} fusion(bf16[2,4,128,512]{3,2,1,0:T(8,128)(2,1)} %get-tuple-element.9, s32[1024]{0:T(1024)S(1)} %pad_clamp_fusion.1), kind=kCustom, calls=%fused_computation.1.clone | custom fusion | bytes 2097168 | tf_op jit(solution)/shard_map/jit(_take)/gather | solution.py:86
  131.0 1.6 gather_fusion.1
  132.7 2.0 convolution_bitcast_fusion
  136.4 7.2 %all-to-all-start.1 = ((bf16[2,64,4,512]{3,2,0,1:T(4,128)(2,1)}), bf16[2,64,4,512]{3,2,0,1:T(4,128)(2,1)S(1)}, u32[]{:S(2)}, u32[]{:S(2)}) async-start(bf16[2,64,4,512]{3,2,0,1:T(4,128)(2,1)} %copy.92), calls=%async_computation.1 | async-start | bytes 1048576 | tf_op jit(solution)/shard_map/all_to_all | solution.py:97
  146.1 30.0 %all-to-all-done.1 = bf16[2,64,4,512]{3,2,0,1:T(4,128)(2,1)S(1)} async-done(((bf16[2,64,4,512]{3,2,0,1:T(4,128)(2,1)}), bf16[2,64,4,512]{3,2,0,1:T(4,128)(2,1)S(1)}, u32[]{:S(2)}, u32[]{:S(2)}) %all-to-all-start.1) | async-done | bytes 524320 | tf_op jit(solution)/shard_map/all_to_all | solution.py:97
  177.6 21.5 %all_to_all.15 = f32[64,1,512]{2,1,0:T(1,128)S(1)} all-to-all(f32[64,1,512]{2,1,0:T(1,128)S(1)} %copy.94), channel_id=1, replica_groups=mesh['ry'=4,'rc'=2,'expert'=64] {'expert'}, dimensions={0} | all-to-all | bytes 262144 | tf_op jit(solution)/shard_map/all_to_all | solution.py:124
  (94 shorter events, 22.0 us)
Async XLA Ops:
  0.0 69.6 %copy-start = (bf16[2,512,1024]{2,1,0:T(8,128)(2,1)S(1)}, bf16[2,512,1024]{2,1,0:T(8,128)(2,1)}, u32[]{:S(2)}) copy-start(bf16[2,512,1024]{2,1,0:T(8,128)(2,1)} %param.17) | copy-start | bytes 6291460
  1.2 5.8 %collective-permute-start = (f32[128]{0:T(128)S(1)}, f32[128]{0:T(128)S(1)}, u32[]{:S(2)}, u32[]{:S(2)}) collective-permute-start(f32[128]{0:T(128)S(1)} %fusion.16), channel_id=1, source_target_pairs={{0,64},{64,0},{1,65},{65,1},{2,66},{66,2},{3,67},{67,3},{4,68},{68... | collective-permute-start | bytes 1544 | tf_op jit(solution)/shard_map/ppermute | solution.py:40
  4.0 15.5 %copy-start.3 = (bf16[128,512]{1,0:T(8,128)(2,1)S(1)}, bf16[128,512]{1,0:T(8,128)(2,1)}, u32[]{:S(2)}) copy-start(bf16[128,512]{1,0:T(8,128)(2,1)} %param.11) | copy-start | bytes 393220
  4.0 15.5 %copy-start.11 = (f32[512]{0:T(512)S(1)}, f32[512]{0:T(512)}, u32[]{:S(2)}) copy-start(f32[512]{0:T(512)} %param.12) | copy-start | bytes 6148
  7.0 5.5 %collective-permute-start.1 = (f32[128]{0:T(128)S(1)}, f32[128]{0:T(128)S(1)}, u32[]{:S(2)}, u32[]{:S(2)}) collective-permute-start(f32[128]{0:T(128)S(1)} %add.119), channel_id=1, source_target_pairs={{0,128},{128,0},{256,384},{384,256},{1,129},{129,1},{257,385},{385... | collective-permute-start | bytes 1544 | tf_op jit(solution)/shard_map/ppermute | solution.py:40
  10.6 8.8 %copy-start.5 = (s32[128,8]{1,0:T(8,128)}, s32[128,8]{1,0:T(8,128)S(1)}, u32[]{:S(2)}) copy-start(s32[128,8]{1,0:T(8,128)S(1)} %fusion.30) | copy-start | bytes 12292
  12.5 7.0 %collective-permute-start.2 = (f32[128]{0:T(128)S(1)}, f32[128]{0:T(128)S(1)}, u32[]{:S(2)}, u32[]{:S(2)}) collective-permute-start(f32[128]{0:T(128)S(1)} %add.120), channel_id=1, source_target_pairs={{0,256},{128,384},{256,0},{384,128},{1,257},{129,385},{257,1},{385... | collective-permute-start | bytes 1544 | tf_op jit(solution)/shard_map/ppermute | solution.py:40
  20.9 48.4 %all-to-all-start = ((bf16[2,64,4,512]{3,2,0,1:T(4,128)(2,1)}), bf16[2,64,4,512]{3,2,0,1:T(4,128)(2,1)S(1)}, u32[]{:S(2)}, u32[]{:S(2)}) async-start(bf16[2,64,4,512]{3,2,0,1:T(4,128)(2,1)} %copy.84), calls=%async_computation | async-start | bytes 1048576 | tf_op jit(solution)/shard_map/all_to_all | solution.py:50
  72.2 4.9 %collective-permute-start.3 = (f32[4,512,128]{2,1,0:T(8,128)}, f32[4,512,128]{2,1,0:T(8,128)}, u32[]{:S(2)}, u32[]{:S(2)}) collective-permute-start(f32[4,512,128]{2,1,0:T(8,128)} %bitcast.72), channel_id=1, source_target_pairs={{0,64},{64,0},{1,65},{65,1},{2,66},{66,2},{3,67},{67,3},{4,68},{68... | collective-permute-start | bytes 3145736 | tf_op jit(solution)/shard_map/ppermute | solution.py:64
  79.5 15.9 %collective-permute-start.4 = (f32[2,512,128]{2,1,0:T(8,128)S(1)}, f32[2,512,128]{2,1,0:T(8,128)S(1)}, u32[]{:S(2)}, u32[]{:S(2)}) collective-permute-start(f32[2,512,128]{2,1,0:T(8,128)S(1)} %dynamic-slice_bitcast_fusion.2), channel_id=1, source_target_pairs={{0,128},{128,0},{256,384},{384,256},{1,129},{129,1},{257,385},{385... | collective-permute-start | bytes 1572872 | tf_op jit(solution)/shard_map/ppermute | solution.py:69
  83.0 43.9 %copy-start.13 = (s32[4]{0:T(128)S(1)}, s32[4]{0:T(128)}, u32[]{:S(2)}) copy-start(s32[4]{0:T(128)} %constant.130.clone) | copy-start | bytes 52
  96.5 10.9 %collective-permute-start.5 = (f32[512,128]{1,0:T(8,128)S(1)}, f32[512,128]{1,0:T(8,128)S(1)}, u32[]{:S(2)}, u32[]{:S(2)}) collective-permute-start(f32[512,128]{1,0:T(8,128)S(1)} %dynamic-slice_bitcast_fusion.3), channel_id=1, source_target_pairs={{0,256},{128,384},{256,0},{384,128},{1,257},{129,385},{257,1},{385... | collective-permute-start | bytes 786440 | tf_op jit(solution)/shard_map/ppermute | solution.py:72
  101.6 25.4 %copy-start.2 = (bf16[2,1024,512]{2,1,0:T(8,128)(2,1)S(1)}, bf16[2,1024,512]{2,1,0:T(8,128)(2,1)}, u32[]{:S(2)}) copy-start(bf16[2,1024,512]{2,1,0:T(8,128)(2,1)} %param.18) | copy-start | bytes 6291460
  107.5 8.4 %collective-permute-start.6 = (bf16[512,128]{1,0:T(8,128)(2,1)S(1)}, bf16[512,128]{1,0:T(8,128)(2,1)S(1)}, u32[]{:S(2)}, u32[]{:S(2)}) collective-permute-start(bf16[512,128]{1,0:T(8,128)(2,1)S(1)} %multiply_convert_fusion), channel_id=1, source_target_pairs={{0,256},{128,384},{256,0},{384,128},{1,257},{129,385},{257,1},{385... | collective-permute-start | bytes 393224 | tf_op jit(solution)/shard_map/ppermute | solution.py:75
  115.9 8.3 %collective-permute-start.7 = (bf16[2,512,128]{2,1,0:T(8,128)(2,1)S(1)}, bf16[2,512,128]{2,1,0:T(8,128)(2,1)S(1)}, u32[]{:S(2)}, u32[]{:S(2)}) collective-permute-start(bf16[2,512,128]{2,1,0:T(8,128)(2,1)S(1)} %pad_maximum_fusion.1), channel_id=1, source_target_pairs={{0,128},{128,0},{256,384},{384,256},{1,129},{129,1},{257,385},{385... | collective-permute-start | bytes 786440 | tf_op jit(solution)/shard_map/ppermute | solution.py:78
  124.1 2.9 %copy-start.7 = (bf16[2,512,128]{2,1,0:T(8,128)(2,1)}, bf16[2,512,128]{2,1,0:T(8,128)(2,1)S(1)}, u32[]{:S(2)}) copy-start(bf16[2,512,128]{2,1,0:T(8,128)(2,1)S(1)} %collective-permute-done.7) | copy-start | bytes 786436
  125.0 7.7 %collective-permute-start.8 = (bf16[4,512,128]{2,1,0:T(8,128)(2,1)}, bf16[4,512,128]{2,1,0:T(8,128)(2,1)}, u32[]{:S(2)}, u32[]{:S(2)}) collective-permute-start(bf16[4,512,128]{2,1,0:T(8,128)(2,1)} %pad_maximum_fusion), channel_id=1, source_target_pairs={{0,64},{64,0},{1,65},{65,1},{2,66},{66,2},{3,67},{67,3},{4,68},{68... | collective-permute-start | bytes 1572872 | tf_op jit(solution)/shard_map/ppermute | solution.py:81
  132.7 2.0 %copy-start.4 = (bf16[4,2,128,512]{3,2,1,0:T(8,128)(2,1)S(1)}, bf16[4,2,128,512]{3,2,1,0:T(8,128)(2,1)}, u32[]{:S(2)}) copy-start(bf16[4,2,128,512]{3,2,1,0:T(8,128)(2,1)} %gather_fusion.1) | copy-start | bytes 3145732
  132.7 2.0 %copy-start.8 = (bf16[2,512,128]{2,1,0:T(8,128)(2,1)S(1)}, bf16[2,512,128]{2,1,0:T(8,128)(2,1)}, u32[]{:S(2)}) copy-start(bf16[2,512,128]{2,1,0:T(8,128)(2,1)} %copy-done.7) | copy-start | bytes 786436
  135.2 8.3 %copy-start.10 = (f32[128,8]{0,1:T(8,128)S(1)}, f32[128,8]{0,1:T(8,128)}, u32[]{:S(2)}) copy-start(f32[128,8]{0,1:T(8,128)} %param.13) | copy-start | bytes 12292
  135.3 8.4 %copy-start.9 = (s32[128]{0:T(128)S(1)}, s32[128]{0:T(128)}, u32[]{:S(2)}) copy-start(s32[128]{0:T(128)} %param.16) | copy-start | bytes 1540
  135.3 8.9 %copy-start.12 = (s32[128]{0:T(128)S(1)}, s32[128]{0:T(128)}, u32[]{:S(2)}) copy-start(s32[128]{0:T(128)} %param.14) | copy-start | bytes 1540
  135.3 10.1 %copy-start.6 = (s32[128,8]{1,0:T(8,128)S(1)}, s32[128,8]{1,0:T(8,128)}, u32[]{:S(2)}) copy-start(s32[128,8]{1,0:T(8,128)} %copy-done.5) | copy-start | bytes 12292
  136.4 39.7 %all-to-all-start.1 = ((bf16[2,64,4,512]{3,2,0,1:T(4,128)(2,1)}), bf16[2,64,4,512]{3,2,0,1:T(4,128)(2,1)S(1)}, u32[]{:S(2)}, u32[]{:S(2)}) async-start(bf16[2,64,4,512]{3,2,0,1:T(4,128)(2,1)} %copy.92), calls=%async_computation.1 | async-start | bytes 1048576 | tf_op jit(solution)/shard_map/all_to_all | solution.py:97
  (1 other events, 1.0 us)

commit v7 on v5

--- a/solution.py
+++ b/solution.py
@@ -32,7 +32,9 @@
     local_id = route_flat % local_experts
     slot_index = (local_id * owner_count + owner_id) * capacity + position
     slot_index = jnp.where(pair_live > 0, slot_index, slot_total)
-    squares = lax.psum(jnp.sum(widened * widened, axis=1), ("ry", "rc"))
+    squares = jnp.sum(widened * widened, axis=1)
+    squares = squares + lax.ppermute(squares, "rc", [(0, 1), (1, 0)])
+    squares = lax.psum(squares, "ry")
     rinv_rows = lax.rsqrt(squares / (feat_width * rep_count) + 1e-06)
     normed = (widened * rinv_rows[:, None] * norm_gain[None, :]).astype(jnp.bfloat16)
     slot_ids = jnp.arange(slot_total, dtype=jnp.int32)

time: 175 us -> 175 us (level)
  blocking collectives: 66.3 us -> 62.2 us
  starting transfers between devices: 29.8 us -> 31.9 us
    psum x1, blocking collectives: 14.9 us -> 10.7 us  [per_device(): squares = lax.psum(squares, 'ry')]
    ppermute x0 -> x1, starting transfers between devices: none -> 1.92 us  [per_device(): squares = squares + lax.ppermute(squares, 'rc', [(0, 1), (1, 0)])]
  transfers between devices with their start and end apart: 4 -> 5, of which waited for: 4 -> 4; matrix products, arithmetic and copies ran while one was open for 2% -> 4% of each run, Pallas kernels for 0% -> 0%
where the time goes in v7:
time: 175 us; the launch traced here: 174 us
  waiting for transfers between devices  63.4 us (36%)
  blocking collectives  62.2 us (36%)
  starting transfers between devices  31.9 us (18%)
  local copies, waits for them, and re-layouts  8.23 us (5%)
  other arithmetic  5.81 us (3%)
  matrix products  2.31 us (1%)
    all_to_all x1, waiting for transfers between devices, per_device(): lax.all_to_all(outbound, 'expert', split_axis=1, concat_axis=1, tiled=True)  29.8 us
    all_to_all x1, waiting for transfers between devices, per_device(): lax.all_to_all(expert_out, 'expert', split_axis=1, concat_axis=1, tiled=T...  29.7 us
    all_to_all x1, blocking collectives, per_device(): lax.all_to_all(leaving, 'expert', split_axis=0, concat_axis=0, tiled=True)  21.6 us
    all_to_all x1, starting transfers between devices, per_device(): lax.all_to_all(outbound, 'expert', split_axis=1, concat_axis=1, tiled=True)  18.8 us
    all_to_all x1, blocking collectives, per_device(): lax.all_to_all(half_sum, 'ry', split_axis=0, concat_axis=0, tiled=True)  18.1 us
    all_to_all x1, blocking collectives, per_device(): lax.all_to_all(act_tile, 'ry', split_axis=0, concat_axis=0, tiled=True)  11.7 us
    psum x1, blocking collectives, per_device(): squares = lax.psum(squares, 'ry')  10.7 us
    all_to_all x1, starting transfers between devices, per_device(): lax.all_to_all(expert_out, 'expert', split_axis=1, concat_axis=1, tiled=T...  7.34 us
  transfers between devices with their start and end apart: 5, of which 4 were waited for; matrix products, arithmetic and copies ran while one was open for 4% of the time, Pallas kernels for 0%

profile of v7, /device:TPU:6, one launch (start us, length us, event | category | flops | bytes accessed | tf_op | source)
XLA Modules:
  0.0 174.2 jit_solution(2567592640269344490)
XLA Ops:
  0.0 1.2 fusion.6
  1.2 1.9 %collective-permute-start = (f32[128]{0:T(128)S(1)}, f32[128]{0:T(128)S(1)}, u32[]{:S(2)}, u32[]{:S(2)}) collective-permute-start(f32[128]{0:T(128)S(1)} %fusion.6), channel_id=1, source_target_pairs={{0,64},{64,0},{1,65},{65,1},{2,66},{66,2},{3,67},{67,3},{4,68},{68... | collective-permute-start | bytes 1544 | tf_op jit(solution)/shard_map/ppermute | solution.py:36
  3.1 0.8 copy.66
  4.1 0.7 broadcast_subtract_fusion
  4.8 0.7 broadcast_compare_fusion
  7.1 0.9 convert_reduce_fusion
  8.1 10.7 %psum.7 = f32[128]{0:T(128)S(1)} all-reduce(f32[128]{0:T(128)S(1)} %add.89), channel_id=1, replica_groups=mesh['ry'=4,'rc'=2,'expert'=64] {'ry'}, use_global_device_ids=true, to_apply=%region_6.7 | all-reduce | flops 128 | bytes 1024 | tf_op jit(solution)/shard_map/psum | solution.py:37
  19.4 1.0 copy.77
  20.3 18.8 %all-to-all-start = ((bf16[2,64,4,512]{3,2,0,1:T(4,128)(2,1)}), bf16[2,64,4,512]{3,2,0,1:T(4,128)(2,1)S(1)}, u32[]{:S(2)}, u32[]{:S(2)}) async-start(bf16[2,64,4,512]{3,2,0,1:T(4,128)(2,1)} %copy.77), calls=%async_computation | async-start | bytes 1048576 | tf_op jit(solution)/shard_map/all_to_all | solution.py:47
  39.1 29.8 %all-to-all-done = bf16[2,64,4,512]{3,2,0,1:T(4,128)(2,1)S(1)} async-done(((bf16[2,64,4,512]{3,2,0,1:T(4,128)(2,1)}), bf16[2,64,4,512]{3,2,0,1:T(4,128)(2,1)S(1)}, u32[]{:S(2)}, u32[]{:S(2)}) %all-to-all-start) | async-done | bytes 524320 | tf_op jit(solution)/shard_map/all_to_all | solution.py:47
  69.3 0.7 fusion.30
  70.9 1.9 %collective-permute-start.1 = (f32[4,512,128]{2,1,0:T(8,128)S(1)}, f32[4,512,128]{2,1,0:T(8,128)S(1)}, u32[]{:S(2)}, u32[]{:S(2)}) collective-permute-start(f32[4,512,128]{2,1,0:T(8,128)S(1)} %bitcast.54), channel_id=1, source_target_pairs={{0,64},{64,0},{1,65},{65,1},{2,66},{66,2},{3,67},{67,3},{4,68},{68... | collective-permute-start | bytes 3145736 | tf_op jit(solution)/shard_map/ppermute | solution.py:62
  72.9 2.6 %collective-permute-done.1 = f32[4,512,128]{2,1,0:T(8,128)S(1)} collective-permute-done((f32[4,512,128]{2,1,0:T(8,128)S(1)}, f32[4,512,128]{2,1,0:T(8,128)S(1)}, u32[]{:S(2)}, u32[]{:S(2)}) %collective-permute-start.1) | collective-permute-done | bytes 1048608 | tf_op jit(solution)/shard_map/ppermute | solution.py:62
  75.6 18.1 %all_to_all.25 = f32[4,512,128]{2,1,0:T(8,128)S(1)} all-to-all(f32[4,512,128]{2,1,0:T(8,128)S(1)} %fusion.2), channel_id=1, replica_groups=mesh['ry'=4,'rc'=2,'expert'=64] {'ry'}, dimensions={0} | all-to-all | bytes 2097152 | tf_op jit(solution)/shard_map/all_to_all | solution.py:63
  94.0 11.7 %all_to_all.26 = bf16[4,512,128]{2,1,0:T(8,128)(2,1)S(1)} all-to-all(bf16[4,512,128]{2,1,0:T(8,128)(2,1)S(1)} %broadcast_in_dim.61), channel_id=1, replica_groups=mesh['ry'=4,'rc'=2,'expert'=64] {'ry'}, dimensions={0} | all-to-all | bytes 1048576 | tf_op jit(solution)/shard_map/all_to_all | solution.py:67
  105.7 1.9 %collective-permute-start.2 = (bf16[4,512,128]{2,1,0:T(8,128)(2,1)S(1)}, bf16[4,512,128]{2,1,0:T(8,128)(2,1)S(1)}, u32[]{:S(2)}, u32[]{:S(2)}) collective-permute-start(bf16[4,512,128]{2,1,0:T(8,128)(2,1)S(1)} %all_to_all.26), channel_id=1, source_target_pairs={{0,64},{64,0},{1,65},{65,1},{2,66},{66,2},{3,67},{67,3},{4,68},{68... | collective-permute-start | bytes 1572872 | tf_op jit(solution)/shard_map/ppermute | solution.py:68
  108.2 1.2 collective-permute-done.2
  110.1 1.0 copy.83
  111.1 7.3 %all-to-all-start.3 = ((bf16[2,64,4,512]{3,2,0,1:T(4,128)(2,1)}), bf16[2,64,4,512]{3,2,0,1:T(4,128)(2,1)S(1)}, u32[]{:S(2)}, u32[]{:S(2)}) async-start(bf16[2,64,4,512]{3,2,0,1:T(4,128)(2,1)} %copy.83), calls=%async_computation.3 | async-start | bytes 1048576 | tf_op jit(solution)/shard_map/all_to_all | solution.py:80
  119.0 1.0 scatter_custom_fusion
  120.0 0.7 select_reduce_fusion
  120.7 29.7 %all-to-all-done.3 = bf16[2,64,4,512]{3,2,0,1:T(4,128)(2,1)S(1)} async-done(((bf16[2,64,4,512]{3,2,0,1:T(4,128)(2,1)}), bf16[2,64,4,512]{3,2,0,1:T(4,128)(2,1)S(1)}, u32[]{:S(2)}, u32[]{:S(2)}) %all-to-all-start.3) | async-done | bytes 524320 | tf_op jit(solution)/shard_map/all_to_all | solution.py:80
  151.9 21.6 %all_to_all.27 = f32[64,1,512]{2,1,0:T(1,128)S(1)} all-to-all(f32[64,1,512]{2,1,0:T(1,128)S(1)} %copy.85), channel_id=1, replica_groups=mesh['ry'=4,'rc'=2,'expert'=64] {'expert'}, dimensions={0} | all-to-all | bytes 262144 | tf_op jit(solution)/shard_map/all_to_all | solution.py:107
  173.5 0.7 copy.102
  (67 shorter events, 7.2 us)
Async XLA Ops:
  0.0 69.3 %copy-start = (bf16[2,512,1024]{2,1,0:T(8,128)(2,1)S(1)}, bf16[2,512,1024]{2,1,0:T(8,128)(2,1)}, u32[]{:S(2)}) copy-start(bf16[2,512,1024]{2,1,0:T(8,128)(2,1)} %param.14) | copy-start | bytes 6291460
  1.2 6.9 %collective-permute-start = (f32[128]{0:T(128)S(1)}, f32[128]{0:T(128)S(1)}, u32[]{:S(2)}, u32[]{:S(2)}) collective-permute-start(f32[128]{0:T(128)S(1)} %fusion.6), channel_id=1, source_target_pairs={{0,64},{64,0},{1,65},{65,1},{2,66},{66,2},{3,67},{67,3},{4,68},{68... | collective-permute-start | bytes 1544 | tf_op jit(solution)/shard_map/ppermute | solution.py:36
  4.0 14.9 %copy-start.2 = (bf16[128,512]{1,0:T(8,128)(2,1)S(1)}, bf16[128,512]{1,0:T(8,128)(2,1)}, u32[]{:S(2)}) copy-start(bf16[128,512]{1,0:T(8,128)(2,1)} %param.8) | copy-start | bytes 393220
  4.0 14.9 %copy-start.7 = (f32[512]{0:T(512)S(1)}, f32[512]{0:T(512)}, u32[]{:S(2)}) copy-start(f32[512]{0:T(512)} %param.9) | copy-start | bytes 6148
  7.1 11.8 %copy-start.3 = (s32[128,8]{1,0:T(8,128)}, s32[128,8]{1,0:T(8,128)S(1)}, u32[]{:S(2)}) copy-start(s32[128,8]{1,0:T(8,128)S(1)} %fusion.20) | copy-start | bytes 12292
  20.3 48.6 %all-to-all-start = ((bf16[2,64,4,512]{3,2,0,1:T(4,128)(2,1)}), bf16[2,64,4,512]{3,2,0,1:T(4,128)(2,1)S(1)}, u32[]{:S(2)}, u32[]{:S(2)}) async-start(bf16[2,64,4,512]{3,2,0,1:T(4,128)(2,1)} %copy.77), calls=%async_computation | async-start | bytes 1048576 | tf_op jit(solution)/shard_map/all_to_all | solution.py:47
  70.9 4.6 %collective-permute-start.1 = (f32[4,512,128]{2,1,0:T(8,128)S(1)}, f32[4,512,128]{2,1,0:T(8,128)S(1)}, u32[]{:S(2)}, u32[]{:S(2)}) collective-permute-start(f32[4,512,128]{2,1,0:T(8,128)S(1)} %bitcast.54), channel_id=1, source_target_pairs={{0,64},{64,0},{1,65},{65,1},{2,66},{66,2},{3,67},{67,3},{4,68},{68... | collective-permute-start | bytes 3145736 | tf_op jit(solution)/shard_map/ppermute | solution.py:62
  93.8 13.8 %copy-start.1 = (bf16[2,1024,512]{2,1,0:T(8,128)(2,1)S(1)}, bf16[2,1024,512]{2,1,0:T(8,128)(2,1)}, u32[]{:S(2)}) copy-start(bf16[2,1024,512]{2,1,0:T(8,128)(2,1)} %param.15) | copy-start | bytes 6291460
  105.7 3.8 %collective-permute-start.2 = (bf16[4,512,128]{2,1,0:T(8,128)(2,1)S(1)}, bf16[4,512,128]{2,1,0:T(8,128)(2,1)S(1)}, u32[]{:S(2)}, u32[]{:S(2)}) collective-permute-start(bf16[4,512,128]{2,1,0:T(8,128)(2,1)S(1)} %all_to_all.26), channel_id=1, source_target_pairs={{0,64},{64,0},{1,65},{65,1},{2,66},{66,2},{3,67},{67,3},{4,68},{68... | collective-permute-start | bytes 1572872 | tf_op jit(solution)/shard_map/ppermute | solution.py:68
  109.9 8.5 %copy-start.6 = (f32[128,8]{0,1:T(8,128)S(1)}, f32[128,8]{0,1:T(8,128)}, u32[]{:S(2)}) copy-start(f32[128,8]{0,1:T(8,128)} %param.10) | copy-start | bytes 12292
  109.9 8.6 %copy-start.5 = (s32[128]{0:T(128)S(1)}, s32[128]{0:T(128)}, u32[]{:S(2)}) copy-start(s32[128]{0:T(128)} %param.13) | copy-start | bytes 1540
  109.9 9.0 %copy-start.8 = (s32[128]{0:T(128)S(1)}, s32[128]{0:T(128)}, u32[]{:S(2)}) copy-start(s32[128]{0:T(128)} %param.11) | copy-start | bytes 1540
  110.1 9.9 %copy-start.4 = (s32[128,8]{1,0:T(8,128)S(1)}, s32[128,8]{1,0:T(8,128)}, u32[]{:S(2)}) copy-start(s32[128,8]{1,0:T(8,128)} %copy-done.3) | copy-start | bytes 12292
  111.1 39.3 %all-to-all-start.3 = ((bf16[2,64,4,512]{3,2,0,1:T(4,128)(2,1)}), bf16[2,64,4,512]{3,2,0,1:T(4,128)(2,1)S(1)}, u32[]{:S(2)}, u32[]{:S(2)}) async-start(bf16[2,64,4,512]{3,2,0,1:T(4,128)(2,1)} %copy.83), calls=%async_computation.3 | async-start | bytes 1048576 | tf_op jit(solution)/shard_map/all_to_all | solution.py:80

commit v8 on v7

--- a/solution.py
+++ b/solution.py
@@ -30,7 +30,7 @@
     position = jnp.sum(earlier * one_hot, axis=1)
     owner_id = route_flat // local_experts
     local_id = route_flat % local_experts
-    slot_index = (local_id * owner_count + owner_id) * capacity + position
+    slot_index = (owner_id * local_experts + local_id) * capacity + position
     slot_index = jnp.where(pair_live > 0, slot_index, slot_total)
     squares = jnp.sum(widened * widened, axis=1)
     squares = squares + lax.ppermute(squares, "rc", [(0, 1), (1, 0)])
@@ -43,11 +43,13 @@
         (slot_of[None, :, :] == slot_ids[:, None, None]).astype(jnp.float32), axis=2
     ).astype(jnp.bfloat16)
     outbound = jnp.dot(pick, normed, preferred_element_type=jnp.float32).astype(jnp.bfloat16)
-    outbound = outbound.reshape(local_experts, owner_count, capacity, feat_width)
-    received = lax.all_to_all(outbound, "expert", split_axis=1, concat_axis=1, tiled=True)
-    item_count = received.shape[2]
+    outbound = outbound.reshape(owner_count, local_experts * capacity, feat_width)
+    received = lax.all_to_all(outbound, "expert", split_axis=0, concat_axis=0, tiled=True)
+    item_count = capacity
     rows_here = owner_count * item_count
-    flattened = received.reshape(local_experts, rows_here, feat_width)
+    flattened = jnp.transpose(
+        received.reshape(owner_count, local_experts, capacity, feat_width), (1, 0, 2, 3)
+    ).reshape(local_experts, rows_here, feat_width)
     partial_value = jnp.einsum(
         "erd,edh->erh", flattened, up_weight, preferred_element_type=jnp.float32
     )
@@ -77,7 +79,10 @@
     expert_out = expert_out.astype(jnp.bfloat16).reshape(
         local_experts, owner_count, item_count, feat_width
     )
-    returned = lax.all_to_all(expert_out, "expert", split_axis=1, concat_axis=1, tiled=True)
+    expert_out = jnp.transpose(expert_out, (1, 0, 2, 3)).reshape(
+        owner_count, local_experts * item_count, feat_width
+    )
+    returned = lax.all_to_all(expert_out, "expert", split_axis=0, concat_axis=0, tiled=True)
     flat_back = returned.reshape(slot_total, feat_width)
     combine = jnp.sum(
         jnp.where(

time: 175 us -> 176 us (level)
    reshape x4, local copies, waits for them, and re-layouts: 1.34 us -> 3.34 us  [the longest x1 1.16 us: per_device(): flattened = jnp.transpose(received.reshape(owner_count, local_experts, ca...]
where the time goes in v8:
time: 176 us
  waiting for transfers between devices  63.3 us (36%)
  blocking collectives  62.2 us (35%)
  starting transfers between devices  31.9 us (18%)
  local copies, waits for them, and re-layouts  8.98 us (5%)
  other arithmetic  5.81 us (3%)
  matrix products  3.1 us (2%)
    all_to_all x1, waiting for transfers between devices, per_device(): lax.all_to_all(outbound, 'expert', split_axis=0, concat_axis=0, tiled=True)  29.8 us
    all_to_all x1, waiting for transfers between devices, per_device(): lax.all_to_all(expert_out, 'expert', split_axis=0, concat_axis=0, tiled=T...  29.7 us
    all_to_all x1, blocking collectives, per_device(): lax.all_to_all(leaving, 'expert', split_axis=0, concat_axis=0, tiled=True)  21.6 us
    all_to_all x1, starting transfers between devices, per_device(): lax.all_to_all(outbound, 'expert', split_axis=0, concat_axis=0, tiled=True)  18.8 us
    all_to_all x1, blocking collectives, per_device(): lax.all_to_all(half_sum, 'ry', split_axis=0, concat_axis=0, tiled=True)  18.1 us
    all_to_all x1, blocking collectives, per_device(): lax.all_to_all(act_tile, 'ry', split_axis=0, concat_axis=0, tiled=True)  11.7 us
    psum x1, blocking collectives, per_device(): squares = lax.psum(squares, 'ry')  10.7 us
    all_to_all x1, starting transfers between devices, per_device(): lax.all_to_all(expert_out, 'expert', split_axis=0, concat_axis=0, tiled=T...  7.34 us
  transfers between devices with their start and end apart: 5, of which 4 were waited for; matrix products, arithmetic and copies ran while one was open for 4% of the time, Pallas kernels for 0%

profile of v8, /device:TPU:6, one launch (start us, length us, event | category | flops | bytes accessed | tf_op | source)
XLA Modules:
  0.0 175.7 jit_solution(4400456984633823596)
XLA Ops:
  0.0 1.2 fusion.8
  1.2 1.9 %collective-permute-start = (f32[128]{0:T(128)S(1)}, f32[128]{0:T(128)S(1)}, u32[]{:S(2)}, u32[]{:S(2)}) collective-permute-start(f32[128]{0:T(128)S(1)} %fusion.8), channel_id=1, source_target_pairs={{0,64},{64,0},{1,65},{65,1},{2,66},{66,2},{3,67},{67,3},{4,68},{68... | collective-permute-start | bytes 1544 | tf_op jit(solution)/shard_map/ppermute | solution.py:36
  3.1 0.8 copy.65
  7.1 0.9 convert_reduce_fusion
  8.1 10.7 %psum.7 = f32[128]{0:T(128)S(1)} all-reduce(f32[128]{0:T(128)S(1)} %add.89), channel_id=1, replica_groups=mesh['ry'=4,'rc'=2,'expert'=64] {'ry'}, use_global_device_ids=true, to_apply=%region_6.7 | all-reduce | flops 128 | bytes 1024 | tf_op jit(solution)/shard_map/psum | solution.py:37
  18.8 1.2 fusion.2
  20.0 18.8 %all-to-all-start = ((bf16[64,8,512]{2,1,0:T(8,128)(2,1)}), bf16[64,8,512]{2,1,0:T(8,128)(2,1)S(1)}, u32[]{:S(2)}, u32[]{:S(2)}) async-start(bf16[64,8,512]{2,1,0:T(8,128)(2,1)} %fusion.2), calls=%async_computation | async-start | bytes 1048576 | tf_op jit(solution)/shard_map/all_to_all | solution.py:47
  38.8 29.8 %all-to-all-done = bf16[64,8,512]{2,1,0:T(8,128)(2,1)S(1)} async-done(((bf16[64,8,512]{2,1,0:T(8,128)(2,1)}), bf16[64,8,512]{2,1,0:T(8,128)(2,1)S(1)}, u32[]{:S(2)}, u32[]{:S(2)}) %all-to-all-start) | async-done | bytes 524320 | tf_op jit(solution)/shard_map/all_to_all | solution.py:47
  68.8 1.0 copy.101
  69.7 1.2 reshape.160
  70.9 0.7 fusion.32
  72.6 1.9 %collective-permute-start.1 = (f32[4,512,128]{2,1,0:T(8,128)S(1)}, f32[4,512,128]{2,1,0:T(8,128)S(1)}, u32[]{:S(2)}, u32[]{:S(2)}) collective-permute-start(f32[4,512,128]{2,1,0:T(8,128)S(1)} %bitcast.66), channel_id=1, source_target_pairs={{0,64},{64,0},{1,65},{65,1},{2,66},{66,2},{3,67},{67,3},{4,68},{68... | collective-permute-start | bytes 3145736 | tf_op jit(solution)/shard_map/ppermute | solution.py:64
  74.5 2.6 %collective-permute-done.1 = f32[4,512,128]{2,1,0:T(8,128)S(1)} collective-permute-done((f32[4,512,128]{2,1,0:T(8,128)S(1)}, f32[4,512,128]{2,1,0:T(8,128)S(1)}, u32[]{:S(2)}, u32[]{:S(2)}) %collective-permute-start.1) | collective-permute-done | bytes 1048608 | tf_op jit(solution)/shard_map/ppermute | solution.py:64
  77.2 18.1 %all_to_all.25 = f32[4,512,128]{2,1,0:T(8,128)S(1)} all-to-all(f32[4,512,128]{2,1,0:T(8,128)S(1)} %fusion.3), channel_id=1, replica_groups=mesh['ry'=4,'rc'=2,'expert'=64] {'ry'}, dimensions={0} | all-to-all | bytes 2097152 | tf_op jit(solution)/shard_map/all_to_all | solution.py:65
  95.6 11.7 %all_to_all.26 = bf16[4,512,128]{2,1,0:T(8,128)(2,1)S(1)} all-to-all(bf16[4,512,128]{2,1,0:T(8,128)(2,1)S(1)} %broadcast_in_dim.61), channel_id=1, replica_groups=mesh['ry'=4,'rc'=2,'expert'=64] {'ry'}, dimensions={0} | all-to-all | bytes 1048576 | tf_op jit(solution)/shard_map/all_to_all | solution.py:69
  107.3 1.9 %collective-permute-start.2 = (bf16[4,512,128]{2,1,0:T(8,128)(2,1)S(1)}, bf16[4,512,128]{2,1,0:T(8,128)(2,1)S(1)}, u32[]{:S(2)}, u32[]{:S(2)}) collective-permute-start(bf16[4,512,128]{2,1,0:T(8,128)(2,1)S(1)} %all_to_all.26), channel_id=1, source_target_pairs={{0,64},{64,0},{1,65},{65,1},{2,66},{66,2},{3,67},{67,3},{4,68},{68... | collective-permute-start | bytes 1572872 | tf_op jit(solution)/shard_map/ppermute | solution.py:70
  109.9 1.2 collective-permute-done.2
  111.8 1.1 copy.82
  112.9 7.3 %all-to-all-start.3 = ((bf16[64,8,512]{2,1,0:T(8,128)(2,1)}), bf16[64,8,512]{2,1,0:T(8,128)(2,1)S(1)}, u32[]{:S(2)}, u32[]{:S(2)}) async-start(bf16[64,8,512]{2,1,0:T(8,128)(2,1)} %copy.82), calls=%async_computation.3 | async-start | bytes 1048576 | tf_op jit(solution)/shard_map/all_to_all | solution.py:85
  120.8 1.0 scatter_custom_fusion
  121.9 0.7 select_reduce_fusion
  122.6 29.7 %all-to-all-done.3 = bf16[64,8,512]{2,1,0:T(8,128)(2,1)S(1)} async-done(((bf16[64,8,512]{2,1,0:T(8,128)(2,1)}), bf16[64,8,512]{2,1,0:T(8,128)(2,1)S(1)}, u32[]{:S(2)}, u32[]{:S(2)}) %all-to-all-start.3) | async-done | bytes 524320 | tf_op jit(solution)/shard_map/all_to_all | solution.py:85
  153.4 21.6 %all_to_all.27 = f32[64,1,512]{2,1,0:T(1,128)S(1)} all-to-all(f32[64,1,512]{2,1,0:T(1,128)S(1)} %copy.83), channel_id=1, replica_groups=mesh['ry'=4,'rc'=2,'expert'=64] {'expert'}, dimensions={0} | all-to-all | bytes 262144 | tf_op jit(solution)/shard_map/all_to_all | solution.py:112
  175.1 0.7 copy.102
  (65 shorter events, 7.6 us)
Async XLA Ops:
  0.0 70.9 %copy-start = (bf16[2,512,1024]{2,1,0:T(8,128)(2,1)S(1)}, bf16[2,512,1024]{2,1,0:T(8,128)(2,1)}, u32[]{:S(2)}) copy-start(bf16[2,512,1024]{2,1,0:T(8,128)(2,1)} %param.14) | copy-start | bytes 6291460
  1.2 6.9 %collective-permute-start = (f32[128]{0:T(128)S(1)}, f32[128]{0:T(128)S(1)}, u32[]{:S(2)}, u32[]{:S(2)}) collective-permute-start(f32[128]{0:T(128)S(1)} %fusion.8), channel_id=1, source_target_pairs={{0,64},{64,0},{1,65},{65,1},{2,66},{66,2},{3,67},{67,3},{4,68},{68... | collective-permute-start | bytes 1544 | tf_op jit(solution)/shard_map/ppermute | solution.py:36
  4.0 14.9 %copy-start.2 = (bf16[128,512]{1,0:T(8,128)(2,1)S(1)}, bf16[128,512]{1,0:T(8,128)(2,1)}, u32[]{:S(2)}) copy-start(bf16[128,512]{1,0:T(8,128)(2,1)} %param.8) | copy-start | bytes 393220
  4.0 14.9 %copy-start.7 = (f32[512]{0:T(512)S(1)}, f32[512]{0:T(512)}, u32[]{:S(2)}) copy-start(f32[512]{0:T(512)} %param.9) | copy-start | bytes 6148
  7.1 31.7 %copy-start.3 = (s32[128,8]{1,0:T(8,128)}, s32[128,8]{1,0:T(8,128)S(1)}, u32[]{:S(2)}) copy-start(s32[128,8]{1,0:T(8,128)S(1)} %fusion.22) | copy-start | bytes 12292
  20.0 48.6 %all-to-all-start = ((bf16[64,8,512]{2,1,0:T(8,128)(2,1)}), bf16[64,8,512]{2,1,0:T(8,128)(2,1)S(1)}, u32[]{:S(2)}, u32[]{:S(2)}) async-start(bf16[64,8,512]{2,1,0:T(8,128)(2,1)} %fusion.2), calls=%async_computation | async-start | bytes 1048576 | tf_op jit(solution)/shard_map/all_to_all | solution.py:47
  72.6 4.6 %collective-permute-start.1 = (f32[4,512,128]{2,1,0:T(8,128)S(1)}, f32[4,512,128]{2,1,0:T(8,128)S(1)}, u32[]{:S(2)}, u32[]{:S(2)}) collective-permute-start(f32[4,512,128]{2,1,0:T(8,128)S(1)} %bitcast.66), channel_id=1, source_target_pairs={{0,64},{64,0},{1,65},{65,1},{2,66},{66,2},{3,67},{67,3},{4,68},{68... | collective-permute-start | bytes 3145736 | tf_op jit(solution)/shard_map/ppermute | solution.py:64
  95.4 13.8 %copy-start.1 = (bf16[2,1024,512]{2,1,0:T(8,128)(2,1)S(1)}, bf16[2,1024,512]{2,1,0:T(8,128)(2,1)}, u32[]{:S(2)}) copy-start(bf16[2,1024,512]{2,1,0:T(8,128)(2,1)} %param.15) | copy-start | bytes 6291460
  107.3 3.8 %collective-permute-start.2 = (bf16[4,512,128]{2,1,0:T(8,128)(2,1)S(1)}, bf16[4,512,128]{2,1,0:T(8,128)(2,1)S(1)}, u32[]{:S(2)}, u32[]{:S(2)}) collective-permute-start(bf16[4,512,128]{2,1,0:T(8,128)(2,1)S(1)} %all_to_all.26), channel_id=1, source_target_pairs={{0,64},{64,0},{1,65},{65,1},{2,66},{66,2},{3,67},{67,3},{4,68},{68... | collective-permute-start | bytes 1572872 | tf_op jit(solution)/shard_map/ppermute | solution.py:70
  111.5 8.7 %copy-start.6 = (f32[128,8]{0,1:T(8,128)S(1)}, f32[128,8]{0,1:T(8,128)}, u32[]{:S(2)}) copy-start(f32[128,8]{0,1:T(8,128)} %param.10) | copy-start | bytes 12292
  111.6 8.8 %copy-start.5 = (s32[128]{0:T(128)S(1)}, s32[128]{0:T(128)}, u32[]{:S(2)}) copy-start(s32[128]{0:T(128)} %param.13) | copy-start | bytes 1540
  111.6 9.3 %copy-start.8 = (s32[128]{0:T(128)S(1)}, s32[128]{0:T(128)}, u32[]{:S(2)}) copy-start(s32[128]{0:T(128)} %param.11) | copy-start | bytes 1540
  111.6 10.3 %copy-start.4 = (s32[128,8]{1,0:T(8,128)S(1)}, s32[128,8]{1,0:T(8,128)}, u32[]{:S(2)}) copy-start(s32[128,8]{1,0:T(8,128)} %copy-done.3) | copy-start | bytes 12292
  112.9 39.3 %all-to-all-start.3 = ((bf16[64,8,512]{2,1,0:T(8,128)(2,1)}), bf16[64,8,512]{2,1,0:T(8,128)(2,1)S(1)}, u32[]{:S(2)}, u32[]{:S(2)}) async-start(bf16[64,8,512]{2,1,0:T(8,128)(2,1)} %copy.82), calls=%async_computation.3 | async-start | bytes 1048576 | tf_op jit(solution)/shard_map/all_to_all | solution.py:85

commit v9 on v7

--- a/solution.py
+++ b/solution.py
@@ -34,7 +34,9 @@
     slot_index = jnp.where(pair_live > 0, slot_index, slot_total)
     squares = jnp.sum(widened * widened, axis=1)
     squares = squares + lax.ppermute(squares, "rc", [(0, 1), (1, 0)])
-    squares = lax.psum(squares, "ry")
+    chip_count = lax.axis_size("ry")
+    spread = jnp.broadcast_to(squares[None], (chip_count,) + squares.shape)
+    squares = jnp.sum(lax.all_to_all(spread, "ry", 0, 0, tiled=True), axis=0)
     rinv_rows = lax.rsqrt(squares / (feat_width * rep_count) + 1e-06)
     normed = (widened * rinv_rows[:, None] * norm_gain[None, :]).astype(jnp.bfloat16)
     slot_ids = jnp.arange(slot_total, dtype=jnp.int32)

time: 175 us -> 174 us (level)
  blocking collectives: 62.2 us -> 51.4 us
  waiting for transfers between devices: 63.4 us -> 68.3 us
  starting transfers between devices: 31.9 us -> 36.3 us
    psum x1 -> x0, blocking collectives: 10.7 us -> none  [per_device(): squares = lax.psum(squares, 'ry')]
    all_to_all x0 -> x1, starting transfers between devices: none -> 4.46 us  [per_device(): squares = jnp.sum(lax.all_to_all(spread, 'ry', 0, 0, tiled=True), axis=0)]
    all_to_all x0 -> x1, waiting for transfers between devices: none -> 4.25 us  [per_device(): squares = jnp.sum(lax.all_to_all(spread, 'ry', 0, 0, tiled=True), axis=0)]
  transfers between devices with their start and end apart: 5 -> 6, of which waited for: 4 -> 5; matrix products, arithmetic and copies ran while one was open for 4% -> 4% of each run, Pallas kernels for 0% -> 0%
where the time goes in v9:
time: 174 us; the launch traced here: 173 us
  waiting for transfers between devices  68.3 us (39%)
  blocking collectives  51.4 us (30%)
  starting transfers between devices  36.3 us (21%)
  local copies, waits for them, and re-layouts  8.85 us (5%)
  other arithmetic  5.8 us (3%)
  matrix products  2.31 us (1%)
    all_to_all x1, waiting for transfers between devices, per_device(): lax.all_to_all(outbound, 'expert', split_axis=1, concat_axis=1, tiled=True)  30.5 us
    all_to_all x1, waiting for transfers between devices, per_device(): lax.all_to_all(expert_out, 'expert', split_axis=1, concat_axis=1, tiled=T...  29.7 us
    all_to_all x1, blocking collectives, per_device(): lax.all_to_all(leaving, 'expert', split_axis=0, concat_axis=0, tiled=True)  21.6 us
    all_to_all x1, starting transfers between devices, per_device(): lax.all_to_all(outbound, 'expert', split_axis=1, concat_axis=1, tiled=True)  18.8 us
    all_to_all x1, blocking collectives, per_device(): lax.all_to_all(half_sum, 'ry', split_axis=0, concat_axis=0, tiled=True)  18.1 us
    all_to_all x1, blocking collectives, per_device(): lax.all_to_all(act_tile, 'ry', split_axis=0, concat_axis=0, tiled=True)  11.7 us
    all_to_all x1, starting transfers between devices, per_device(): lax.all_to_all(expert_out, 'expert', split_axis=1, concat_axis=1, tiled=T...  7.3 us
    all_to_all x1, starting transfers between devices, per_device(): squares = jnp.sum(lax.all_to_all(spread, 'ry', 0, 0, tiled=True), axis=0)  4.46 us
  transfers between devices with their start and end apart: 6, of which 5 were waited for; matrix products, arithmetic and copies ran while one was open for 4% of the time, Pallas kernels for 0%

profile of v9, /device:TPU:6, one launch (start us, length us, event | category | flops | bytes accessed | tf_op | source)
XLA Modules:
  0.0 173.4 jit_solution(16485762903913424562)
XLA Ops:
  0.0 1.2 fusion.6
  1.2 1.9 %collective-permute-start = (f32[128]{0:T(128)S(1)}, f32[128]{0:T(128)S(1)}, u32[]{:S(2)}, u32[]{:S(2)}) collective-permute-start(f32[128]{0:T(128)S(1)} %fusion.6), channel_id=1, source_target_pairs={{0,64},{64,0},{1,65},{65,1},{2,66},{66,2},{3,67},{67,3},{4,68},{68... | collective-permute-start | bytes 1544 | tf_op jit(solution)/shard_map/ppermute | solution.py:36
  3.1 0.8 copy.86
  4.1 0.7 broadcast_subtract_fusion
  7.8 4.5 %all-to-all-start = ((f32[4,1,128]{2,1,0:T(1,128)}), f32[4,1,128]{2,1,0:T(1,128)S(1)}, u32[]{:S(2)}, u32[]{:S(2)}) async-start(f32[4,1,128]{2,1,0:T(1,128)} %broadcast_in_dim.67), calls=%async_computation | async-start | bytes 4096 | tf_op jit(solution)/shard_map/all_to_all | solution.py:39
  12.2 0.9 convert_reduce_fusion
  13.1 4.2 %all-to-all-done = f32[4,1,128]{2,1,0:T(1,128)S(1)} async-done(((f32[4,1,128]{2,1,0:T(1,128)}), f32[4,1,128]{2,1,0:T(1,128)S(1)}, u32[]{:S(2)}, u32[]{:S(2)}) %all-to-all-start) | async-done | bytes 2080 | tf_op jit(solution)/shard_map/all_to_all | solution.py:39
  17.9 1.0 copy.98
  18.9 18.8 %all-to-all-start.1 = ((bf16[2,64,4,512]{3,2,0,1:T(4,128)(2,1)}), bf16[2,64,4,512]{3,2,0,1:T(4,128)(2,1)S(1)}, u32[]{:S(2)}, u32[]{:S(2)}) async-start(bf16[2,64,4,512]{3,2,0,1:T(4,128)(2,1)} %copy.98), calls=%async_computation.1 | async-start | bytes 1048576 | tf_op jit(solution)/shard_map/all_to_all | solution.py:49
  37.7 30.5 %all-to-all-done.1 = bf16[2,64,4,512]{3,2,0,1:T(4,128)(2,1)S(1)} async-done(((bf16[2,64,4,512]{3,2,0,1:T(4,128)(2,1)}), bf16[2,64,4,512]{3,2,0,1:T(4,128)(2,1)S(1)}, u32[]{:S(2)}, u32[]{:S(2)}) %all-to-all-start.1) | async-done | bytes 524320 | tf_op jit(solution)/shard_map/all_to_all | solution.py:49
  68.6 0.7 fusion.30
  70.2 1.9 %collective-permute-start.1 = (f32[4,512,128]{2,1,0:T(8,128)S(1)}, f32[4,512,128]{2,1,0:T(8,128)S(1)}, u32[]{:S(2)}, u32[]{:S(2)}) collective-permute-start(f32[4,512,128]{2,1,0:T(8,128)S(1)} %bitcast.55), channel_id=1, source_target_pairs={{0,64},{64,0},{1,65},{65,1},{2,66},{66,2},{3,67},{67,3},{4,68},{68... | collective-permute-start | bytes 3145736 | tf_op jit(solution)/shard_map/ppermute | solution.py:64
  72.1 2.6 %collective-permute-done.1 = f32[4,512,128]{2,1,0:T(8,128)S(1)} collective-permute-done((f32[4,512,128]{2,1,0:T(8,128)S(1)}, f32[4,512,128]{2,1,0:T(8,128)S(1)}, u32[]{:S(2)}, u32[]{:S(2)}) %collective-permute-start.1) | collective-permute-done | bytes 1048608 | tf_op jit(solution)/shard_map/ppermute | solution.py:64
  74.9 18.1 %all_to_all.31 = f32[4,512,128]{2,1,0:T(8,128)S(1)} all-to-all(f32[4,512,128]{2,1,0:T(8,128)S(1)} %fusion.2), channel_id=1, replica_groups=mesh['ry'=4,'rc'=2,'expert'=64] {'ry'}, dimensions={0} | all-to-all | bytes 2097152 | tf_op jit(solution)/shard_map/all_to_all | solution.py:65
  93.2 11.7 %all_to_all.32 = bf16[4,512,128]{2,1,0:T(8,128)(2,1)S(1)} all-to-all(bf16[4,512,128]{2,1,0:T(8,128)(2,1)S(1)} %broadcast_in_dim.68), channel_id=1, replica_groups=mesh['ry'=4,'rc'=2,'expert'=64] {'ry'}, dimensions={0} | all-to-all | bytes 1048576 | tf_op jit(solution)/shard_map/all_to_all | solution.py:69
  105.0 1.9 %collective-permute-start.2 = (bf16[4,512,128]{2,1,0:T(8,128)(2,1)S(1)}, bf16[4,512,128]{2,1,0:T(8,128)(2,1)S(1)}, u32[]{:S(2)}, u32[]{:S(2)}) collective-permute-start(bf16[4,512,128]{2,1,0:T(8,128)(2,1)S(1)} %all_to_all.32), channel_id=1, source_target_pairs={{0,64},{64,0},{1,65},{65,1},{2,66},{66,2},{3,67},{67,3},{4,68},{68... | collective-permute-start | bytes 1572872 | tf_op jit(solution)/shard_map/ppermute | solution.py:70
  107.5 1.2 collective-permute-done.2
  109.4 1.0 copy.104
  110.3 7.3 %all-to-all-start.4 = ((bf16[2,64,4,512]{3,2,0,1:T(4,128)(2,1)}), bf16[2,64,4,512]{3,2,0,1:T(4,128)(2,1)S(1)}, u32[]{:S(2)}, u32[]{:S(2)}) async-start(bf16[2,64,4,512]{3,2,0,1:T(4,128)(2,1)} %copy.104), calls=%async_computation.4 | async-start | bytes 1048576 | tf_op jit(solution)/shard_map/all_to_all | solution.py:82
  118.2 1.0 scatter_custom_fusion
  119.3 0.7 select_reduce_fusion
  120.0 29.7 %all-to-all-done.4 = bf16[2,64,4,512]{3,2,0,1:T(4,128)(2,1)S(1)} async-done(((bf16[2,64,4,512]{3,2,0,1:T(4,128)(2,1)}), bf16[2,64,4,512]{3,2,0,1:T(4,128)(2,1)S(1)}, u32[]{:S(2)}, u32[]{:S(2)}) %all-to-all-start.4) | async-done | bytes 524320 | tf_op jit(solution)/shard_map/all_to_all | solution.py:82
  151.1 21.6 %all_to_all.33 = f32[64,1,512]{2,1,0:T(1,128)S(1)} all-to-all(f32[64,1,512]{2,1,0:T(1,128)S(1)} %copy.106), channel_id=1, replica_groups=mesh['ry'=4,'rc'=2,'expert'=64] {'expert'}, dimensions={0} | all-to-all | bytes 262144 | tf_op jit(solution)/shard_map/all_to_all | solution.py:109
  172.8 0.7 copy.123
  (70 shorter events, 8.5 us)
Async XLA Ops:
  0.0 68.5 %copy-start = (bf16[2,512,1024]{2,1,0:T(8,128)(2,1)S(1)}, bf16[2,512,1024]{2,1,0:T(8,128)(2,1)}, u32[]{:S(2)}) copy-start(bf16[2,512,1024]{2,1,0:T(8,128)(2,1)} %param.14) | copy-start | bytes 6291460
  1.2 6.0 %collective-permute-start = (f32[128]{0:T(128)S(1)}, f32[128]{0:T(128)S(1)}, u32[]{:S(2)}, u32[]{:S(2)}) collective-permute-start(f32[128]{0:T(128)S(1)} %fusion.6), channel_id=1, source_target_pairs={{0,64},{64,0},{1,65},{65,1},{2,66},{66,2},{3,67},{67,3},{4,68},{68... | collective-permute-start | bytes 1544 | tf_op jit(solution)/shard_map/ppermute | solution.py:36
  4.0 13.4 %copy-start.2 = (bf16[128,512]{1,0:T(8,128)(2,1)S(1)}, bf16[128,512]{1,0:T(8,128)(2,1)}, u32[]{:S(2)}) copy-start(bf16[128,512]{1,0:T(8,128)(2,1)} %param.8) | copy-start | bytes 393220
  4.0 13.4 %copy-start.7 = (f32[512]{0:T(512)S(1)}, f32[512]{0:T(512)}, u32[]{:S(2)}) copy-start(f32[512]{0:T(512)} %param.9) | copy-start | bytes 6148
  7.1 10.3 %copy-start.3 = (s32[128,8]{1,0:T(8,128)}, s32[128,8]{1,0:T(8,128)S(1)}, u32[]{:S(2)}) copy-start(s32[128,8]{1,0:T(8,128)S(1)} %fusion.20) | copy-start | bytes 12292
  7.8 9.6 %all-to-all-start = ((f32[4,1,128]{2,1,0:T(1,128)}), f32[4,1,128]{2,1,0:T(1,128)S(1)}, u32[]{:S(2)}, u32[]{:S(2)}) async-start(f32[4,1,128]{2,1,0:T(1,128)} %broadcast_in_dim.67), calls=%async_computation | async-start | bytes 4096 | tf_op jit(solution)/shard_map/all_to_all | solution.py:39
  18.9 49.3 %all-to-all-start.1 = ((bf16[2,64,4,512]{3,2,0,1:T(4,128)(2,1)}), bf16[2,64,4,512]{3,2,0,1:T(4,128)(2,1)S(1)}, u32[]{:S(2)}, u32[]{:S(2)}) async-start(bf16[2,64,4,512]{3,2,0,1:T(4,128)(2,1)} %copy.98), calls=%async_computation.1 | async-start | bytes 1048576 | tf_op jit(solution)/shard_map/all_to_all | solution.py:49
  70.2 4.6 %collective-permute-start.1 = (f32[4,512,128]{2,1,0:T(8,128)S(1)}, f32[4,512,128]{2,1,0:T(8,128)S(1)}, u32[]{:S(2)}, u32[]{:S(2)}) collective-permute-start(f32[4,512,128]{2,1,0:T(8,128)S(1)} %bitcast.55), channel_id=1, source_target_pairs={{0,64},{64,0},{1,65},{65,1},{2,66},{66,2},{3,67},{67,3},{4,68},{68... | collective-permute-start | bytes 3145736 | tf_op jit(solution)/shard_map/ppermute | solution.py:64
  93.0 13.8 %copy-start.1 = (bf16[2,1024,512]{2,1,0:T(8,128)(2,1)S(1)}, bf16[2,1024,512]{2,1,0:T(8,128)(2,1)}, u32[]{:S(2)}) copy-start(bf16[2,1024,512]{2,1,0:T(8,128)(2,1)} %param.15) | copy-start | bytes 6291460
  105.0 3.8 %collective-permute-start.2 = (bf16[4,512,128]{2,1,0:T(8,128)(2,1)S(1)}, bf16[4,512,128]{2,1,0:T(8,128)(2,1)S(1)}, u32[]{:S(2)}, u32[]{:S(2)}) collective-permute-start(bf16[4,512,128]{2,1,0:T(8,128)(2,1)S(1)} %all_to_all.32), channel_id=1, source_target_pairs={{0,64},{64,0},{1,65},{65,1},{2,66},{66,2},{3,67},{67,3},{4,68},{68... | collective-permute-start | bytes 1572872 | tf_op jit(solution)/shard_map/ppermute | solution.py:70
  109.2 8.5 %copy-start.6 = (f32[128,8]{0,1:T(8,128)S(1)}, f32[128,8]{0,1:T(8,128)}, u32[]{:S(2)}) copy-start(f32[128,8]{0,1:T(8,128)} %param.10) | copy-start | bytes 12292
  109.2 8.6 %copy-start.5 = (s32[128]{0:T(128)S(1)}, s32[128]{0:T(128)}, u32[]{:S(2)}) copy-start(s32[128]{0:T(128)} %param.13) | copy-start | bytes 1540
  109.2 9.0 %copy-start.8 = (s32[128]{0:T(128)S(1)}, s32[128]{0:T(128)}, u32[]{:S(2)}) copy-start(s32[128]{0:T(128)} %param.11) | copy-start | bytes 1540
  109.4 9.9 %copy-start.4 = (s32[128,8]{1,0:T(8,128)S(1)}, s32[128,8]{1,0:T(8,128)}, u32[]{:S(2)}) copy-start(s32[128,8]{1,0:T(8,128)} %copy-done.3) | copy-start | bytes 12292
  110.3 39.3 %all-to-all-start.4 = ((bf16[2,64,4,512]{3,2,0,1:T(4,128)(2,1)}), bf16[2,64,4,512]{3,2,0,1:T(4,128)(2,1)S(1)}, u32[]{:S(2)}, u32[]{:S(2)}) async-start(bf16[2,64,4,512]{3,2,0,1:T(4,128)(2,1)} %copy.104), calls=%async_computation.4 | async-start | bytes 1048576 | tf_op jit(solution)/shard_map/all_to_all | solution.py:82

commit v10 on v7

--- a/solution.py
+++ b/solution.py
@@ -33,8 +33,8 @@
     slot_index = (local_id * owner_count + owner_id) * capacity + position
     slot_index = jnp.where(pair_live > 0, slot_index, slot_total)
     squares = jnp.sum(widened * widened, axis=1)
-    squares = squares + lax.ppermute(squares, "rc", [(0, 1), (1, 0)])
-    squares = lax.psum(squares, "ry")
+    spread = jnp.broadcast_to(squares[None], (rep_count,) + squares.shape)
+    squares = jnp.sum(lax.all_to_all(spread, ("ry", "rc"), 0, 0, tiled=True), axis=0)
     rinv_rows = lax.rsqrt(squares / (feat_width * rep_count) + 1e-06)
     normed = (widened * rinv_rows[:, None] * norm_gain[None, :]).astype(jnp.bfloat16)
     slot_ids = jnp.arange(slot_total, dtype=jnp.int32)

time: 175 us -> 170 us (0.971)
  blocking collectives: 62.2 us -> 52.3 us
  waiting for transfers between devices: 63.4 us -> 65.9 us
  starting transfers between devices: 31.9 us -> 34 us
    psum x1 -> x0, blocking collectives: 10.7 us -> none  [per_device(): squares = lax.psum(squares, 'ry')]
    all_to_all x0 -> x1, starting transfers between devices: none -> 4.47 us  [per_device(): lax.all_to_all(spread, ('ry', 'rc'), 0, 0, tiled=True)]
    all_to_all x1, waiting for transfers between devices: 29.8 us -> 32.1 us  [per_device(): lax.all_to_all(outbound, 'expert', split_axis=1, concat_axis=1, tiled=True)]
    ppermute x1 -> x0, starting transfers between devices: 1.92 us -> none  [per_device(): squares = squares + lax.ppermute(squares, 'rc', [(0, 1), (1, 0)])]
  transfers between devices with their start and end apart: 5 -> 5, of which waited for: 4 -> 5; matrix products, arithmetic and copies ran while one was open for 4% -> 5% of each run, Pallas kernels for 0% -> 0%
where the time goes in v10:
time: 170 us
  waiting for transfers between devices  65.9 us (39%)
  blocking collectives  52.3 us (31%)
  starting transfers between devices  34 us (20%)
  local copies, waits for them, and re-layouts  8.83 us (5%)
  other arithmetic  5.82 us (3%)
  matrix products  2.31 us (1%)
    all_to_all x1, waiting for transfers between devices, per_device(): lax.all_to_all(outbound, 'expert', split_axis=1, concat_axis=1, tiled=True)  32.1 us
    all_to_all x1, waiting for transfers between devices, per_device(): lax.all_to_all(expert_out, 'expert', split_axis=1, concat_axis=1, tiled=T...  29.7 us
    all_to_all x1, blocking collectives, per_device(): lax.all_to_all(leaving, 'expert', split_axis=0, concat_axis=0, tiled=True)  21.6 us
    all_to_all x1, blocking collectives, per_device(): lax.all_to_all(half_sum, 'ry', split_axis=0, concat_axis=0, tiled=True)  19.6 us
    all_to_all x1, starting transfers between devices, per_device(): lax.all_to_all(outbound, 'expert', split_axis=1, concat_axis=1, tiled=True)  18.8 us
    all_to_all x1, blocking collectives, per_device(): lax.all_to_all(act_tile, 'ry', split_axis=0, concat_axis=0, tiled=True)  11.2 us
    all_to_all x1, starting transfers between devices, per_device(): lax.all_to_all(expert_out, 'expert', split_axis=1, concat_axis=1, tiled=T...  6.9 us
    all_to_all x1, starting transfers between devices, per_device(): lax.all_to_all(spread, ('ry', 'rc'), 0, 0, tiled=True)  4.47 us
  transfers between devices with their start and end apart: 5, of which 5 were waited for; matrix products, arithmetic and copies ran while one was open for 5% of the time, Pallas kernels for 0%

profile of v10, /device:TPU:6, one launch (start us, length us, event | category | flops | bytes accessed | tf_op | source)
XLA Modules:
  0.0 169.6 jit_solution(11784881906638747288)
XLA Ops:
  0.0 1.2 fusion.6
  1.8 4.5 %all-to-all-start = ((f32[8,1,128]{2,1,0:T(1,128)}), f32[8,1,128]{2,1,0:T(1,128)S(1)}, u32[]{:S(2)}, u32[]{:S(2)}) async-start(f32[8,1,128]{2,1,0:T(1,128)} %broadcast_in_dim.67), calls=%async_computation | async-start | bytes 8192 | tf_op jit(solution)/shard_map/all_to_all | solution.py:37
  6.2 0.8 copy.86
  7.2 0.7 broadcast_subtract_fusion
  7.9 0.7 broadcast_compare_fusion
  10.3 0.9 convert_reduce_fusion
  12.1 1.0 copy.98
  13.1 18.8 %all-to-all-start.1 = ((bf16[2,64,4,512]{3,2,0,1:T(4,128)(2,1)}), bf16[2,64,4,512]{3,2,0,1:T(4,128)(2,1)S(1)}, u32[]{:S(2)}, u32[]{:S(2)}) async-start(bf16[2,64,4,512]{3,2,0,1:T(4,128)(2,1)} %copy.98), calls=%async_computation.1 | async-start | bytes 1048576 | tf_op jit(solution)/shard_map/all_to_all | solution.py:47
  31.9 32.1 %all-to-all-done.1 = bf16[2,64,4,512]{3,2,0,1:T(4,128)(2,1)S(1)} async-done(((bf16[2,64,4,512]{3,2,0,1:T(4,128)(2,1)}), bf16[2,64,4,512]{3,2,0,1:T(4,128)(2,1)S(1)}, u32[]{:S(2)}, u32[]{:S(2)}) %all-to-all-start.1) | async-done | bytes 524320 | tf_op jit(solution)/shard_map/all_to_all | solution.py:47
  64.2 0.7 fusion.30
  65.9 1.9 %collective-permute-start = (f32[4,512,128]{2,1,0:T(8,128)S(1)}, f32[4,512,128]{2,1,0:T(8,128)S(1)}, u32[]{:S(2)}, u32[]{:S(2)}) collective-permute-start(f32[4,512,128]{2,1,0:T(8,128)S(1)} %bitcast.55), channel_id=1, source_target_pairs={{0,64},{64,0},{1,65},{65,1},{2,66},{66,2},{3,67},{67,3},{4,68},{68... | collective-permute-start | bytes 3145736 | tf_op jit(solution)/shard_map/ppermute | solution.py:62
  67.8 2.6 %collective-permute-done = f32[4,512,128]{2,1,0:T(8,128)S(1)} collective-permute-done((f32[4,512,128]{2,1,0:T(8,128)S(1)}, f32[4,512,128]{2,1,0:T(8,128)S(1)}, u32[]{:S(2)}, u32[]{:S(2)}) %collective-permute-start) | collective-permute-done | bytes 1048608 | tf_op jit(solution)/shard_map/ppermute | solution.py:62
  70.6 19.6 %all_to_all.31 = f32[4,512,128]{2,1,0:T(8,128)S(1)} all-to-all(f32[4,512,128]{2,1,0:T(8,128)S(1)} %fusion.2), channel_id=1, replica_groups=mesh['ry'=4,'rc'=2,'expert'=64] {'ry'}, dimensions={0} | all-to-all | bytes 2097152 | tf_op jit(solution)/shard_map/all_to_all | solution.py:63
  90.4 11.2 %all_to_all.32 = bf16[4,512,128]{2,1,0:T(8,128)(2,1)S(1)} all-to-all(bf16[4,512,128]{2,1,0:T(8,128)(2,1)S(1)} %broadcast_in_dim.68), channel_id=1, replica_groups=mesh['ry'=4,'rc'=2,'expert'=64] {'ry'}, dimensions={0} | all-to-all | bytes 1048576 | tf_op jit(solution)/shard_map/all_to_all | solution.py:67
  101.5 1.9 %collective-permute-start.1 = (bf16[4,512,128]{2,1,0:T(8,128)(2,1)S(1)}, bf16[4,512,128]{2,1,0:T(8,128)(2,1)S(1)}, u32[]{:S(2)}, u32[]{:S(2)}) collective-permute-start(bf16[4,512,128]{2,1,0:T(8,128)(2,1)S(1)} %all_to_all.32), channel_id=1, source_target_pairs={{0,64},{64,0},{1,65},{65,1},{2,66},{66,2},{3,67},{67,3},{4,68},{68... | collective-permute-start | bytes 1572872 | tf_op jit(solution)/shard_map/ppermute | solution.py:68
  104.1 1.2 collective-permute-done.1
  105.9 1.0 copy.104
  106.9 6.9 %all-to-all-start.4 = ((bf16[2,64,4,512]{3,2,0,1:T(4,128)(2,1)}), bf16[2,64,4,512]{3,2,0,1:T(4,128)(2,1)S(1)}, u32[]{:S(2)}, u32[]{:S(2)}) async-start(bf16[2,64,4,512]{3,2,0,1:T(4,128)(2,1)} %copy.104), calls=%async_computation.4 | async-start | bytes 1048576 | tf_op jit(solution)/shard_map/all_to_all | solution.py:80
  114.4 1.0 scatter_custom_fusion
  115.4 0.7 select_reduce_fusion
  116.1 29.7 %all-to-all-done.4 = bf16[2,64,4,512]{3,2,0,1:T(4,128)(2,1)S(1)} async-done(((bf16[2,64,4,512]{3,2,0,1:T(4,128)(2,1)}), bf16[2,64,4,512]{3,2,0,1:T(4,128)(2,1)S(1)}, u32[]{:S(2)}, u32[]{:S(2)}) %all-to-all-start.4) | async-done | bytes 524320 | tf_op jit(solution)/shard_map/all_to_all | solution.py:80
  146.5 0.7 gather_fusion
  147.3 21.6 %all_to_all.33 = f32[64,1,512]{2,1,0:T(1,128)S(1)} all-to-all(f32[64,1,512]{2,1,0:T(1,128)S(1)} %copy.106), channel_id=1, replica_groups=mesh['ry'=4,'rc'=2,'expert'=64] {'expert'}, dimensions={0} | all-to-all | bytes 262144 | tf_op jit(solution)/shard_map/all_to_all | solution.py:107
  168.9 0.7 copy.123
  (67 shorter events, 7.5 us)
Async XLA Ops:
  0.0 64.2 %copy-start = (bf16[2,512,1024]{2,1,0:T(8,128)(2,1)S(1)}, bf16[2,512,1024]{2,1,0:T(8,128)(2,1)}, u32[]{:S(2)}) copy-start(bf16[2,512,1024]{2,1,0:T(8,128)(2,1)} %param.14) | copy-start | bytes 6291460
  1.8 9.8 %all-to-all-start = ((f32[8,1,128]{2,1,0:T(1,128)}), f32[8,1,128]{2,1,0:T(1,128)S(1)}, u32[]{:S(2)}, u32[]{:S(2)}) async-start(f32[8,1,128]{2,1,0:T(1,128)} %broadcast_in_dim.67), calls=%async_computation | async-start | bytes 8192 | tf_op jit(solution)/shard_map/all_to_all | solution.py:37
  7.1 4.4 %copy-start.2 = (bf16[128,512]{1,0:T(8,128)(2,1)S(1)}, bf16[128,512]{1,0:T(8,128)(2,1)}, u32[]{:S(2)}) copy-start(bf16[128,512]{1,0:T(8,128)(2,1)} %param.8) | copy-start | bytes 393220
  7.1 4.4 %copy-start.7 = (f32[512]{0:T(512)S(1)}, f32[512]{0:T(512)}, u32[]{:S(2)}) copy-start(f32[512]{0:T(512)} %param.9) | copy-start | bytes 6148
  10.2 1.3 copy-start.3
  13.1 50.9 %all-to-all-start.1 = ((bf16[2,64,4,512]{3,2,0,1:T(4,128)(2,1)}), bf16[2,64,4,512]{3,2,0,1:T(4,128)(2,1)S(1)}, u32[]{:S(2)}, u32[]{:S(2)}) async-start(bf16[2,64,4,512]{3,2,0,1:T(4,128)(2,1)} %copy.98), calls=%async_computation.1 | async-start | bytes 1048576 | tf_op jit(solution)/shard_map/all_to_all | solution.py:47
  65.9 4.6 %collective-permute-start = (f32[4,512,128]{2,1,0:T(8,128)S(1)}, f32[4,512,128]{2,1,0:T(8,128)S(1)}, u32[]{:S(2)}, u32[]{:S(2)}) collective-permute-start(f32[4,512,128]{2,1,0:T(8,128)S(1)} %bitcast.55), channel_id=1, source_target_pairs={{0,64},{64,0},{1,65},{65,1},{2,66},{66,2},{3,67},{67,3},{4,68},{68... | collective-permute-start | bytes 3145736 | tf_op jit(solution)/shard_map/ppermute | solution.py:62
  90.2 13.3 %copy-start.1 = (bf16[2,1024,512]{2,1,0:T(8,128)(2,1)S(1)}, bf16[2,1024,512]{2,1,0:T(8,128)(2,1)}, u32[]{:S(2)}) copy-start(bf16[2,1024,512]{2,1,0:T(8,128)(2,1)} %param.15) | copy-start | bytes 6291460
  101.5 3.8 %collective-permute-start.1 = (bf16[4,512,128]{2,1,0:T(8,128)(2,1)S(1)}, bf16[4,512,128]{2,1,0:T(8,128)(2,1)S(1)}, u32[]{:S(2)}, u32[]{:S(2)}) collective-permute-start(bf16[4,512,128]{2,1,0:T(8,128)(2,1)S(1)} %all_to_all.32), channel_id=1, source_target_pairs={{0,64},{64,0},{1,65},{65,1},{2,66},{66,2},{3,67},{67,3},{4,68},{68... | collective-permute-start | bytes 1572872 | tf_op jit(solution)/shard_map/ppermute | solution.py:68
  105.8 8.1 %copy-start.6 = (f32[128,8]{0,1:T(8,128)S(1)}, f32[128,8]{0,1:T(8,128)}, u32[]{:S(2)}) copy-start(f32[128,8]{0,1:T(8,128)} %param.10) | copy-start | bytes 12292
  105.8 8.2 %copy-start.5 = (s32[128]{0:T(128)S(1)}, s32[128]{0:T(128)}, u32[]{:S(2)}) copy-start(s32[128]{0:T(128)} %param.13) | copy-start | bytes 1540
  105.8 8.6 %copy-start.8 = (s32[128]{0:T(128)S(1)}, s32[128]{0:T(128)}, u32[]{:S(2)}) copy-start(s32[128]{0:T(128)} %param.11) | copy-start | bytes 1540
  105.9 9.5 %copy-start.4 = (s32[128,8]{1,0:T(8,128)S(1)}, s32[128,8]{1,0:T(8,128)}, u32[]{:S(2)}) copy-start(s32[128,8]{1,0:T(8,128)} %copy-done.3) | copy-start | bytes 12292
  106.9 38.9 %all-to-all-start.4 = ((bf16[2,64,4,512]{3,2,0,1:T(4,128)(2,1)}), bf16[2,64,4,512]{3,2,0,1:T(4,128)(2,1)S(1)}, u32[]{:S(2)}, u32[]{:S(2)}) async-start(bf16[2,64,4,512]{3,2,0,1:T(4,128)(2,1)} %copy.104), calls=%async_computation.4 | async-start | bytes 1048576 | tf_op jit(solution)/shard_map/all_to_all | solution.py:80

commit v11 on v10

--- a/solution.py
+++ b/solution.py
@@ -32,8 +32,13 @@
     local_id = route_flat % local_experts
     slot_index = (local_id * owner_count + owner_id) * capacity + position
     slot_index = jnp.where(pair_live > 0, slot_index, slot_total)
-    squares = jnp.sum(widened * widened, axis=1)
-    spread = jnp.broadcast_to(squares[None], (rep_count,) + squares.shape)
+    squares = jnp.dot(
+        widened * widened,
+        jnp.ones((feat_width, rep_count), jnp.float32),
+        precision=lax.Precision.HIGHEST,
+        preferred_element_type=jnp.float32,
+    )
+    spread = jnp.transpose(squares)
     squares = jnp.sum(lax.all_to_all(spread, ("ry", "rc"), 0, 0, tiled=True), axis=0)
     rinv_rows = lax.rsqrt(squares / (feat_width * rep_count) + 1e-06)
     normed = (widened * rinv_rows[:, None] * norm_gain[None, :]).astype(jnp.bfloat16)

time: 170 us -> 170 us (level)
  matrix products: 2.31 us -> 4.35 us
    dot_general x0 -> x1, matrix products: none -> 2.04 us  [per_device(): jnp.dot(widened * widened, jnp.ones((feat_width, rep_count), jnp.float32)...]
where the time goes in v11:
time: 170 us
  waiting for transfers between devices  65.9 us (39%)
  blocking collectives  52.3 us (31%)
  starting transfers between devices  34 us (20%)
  local copies, waits for them, and re-layouts  8.22 us (5%)
  other arithmetic  4.67 us (3%)
  matrix products  4.35 us (3%)
    all_to_all x1, waiting for transfers between devices, per_device(): lax.all_to_all(outbound, 'expert', split_axis=1, concat_axis=1, tiled=True)  32.1 us
    all_to_all x1, waiting for transfers between devices, per_device(): lax.all_to_all(expert_out, 'expert', split_axis=1, concat_axis=1, tiled=T...  29.7 us
    all_to_all x1, blocking collectives, per_device(): lax.all_to_all(leaving, 'expert', split_axis=0, concat_axis=0, tiled=True)  21.6 us
    all_to_all x1, blocking collectives, per_device(): lax.all_to_all(half_sum, 'ry', split_axis=0, concat_axis=0, tiled=True)  19.6 us
    all_to_all x1, starting transfers between devices, per_device(): lax.all_to_all(outbound, 'expert', split_axis=1, concat_axis=1, tiled=True)  18.8 us
    all_to_all x1, blocking collectives, per_device(): lax.all_to_all(act_tile, 'ry', split_axis=0, concat_axis=0, tiled=True)  11.2 us
    all_to_all x1, starting transfers between devices, per_device(): lax.all_to_all(expert_out, 'expert', split_axis=1, concat_axis=1, tiled=T...  6.91 us
    all_to_all x1, starting transfers between devices, per_device(): lax.all_to_all(spread, ('ry', 'rc'), 0, 0, tiled=True)  4.47 us
  transfers between devices with their start and end apart: 5, of which 5 were waited for; matrix products, arithmetic and copies ran while one was open for 5% of the time, Pallas kernels for 0%

profile of v11, /device:TPU:6, one launch (start us, length us, event | category | flops | bytes accessed | tf_op | source)
XLA Modules:
  0.0 169.9 jit_solution(9049136869835600078)
XLA Ops:
  0.0 2.0 %fusion.6 = f32[8,128]{1,0:T(8,128)} fusion(bf16[128,512]{1,0:T(8,128)(2,1)} %param.8), kind=kOutput, calls=%fused_computation.25 | convolution fusion | flops 6422528 | bytes 135168 | tf_op jit(solution)/shard_map/dot_general | solution.py:35
  2.0 4.5 %all-to-all-start = ((f32[8,1,128]{2,1,0:T(1,128)}), f32[8,1,128]{2,1,0:T(1,128)S(1)}, u32[]{:S(2)}, u32[]{:S(2)}) async-start(f32[8,1,128]{2,1,0:T(1,128)} %bitcast.5), calls=%async_computation | async-start | bytes 8192 | tf_op jit(solution)/shard_map/all_to_all | solution.py:42
  6.5 0.8 copy.68
  7.5 0.7 broadcast_subtract_fusion
  8.2 0.7 broadcast_compare_fusion
  10.6 0.9 convert_reduce_fusion
  12.4 1.0 copy.80
  13.3 18.8 %all-to-all-start.1 = ((bf16[2,64,4,512]{3,2,0,1:T(4,128)(2,1)}), bf16[2,64,4,512]{3,2,0,1:T(4,128)(2,1)S(1)}, u32[]{:S(2)}, u32[]{:S(2)}) async-start(bf16[2,64,4,512]{3,2,0,1:T(4,128)(2,1)} %copy.80), calls=%async_computation.1 | async-start | bytes 1048576 | tf_op jit(solution)/shard_map/all_to_all | solution.py:52
  32.1 32.1 %all-to-all-done.1 = bf16[2,64,4,512]{3,2,0,1:T(4,128)(2,1)S(1)} async-done(((bf16[2,64,4,512]{3,2,0,1:T(4,128)(2,1)}), bf16[2,64,4,512]{3,2,0,1:T(4,128)(2,1)S(1)}, u32[]{:S(2)}, u32[]{:S(2)}) %all-to-all-start.1) | async-done | bytes 524320 | tf_op jit(solution)/shard_map/all_to_all | solution.py:52
  64.5 0.7 fusion.32
  66.2 1.9 %collective-permute-start = (f32[4,512,128]{2,1,0:T(8,128)S(1)}, f32[4,512,128]{2,1,0:T(8,128)S(1)}, u32[]{:S(2)}, u32[]{:S(2)}) collective-permute-start(f32[4,512,128]{2,1,0:T(8,128)S(1)} %bitcast.57), channel_id=1, source_target_pairs={{0,64},{64,0},{1,65},{65,1},{2,66},{66,2},{3,67},{67,3},{4,68},{68... | collective-permute-start | bytes 3145736 | tf_op jit(solution)/shard_map/ppermute | solution.py:67
  68.1 2.6 %collective-permute-done = f32[4,512,128]{2,1,0:T(8,128)S(1)} collective-permute-done((f32[4,512,128]{2,1,0:T(8,128)S(1)}, f32[4,512,128]{2,1,0:T(8,128)S(1)}, u32[]{:S(2)}, u32[]{:S(2)}) %collective-permute-start) | collective-permute-done | bytes 1048608 | tf_op jit(solution)/shard_map/ppermute | solution.py:67
  70.8 19.6 %all_to_all.34 = f32[4,512,128]{2,1,0:T(8,128)S(1)} all-to-all(f32[4,512,128]{2,1,0:T(8,128)S(1)} %fusion.2), channel_id=1, replica_groups=mesh['ry'=4,'rc'=2,'expert'=64] {'ry'}, dimensions={0} | all-to-all | bytes 2097152 | tf_op jit(solution)/shard_map/all_to_all | solution.py:68
  90.6 11.2 %all_to_all.35 = bf16[4,512,128]{2,1,0:T(8,128)(2,1)S(1)} all-to-all(bf16[4,512,128]{2,1,0:T(8,128)(2,1)S(1)} %broadcast_in_dim.65), channel_id=1, replica_groups=mesh['ry'=4,'rc'=2,'expert'=64] {'ry'}, dimensions={0} | all-to-all | bytes 1048576 | tf_op jit(solution)/shard_map/all_to_all | solution.py:72
  101.8 1.9 %collective-permute-start.1 = (bf16[4,512,128]{2,1,0:T(8,128)(2,1)S(1)}, bf16[4,512,128]{2,1,0:T(8,128)(2,1)S(1)}, u32[]{:S(2)}, u32[]{:S(2)}) collective-permute-start(bf16[4,512,128]{2,1,0:T(8,128)(2,1)S(1)} %all_to_all.35), channel_id=1, source_target_pairs={{0,64},{64,0},{1,65},{65,1},{2,66},{66,2},{3,67},{67,3},{4,68},{68... | collective-permute-start | bytes 1572872 | tf_op jit(solution)/shard_map/ppermute | solution.py:73
  104.4 1.2 collective-permute-done.1
  106.2 1.0 copy.86
  107.2 6.9 %all-to-all-start.4 = ((bf16[2,64,4,512]{3,2,0,1:T(4,128)(2,1)}), bf16[2,64,4,512]{3,2,0,1:T(4,128)(2,1)S(1)}, u32[]{:S(2)}, u32[]{:S(2)}) async-start(bf16[2,64,4,512]{3,2,0,1:T(4,128)(2,1)} %copy.86), calls=%async_computation.4 | async-start | bytes 1048576 | tf_op jit(solution)/shard_map/all_to_all | solution.py:85
  114.7 1.0 scatter_custom_fusion
  115.7 0.7 select_reduce_fusion
  116.4 29.7 %all-to-all-done.4 = bf16[2,64,4,512]{3,2,0,1:T(4,128)(2,1)S(1)} async-done(((bf16[2,64,4,512]{3,2,0,1:T(4,128)(2,1)}), bf16[2,64,4,512]{3,2,0,1:T(4,128)(2,1)S(1)}, u32[]{:S(2)}, u32[]{:S(2)}) %all-to-all-start.4) | async-done | bytes 524320 | tf_op jit(solution)/shard_map/all_to_all | solution.py:85
  146.8 0.7 gather_fusion
  147.6 21.6 %all_to_all.36 = f32[64,1,512]{2,1,0:T(1,128)S(1)} all-to-all(f32[64,1,512]{2,1,0:T(1,128)S(1)} %copy.88), channel_id=1, replica_groups=mesh['ry'=4,'rc'=2,'expert'=64] {'expert'}, dimensions={0} | all-to-all | bytes 262144 | tf_op jit(solution)/shard_map/all_to_all | solution.py:112
  169.2 0.7 copy.105
  (66 shorter events, 6.9 us)
Async XLA Ops:
  0.0 64.5 %copy-start = (bf16[2,512,1024]{2,1,0:T(8,128)(2,1)S(1)}, bf16[2,512,1024]{2,1,0:T(8,128)(2,1)}, u32[]{:S(2)}) copy-start(bf16[2,512,1024]{2,1,0:T(8,128)(2,1)} %param.14) | copy-start | bytes 6291460
  2.0 9.8 %all-to-all-start = ((f32[8,1,128]{2,1,0:T(1,128)}), f32[8,1,128]{2,1,0:T(1,128)S(1)}, u32[]{:S(2)}, u32[]{:S(2)}) async-start(f32[8,1,128]{2,1,0:T(1,128)} %bitcast.5), calls=%async_computation | async-start | bytes 8192 | tf_op jit(solution)/shard_map/all_to_all | solution.py:42
  7.4 4.5 %copy-start.2 = (bf16[128,512]{1,0:T(8,128)(2,1)S(1)}, bf16[128,512]{1,0:T(8,128)(2,1)}, u32[]{:S(2)}) copy-start(bf16[128,512]{1,0:T(8,128)(2,1)} %param.8) | copy-start | bytes 393220
  7.4 4.5 %copy-start.7 = (f32[512]{0:T(512)S(1)}, f32[512]{0:T(512)}, u32[]{:S(2)}) copy-start(f32[512]{0:T(512)} %param.9) | copy-start | bytes 6148
  10.5 1.3 copy-start.3
  13.3 50.9 %all-to-all-start.1 = ((bf16[2,64,4,512]{3,2,0,1:T(4,128)(2,1)}), bf16[2,64,4,512]{3,2,0,1:T(4,128)(2,1)S(1)}, u32[]{:S(2)}, u32[]{:S(2)}) async-start(bf16[2,64,4,512]{3,2,0,1:T(4,128)(2,1)} %copy.80), calls=%async_computation.1 | async-start | bytes 1048576 | tf_op jit(solution)/shard_map/all_to_all | solution.py:52
  66.2 4.6 %collective-permute-start = (f32[4,512,128]{2,1,0:T(8,128)S(1)}, f32[4,512,128]{2,1,0:T(8,128)S(1)}, u32[]{:S(2)}, u32[]{:S(2)}) collective-permute-start(f32[4,512,128]{2,1,0:T(8,128)S(1)} %bitcast.57), channel_id=1, source_target_pairs={{0,64},{64,0},{1,65},{65,1},{2,66},{66,2},{3,67},{67,3},{4,68},{68... | collective-permute-start | bytes 3145736 | tf_op jit(solution)/shard_map/ppermute | solution.py:67
  90.5 13.3 %copy-start.1 = (bf16[2,1024,512]{2,1,0:T(8,128)(2,1)S(1)}, bf16[2,1024,512]{2,1,0:T(8,128)(2,1)}, u32[]{:S(2)}) copy-start(bf16[2,1024,512]{2,1,0:T(8,128)(2,1)} %param.15) | copy-start | bytes 6291460
  101.8 3.8 %collective-permute-start.1 = (bf16[4,512,128]{2,1,0:T(8,128)(2,1)S(1)}, bf16[4,512,128]{2,1,0:T(8,128)(2,1)S(1)}, u32[]{:S(2)}, u32[]{:S(2)}) collective-permute-start(bf16[4,512,128]{2,1,0:T(8,128)(2,1)S(1)} %all_to_all.35), channel_id=1, source_target_pairs={{0,64},{64,0},{1,65},{65,1},{2,66},{66,2},{3,67},{67,3},{4,68},{68... | collective-permute-start | bytes 1572872 | tf_op jit(solution)/shard_map/ppermute | solution.py:73
  106.0 8.1 %copy-start.6 = (f32[128,8]{0,1:T(8,128)S(1)}, f32[128,8]{0,1:T(8,128)}, u32[]{:S(2)}) copy-start(f32[128,8]{0,1:T(8,128)} %param.10) | copy-start | bytes 12292
  106.0 8.2 %copy-start.5 = (s32[128]{0:T(128)S(1)}, s32[128]{0:T(128)}, u32[]{:S(2)}) copy-start(s32[128]{0:T(128)} %param.13) | copy-start | bytes 1540
  106.1 8.6 %copy-start.8 = (s32[128]{0:T(128)S(1)}, s32[128]{0:T(128)}, u32[]{:S(2)}) copy-start(s32[128]{0:T(128)} %param.11) | copy-start | bytes 1540
  106.2 9.5 %copy-start.4 = (s32[128,8]{1,0:T(8,128)S(1)}, s32[128,8]{1,0:T(8,128)}, u32[]{:S(2)}) copy-start(s32[128,8]{1,0:T(8,128)} %copy-done.3) | copy-start | bytes 12292
  107.2 38.9 %all-to-all-start.4 = ((bf16[2,64,4,512]{3,2,0,1:T(4,128)(2,1)}), bf16[2,64,4,512]{3,2,0,1:T(4,128)(2,1)S(1)}, u32[]{:S(2)}, u32[]{:S(2)}) async-start(bf16[2,64,4,512]{3,2,0,1:T(4,128)(2,1)} %copy.86), calls=%async_computation.4 | async-start | bytes 1048576 | tf_op jit(solution)/shard_map/all_to_all | solution.py:85

commit v12 on v10

--- a/solution.py
+++ b/solution.py
@@ -21,27 +21,31 @@
     hid_part = hid // rep_count
     widened = tokens.astype(jnp.float32)
     survive = 1 - exit_flags
-    pair_live = jnp.repeat(survive, route_count)
-    route_flat = routes.reshape(-1)
-    one_hot = (route_flat[:, None] == jnp.arange(experts_all, dtype=jnp.int32)[None, :]).astype(
-        jnp.int32
-    ) * pair_live[:, None]
-    earlier = jnp.cumsum(one_hot, axis=0) - one_hot
-    position = jnp.sum(earlier * one_hot, axis=1)
-    owner_id = route_flat // local_experts
-    local_id = route_flat % local_experts
-    slot_index = (local_id * owner_count + owner_id) * capacity + position
-    slot_index = jnp.where(pair_live > 0, slot_index, slot_total)
+    hit = routes[:, :, None] == jnp.arange(experts_all, dtype=jnp.int32)[None, None, :]
+    chosen = jnp.sum(hit.astype(jnp.float32), axis=1) * survive[:, None].astype(jnp.float32)
+    gate_of = jnp.sum(jnp.where(hit, gate_weights[:, :, None], 0.0), axis=1)
+    row_ids = jnp.arange(row_count, dtype=jnp.int32)
+    before = (row_ids[:, None] > row_ids[None, :]).astype(jnp.bfloat16)
+    count = jnp.dot(before, chosen.astype(jnp.bfloat16), preferred_element_type=jnp.float32)
+    cap_ids = jnp.arange(capacity, dtype=jnp.float32)
+    in_slot = chosen[:, :, None] * (count[:, :, None] == cap_ids[None, None, :]).astype(
+        jnp.float32
+    )
+    in_slot = jnp.transpose(
+        in_slot.reshape(row_count, owner_count, local_experts, capacity), (0, 2, 1, 3)
+    ).reshape(row_count, slot_total)
+    gate_slot = jnp.transpose(
+        gate_of.reshape(row_count, owner_count, local_experts, 1), (0, 2, 1, 3)
+    )
+    gate_slot = jnp.broadcast_to(
+        gate_slot, (row_count, local_experts, owner_count, capacity)
+    ).reshape(row_count, slot_total)
     squares = jnp.sum(widened * widened, axis=1)
     spread = jnp.broadcast_to(squares[None], (rep_count,) + squares.shape)
     squares = jnp.sum(lax.all_to_all(spread, ("ry", "rc"), 0, 0, tiled=True), axis=0)
     rinv_rows = lax.rsqrt(squares / (feat_width * rep_count) + 1e-06)
     normed = (widened * rinv_rows[:, None] * norm_gain[None, :]).astype(jnp.bfloat16)
-    slot_ids = jnp.arange(slot_total, dtype=jnp.int32)
-    slot_of = slot_index.reshape(row_count, route_count)
-    pick = jnp.sum(
-        (slot_of[None, :, :] == slot_ids[:, None, None]).astype(jnp.float32), axis=2
-    ).astype(jnp.bfloat16)
+    pick = jnp.transpose(in_slot).astype(jnp.bfloat16)
     outbound = jnp.dot(pick, normed, preferred_element_type=jnp.float32).astype(jnp.bfloat16)
     outbound = outbound.reshape(local_experts, owner_count, capacity, feat_width)
     received = lax.all_to_all(outbound, "expert", split_axis=1, concat_axis=1, tiled=True)
@@ -79,12 +83,7 @@
     )
     returned = lax.all_to_all(expert_out, "expert", split_axis=1, concat_axis=1, tiled=True)
     flat_back = returned.reshape(slot_total, feat_width)
-    combine = jnp.sum(
-        jnp.where(
-            slot_of[:, :, None] == slot_ids[None, None, :], gate_weights[:, :, None], 0.0
-        ),
-        axis=1,
-    )
+    combine = in_slot * gate_slot
     mixture = jnp.dot(
         combine,
         flat_back.astype(jnp.float32),

time: 170 us -> 172 us (1.012)
  transfers between devices with their start and end apart: 5 -> 5, of which waited for: 5 -> 4; matrix products, arithmetic and copies ran while one was open for 5% -> 5% of each run, Pallas kernels for 0% -> 0%
where the time goes in v12:
time: 172 us; the launch traced here: 171 us
  waiting for transfers between devices  67.1 us (39%)
  blocking collectives  52.2 us (30%)
  starting transfers between devices  34 us (20%)
  local copies, waits for them, and re-layouts  9.09 us (5%)
  other arithmetic  5.69 us (3%)
  matrix products  2.72 us (2%)
    all_to_all x1, waiting for transfers between devices, per_device(): lax.all_to_all(outbound, 'expert', split_axis=1, concat_axis=1, tiled=True)  32.5 us
    all_to_all x1, waiting for transfers between devices, per_device(): lax.all_to_all(expert_out, 'expert', split_axis=1, concat_axis=1, tiled=T...  30.7 us
    all_to_all x1, blocking collectives, per_device(): lax.all_to_all(leaving, 'expert', split_axis=0, concat_axis=0, tiled=True)  21.6 us
    all_to_all x1, blocking collectives, per_device(): lax.all_to_all(half_sum, 'ry', split_axis=0, concat_axis=0, tiled=True)  19.4 us
    all_to_all x1, starting transfers between devices, per_device(): lax.all_to_all(outbound, 'expert', split_axis=1, concat_axis=1, tiled=True)  18.8 us
    all_to_all x1, blocking collectives, per_device(): lax.all_to_all(act_tile, 'ry', split_axis=0, concat_axis=0, tiled=True)  11.2 us
    all_to_all x1, starting transfers between devices, per_device(): lax.all_to_all(expert_out, 'expert', split_axis=1, concat_axis=1, tiled=T...  6.91 us
    all_to_all x1, starting transfers between devices, per_device(): lax.all_to_all(spread, ('ry', 'rc'), 0, 0, tiled=True)  4.47 us
  transfers between devices with their start and end apart: 5, of which 4 were waited for; matrix products, arithmetic and copies ran while one was open for 5% of the time, Pallas kernels for 0%

profile of v12, /device:TPU:6, one launch (start us, length us, event | category | flops | bytes accessed | tf_op | source)
XLA Modules:
  0.0 171.2 jit_solution(14117990558108342181)
XLA Ops:
  0.0 1.2 fusion.5
  1.8 4.5 %all-to-all-start = ((f32[8,1,128]{2,1,0:T(1,128)}), f32[8,1,128]{2,1,0:T(1,128)S(1)}, u32[]{:S(2)}, u32[]{:S(2)}) async-start(f32[8,1,128]{2,1,0:T(1,128)} %broadcast_in_dim.31), calls=%async_computation | async-start | bytes 8192 | tf_op jit(solution)/shard_map/all_to_all | solution.py:45
  6.9 0.7 fusion.16
  7.8 0.8 fusion.14
  8.7 0.7 compare_select_fusion.1
  9.4 0.8 copy.58
  10.1 0.8 copy.62
  10.9 1.0 select_reduce_fusion
  13.5 1.0 copy.66
  14.5 18.8 %all-to-all-start.1 = ((bf16[2,64,4,512]{3,2,0,1:T(4,128)(2,1)}), bf16[2,64,4,512]{3,2,0,1:T(4,128)(2,1)S(1)}, u32[]{:S(2)}, u32[]{:S(2)}) async-start(bf16[2,64,4,512]{3,2,0,1:T(4,128)(2,1)} %copy.66), calls=%async_computation.1 | async-start | bytes 1048576 | tf_op jit(solution)/shard_map/all_to_all | solution.py:51
  33.3 32.5 %all-to-all-done.1 = bf16[2,64,4,512]{3,2,0,1:T(4,128)(2,1)S(1)} async-done(((bf16[2,64,4,512]{3,2,0,1:T(4,128)(2,1)}), bf16[2,64,4,512]{3,2,0,1:T(4,128)(2,1)S(1)}, u32[]{:S(2)}, u32[]{:S(2)}) %all-to-all-start.1) | async-done | bytes 524320 | tf_op jit(solution)/shard_map/all_to_all | solution.py:51
  66.1 0.7 fusion.22
  67.8 1.9 %collective-permute-start = (f32[4,512,128]{2,1,0:T(8,128)S(1)}, f32[4,512,128]{2,1,0:T(8,128)S(1)}, u32[]{:S(2)}, u32[]{:S(2)}) collective-permute-start(f32[4,512,128]{2,1,0:T(8,128)S(1)} %bitcast.63), channel_id=1, source_target_pairs={{0,64},{64,0},{1,65},{65,1},{2,66},{66,2},{3,67},{67,3},{4,68},{68... | collective-permute-start | bytes 3145736 | tf_op jit(solution)/shard_map/ppermute | solution.py:66
  69.7 2.6 %collective-permute-done = f32[4,512,128]{2,1,0:T(8,128)S(1)} collective-permute-done((f32[4,512,128]{2,1,0:T(8,128)S(1)}, f32[4,512,128]{2,1,0:T(8,128)S(1)}, u32[]{:S(2)}, u32[]{:S(2)}) %collective-permute-start) | collective-permute-done | bytes 1048608 | tf_op jit(solution)/shard_map/ppermute | solution.py:66
  72.5 19.4 %all_to_all.31 = f32[4,512,128]{2,1,0:T(8,128)S(1)} all-to-all(f32[4,512,128]{2,1,0:T(8,128)S(1)} %fusion.3), channel_id=1, replica_groups=mesh['ry'=4,'rc'=2,'expert'=64] {'ry'}, dimensions={0} | all-to-all | bytes 2097152 | tf_op jit(solution)/shard_map/all_to_all | solution.py:67
  92.1 11.2 %all_to_all.32 = bf16[4,512,128]{2,1,0:T(8,128)(2,1)S(1)} all-to-all(bf16[4,512,128]{2,1,0:T(8,128)(2,1)S(1)} %broadcast_in_dim.32), channel_id=1, replica_groups=mesh['ry'=4,'rc'=2,'expert'=64] {'ry'}, dimensions={0} | all-to-all | bytes 1048576 | tf_op jit(solution)/shard_map/all_to_all | solution.py:71
  103.3 1.9 %collective-permute-start.1 = (bf16[4,512,128]{2,1,0:T(8,128)(2,1)S(1)}, bf16[4,512,128]{2,1,0:T(8,128)(2,1)S(1)}, u32[]{:S(2)}, u32[]{:S(2)}) collective-permute-start(bf16[4,512,128]{2,1,0:T(8,128)(2,1)S(1)} %all_to_all.32), channel_id=1, source_target_pairs={{0,64},{64,0},{1,65},{65,1},{2,66},{66,2},{3,67},{67,3},{4,68},{68... | collective-permute-start | bytes 1572872 | tf_op jit(solution)/shard_map/ppermute | solution.py:72
  105.8 1.2 collective-permute-done.1
  107.7 1.0 copy.72
  108.6 6.9 %all-to-all-start.4 = ((bf16[2,64,4,512]{3,2,0,1:T(4,128)(2,1)}), bf16[2,64,4,512]{3,2,0,1:T(4,128)(2,1)S(1)}, u32[]{:S(2)}, u32[]{:S(2)}) async-start(bf16[2,64,4,512]{3,2,0,1:T(4,128)(2,1)} %copy.72), calls=%async_computation.4 | async-start | bytes 1048576 | tf_op jit(solution)/shard_map/all_to_all | solution.py:84
  115.7 1.0 scatter_custom_fusion
  116.8 30.7 %all-to-all-done.4 = bf16[2,64,4,512]{3,2,0,1:T(4,128)(2,1)S(1)} async-done(((bf16[2,64,4,512]{3,2,0,1:T(4,128)(2,1)}), bf16[2,64,4,512]{3,2,0,1:T(4,128)(2,1)S(1)}, u32[]{:S(2)}, u32[]{:S(2)}) %all-to-all-start.4) | async-done | bytes 524320 | tf_op jit(solution)/shard_map/all_to_all | solution.py:84
  148.9 21.6 %all_to_all.33 = f32[64,1,512]{2,1,0:T(1,128)S(1)} all-to-all(f32[64,1,512]{2,1,0:T(1,128)S(1)} %copy.75), channel_id=1, replica_groups=mesh['ry'=4,'rc'=2,'expert'=64] {'expert'}, dimensions={0} | all-to-all | bytes 262144 | tf_op jit(solution)/shard_map/all_to_all | solution.py:106
  170.5 0.7 copy.97
  (57 shorter events, 7.2 us)
Async XLA Ops:
  0.0 66.1 %copy-start = (bf16[2,512,1024]{2,1,0:T(8,128)(2,1)S(1)}, bf16[2,512,1024]{2,1,0:T(8,128)(2,1)}, u32[]{:S(2)}) copy-start(bf16[2,512,1024]{2,1,0:T(8,128)(2,1)} %param.14) | copy-start | bytes 6291460
  0.0 13.0 %copy-start.2 = (bf16[128,512]{1,0:T(8,128)(2,1)S(1)}, bf16[128,512]{1,0:T(8,128)(2,1)}, u32[]{:S(2)}) copy-start(bf16[128,512]{1,0:T(8,128)(2,1)} %param.8) | copy-start | bytes 393220
  0.0 13.0 %copy-start.8 = (f32[512]{0:T(512)S(1)}, f32[512]{0:T(512)}, u32[]{:S(2)}) copy-start(f32[512]{0:T(512)} %param.9) | copy-start | bytes 6148
  1.8 10.7 %all-to-all-start = ((f32[8,1,128]{2,1,0:T(1,128)}), f32[8,1,128]{2,1,0:T(1,128)S(1)}, u32[]{:S(2)}, u32[]{:S(2)}) async-start(f32[8,1,128]{2,1,0:T(1,128)} %broadcast_in_dim.31), calls=%async_computation | async-start | bytes 8192 | tf_op jit(solution)/shard_map/all_to_all | solution.py:45
  12.4 0.6 copy-start.3
  12.4 0.6 copy-start.5
  14.5 51.3 %all-to-all-start.1 = ((bf16[2,64,4,512]{3,2,0,1:T(4,128)(2,1)}), bf16[2,64,4,512]{3,2,0,1:T(4,128)(2,1)S(1)}, u32[]{:S(2)}, u32[]{:S(2)}) async-start(bf16[2,64,4,512]{3,2,0,1:T(4,128)(2,1)} %copy.66), calls=%async_computation.1 | async-start | bytes 1048576 | tf_op jit(solution)/shard_map/all_to_all | solution.py:51
  67.8 4.6 %collective-permute-start = (f32[4,512,128]{2,1,0:T(8,128)S(1)}, f32[4,512,128]{2,1,0:T(8,128)S(1)}, u32[]{:S(2)}, u32[]{:S(2)}) collective-permute-start(f32[4,512,128]{2,1,0:T(8,128)S(1)} %bitcast.63), channel_id=1, source_target_pairs={{0,64},{64,0},{1,65},{65,1},{2,66},{66,2},{3,67},{67,3},{4,68},{68... | collective-permute-start | bytes 3145736 | tf_op jit(solution)/shard_map/ppermute | solution.py:66
  91.9 13.3 %copy-start.1 = (bf16[2,1024,512]{2,1,0:T(8,128)(2,1)S(1)}, bf16[2,1024,512]{2,1,0:T(8,128)(2,1)}, u32[]{:S(2)}) copy-start(bf16[2,1024,512]{2,1,0:T(8,128)(2,1)} %param.15) | copy-start | bytes 6291460
  103.3 3.8 %collective-permute-start.1 = (bf16[4,512,128]{2,1,0:T(8,128)(2,1)S(1)}, bf16[4,512,128]{2,1,0:T(8,128)(2,1)S(1)}, u32[]{:S(2)}, u32[]{:S(2)}) collective-permute-start(bf16[4,512,128]{2,1,0:T(8,128)(2,1)S(1)} %all_to_all.32), channel_id=1, source_target_pairs={{0,64},{64,0},{1,65},{65,1},{2,66},{66,2},{3,67},{67,3},{4,68},{68... | collective-permute-start | bytes 1572872 | tf_op jit(solution)/shard_map/ppermute | solution.py:72
  107.5 8.1 %copy-start.7 = (f32[128,128]{1,0:T(8,128)S(1)}, f32[128,128]{1,0:T(8,128)}, u32[]{:S(2)}) copy-start(f32[128,128]{1,0:T(8,128)} %get-tuple-element.5) | copy-start | bytes 196612
  107.5 9.2 %copy-start.4 = (f32[128,2,64]{0,2,1:T(8,128)S(1)}, f32[128,2,64]{0,2,1:T(8,128)}, u32[]{:S(2)}) copy-start(f32[128,2,64]{0,2,1:T(8,128)} %copy-done.3) | copy-start | bytes 196612
  107.5 9.2 %copy-start.6 = (f32[128,2,64]{0,2,1:T(8,128)S(1)}, f32[128,2,64]{0,2,1:T(8,128)}, u32[]{:S(2)}) copy-start(f32[128,2,64]{0,2,1:T(8,128)} %copy-done.5) | copy-start | bytes 196612
  108.6 38.9 %all-to-all-start.4 = ((bf16[2,64,4,512]{3,2,0,1:T(4,128)(2,1)}), bf16[2,64,4,512]{3,2,0,1:T(4,128)(2,1)S(1)}, u32[]{:S(2)}, u32[]{:S(2)}) async-start(bf16[2,64,4,512]{3,2,0,1:T(4,128)(2,1)} %copy.72), calls=%async_computation.4 | async-start | bytes 1048576 | tf_op jit(solution)/shard_map/all_to_all | solution.py:84

commit v13 on v10

--- a/solution.py
+++ b/solution.py
@@ -48,17 +48,19 @@
     item_count = received.shape[2]
     rows_here = owner_count * item_count
     flattened = received.reshape(local_experts, rows_here, feat_width)
-    partial_value = jnp.einsum(
-        "erd,edh->erh", flattened, up_weight, preferred_element_type=jnp.float32
-    )
     core = lax.axis_index("rc")
     sibling = [(i, 1 - i) for i in range(2)]
     chips = lax.axis_size("ry")
     quarter = hid // (2 * chips)
-    pieces = partial_value.reshape(local_experts * rows_here, 2 * chips, quarter)
-    pieces = jnp.transpose(pieces, (1, 0, 2)).reshape(2, chips, local_experts * rows_here, quarter)
-    mine = lax.dynamic_index_in_dim(pieces, core, axis=0, keepdims=False)
-    theirs = lax.dynamic_index_in_dim(pieces, 1 - core, axis=0, keepdims=False)
+    up_q = up_weight.reshape(local_experts, feat_width, 2, chips, quarter)
+    up_theirs = lax.dynamic_index_in_dim(up_q, 1 - core, axis=2, keepdims=False)
+    up_mine = lax.dynamic_index_in_dim(up_q, core, axis=2, keepdims=False)
+    theirs = jnp.einsum(
+        "erd,edqj->qerj", flattened, up_theirs, preferred_element_type=jnp.float32
+    ).reshape(chips, local_experts * rows_here, quarter)
+    mine = jnp.einsum(
+        "erd,edqj->qerj", flattened, up_mine, preferred_element_type=jnp.float32
+    ).reshape(chips, local_experts * rows_here, quarter)
     half_sum = mine + lax.ppermute(theirs, "rc", sibling)
     got = lax.all_to_all(half_sum, "ry", split_axis=0, concat_axis=0, tiled=True)
     hidden_part = jnp.sum(got, axis=0)

time: 170 us -> 177 us (1.041)
  local copies, waits for them, and re-layouts: 8.83 us -> 20.5 us
  waiting for transfers between devices: 65.9 us -> 56.4 us
  matrix products: 2.31 us -> 4.55 us
    all_to_all x1, waiting for transfers between devices: 32.1 us -> 25.4 us  [per_device(): lax.all_to_all(outbound, 'expert', split_axis=1, concat_axis=1, tiled=True)]
    transpose x0 -> x2, local copies, waits for them, and re-layouts: none -> 4.1 us  [the longest x1 2.55 us: per_device(): jnp.einsum('erd,edqj->qerj', flattened, up_theirs, preferred_element_type...]
    reshape x0 -> x1, local copies, waits for them, and re-layouts: none -> 3.24 us  [per_device(): up_q = up_weight.reshape(local_experts, feat_width, 2, chips, quarter)]
    ppermute x1, waiting for transfers between devices: 2.63 us -> 0.01 us  [per_device(): half_sum = mine + lax.ppermute(theirs, 'rc', sibling)]
    dot_general x1 -> x2, matrix products: 0.71 us -> 2.96 us  [the longest x1 1.51 us: per_device(): jnp.einsum('erd,edqj->qerj', flattened, up_theirs, preferred_element_type...]
    unnamed x23 -> x21, local copies, waits for them, and re-layouts: 2.14 us -> 3.88 us
  transfers between devices with their start and end apart: 5 -> 5, of which waited for: 5 -> 4; matrix products, arithmetic and copies ran while one was open for 5% -> 10% of each run, Pallas kernels for 0% -> 0%
where the time goes in v13:
time: 177 us; the launch traced here: 176 us
  waiting for transfers between devices  56.4 us (32%)
  blocking collectives  53.3 us (30%)
  starting transfers between devices  34.2 us (19%)
  local copies, waits for them, and re-layouts  20.5 us (12%)
  other arithmetic  6.87 us (4%)
  matrix products  4.55 us (3%)
    all_to_all x1, waiting for transfers between devices, per_device(): lax.all_to_all(expert_out, 'expert', split_axis=1, concat_axis=1, tiled=T...  29.5 us
    all_to_all x1, waiting for transfers between devices, per_device(): lax.all_to_all(outbound, 'expert', split_axis=1, concat_axis=1, tiled=True)  25.4 us
    all_to_all x1, blocking collectives, per_device(): lax.all_to_all(leaving, 'expert', split_axis=0, concat_axis=0, tiled=True)  21.6 us
    all_to_all x1, blocking collectives, per_device(): lax.all_to_all(half_sum, 'ry', split_axis=0, concat_axis=0, tiled=True)  19.9 us
    all_to_all x1, starting transfers between devices, per_device(): lax.all_to_all(outbound, 'expert', split_axis=1, concat_axis=1, tiled=True)  19 us
    all_to_all x1, blocking collectives, per_device(): lax.all_to_all(act_tile, 'ry', split_axis=0, concat_axis=0, tiled=True)  11.8 us
    all_to_all x1, starting transfers between devices, per_device(): lax.all_to_all(expert_out, 'expert', split_axis=1, concat_axis=1, tiled=T...  6.91 us
    all_to_all x1, starting transfers between devices, per_device(): lax.all_to_all(spread, ('ry', 'rc'), 0, 0, tiled=True)  4.47 us
  transfers between devices with their start and end apart: 5, of which 4 were waited for; matrix products, arithmetic and copies ran while one was open for 10% of the time, Pallas kernels for 0%

profile of v13, /device:TPU:6, one launch (start us, length us, event | category | flops | bytes accessed | tf_op | source)
XLA Modules:
  0.0 176.3 jit_solution(14467760956954925120)
XLA Ops:
  0.0 1.0 fusion.9
  1.6 4.5 %all-to-all-start = ((f32[8,1,128]{2,1,0:T(1,128)}), f32[8,1,128]{2,1,0:T(1,128)S(1)}, u32[]{:S(2)}, u32[]{:S(2)}) async-start(f32[8,1,128]{2,1,0:T(1,128)} %broadcast_in_dim.67), calls=%async_computation | async-start | bytes 8192 | tf_op jit(solution)/shard_map/all_to_all | solution.py:37
  11.9 1.0 copy.111
  12.9 19.0 %all-to-all-start.1 = ((bf16[2,64,4,512]{3,2,0,1:T(4,128)(2,1)}), bf16[2,64,4,512]{3,2,0,1:T(4,128)(2,1)}, u32[]{:S(2)}, u32[]{:S(2)}) async-start(bf16[2,64,4,512]{3,2,0,1:T(4,128)(2,1)} %copy.111), calls=%async_computation.1 | async-start | bytes 1048576 | tf_op jit(solution)/shard_map/all_to_all | solution.py:47
  31.9 3.2 %reshape.165 = bf16[2,512,2,4,128]{4,3,2,1,0:T(4,128)(2,1)S(1)} reshape(bf16[2,512,1024]{2,1,0:T(8,128)(2,1)} %param.14) | data formatting | bytes 4194304 | tf_op jit(solution)/shard_map/reshape | solution.py:55
  35.2 1.7 constant_dynamic-slice_fusion.3
  36.9 1.6 copy.124
  38.5 25.4 %all-to-all-done.1 = bf16[2,64,4,512]{3,2,0,1:T(4,128)(2,1)} async-done(((bf16[2,64,4,512]{3,2,0,1:T(4,128)(2,1)}), bf16[2,64,4,512]{3,2,0,1:T(4,128)(2,1)}, u32[]{:S(2)}, u32[]{:S(2)}) %all-to-all-start.1) | async-done | bytes 524320 | tf_op jit(solution)/shard_map/all_to_all | solution.py:47
  63.9 1.2 copy.112
  65.3 1.5 convolution_bitcast_fusion.2
  66.8 2.5 %copy.115 = f32[4,2,256,128]{3,2,1,0:T(8,128)} copy(f32[4,2,256,128]{2,3,0,1:T(8,128)} %convolution_bitcast_fusion.2) | data formatting | bytes 2097152 | tf_op jit(solution)/shard_map/erd,edqj->qerj/transpose | solution.py:58
  69.3 1.9 %collective-permute-start = (f32[4,512,128]{2,1,0:T(8,128)}, f32[4,512,128]{2,1,0:T(8,128)}, u32[]{:S(2)}, u32[]{:S(2)}) collective-permute-start(f32[4,512,128]{2,1,0:T(8,128)} %bitcast.11), channel_id=1, source_target_pairs={{0,64},{64,0},{1,65},{65,1},{2,66},{66,2},{3,67},{67,3},{4,68},{68... | collective-permute-start | bytes 3145736 | tf_op jit(solution)/shard_map/ppermute | solution.py:64
  71.9 1.5 convolution_bitcast_fusion.3
  73.4 1.5 copy.113
  74.9 1.3 bitcast_add_fusion
  76.3 19.9 %all_to_all.31 = f32[4,512,128]{2,1,0:T(8,128)S(1)} all-to-all(f32[4,512,128]{2,1,0:T(8,128)S(1)} %bitcast_add_fusion), channel_id=1, replica_groups=mesh['ry'=4,'rc'=2,'expert'=64] {'ry'}, dimensions={0} | all-to-all | bytes 2097152 | tf_op jit(solution)/shard_map/all_to_all | solution.py:65
  96.4 11.8 %all_to_all.32 = bf16[4,512,128]{2,1,0:T(8,128)(2,1)S(1)} all-to-all(bf16[4,512,128]{2,1,0:T(8,128)(2,1)S(1)} %broadcast_in_dim.68), channel_id=1, replica_groups=mesh['ry'=4,'rc'=2,'expert'=64] {'ry'}, dimensions={0} | all-to-all | bytes 1048576 | tf_op jit(solution)/shard_map/all_to_all | solution.py:69
  108.2 1.9 %collective-permute-start.1 = (bf16[4,512,128]{2,1,0:T(8,128)(2,1)S(1)}, bf16[4,512,128]{2,1,0:T(8,128)(2,1)S(1)}, u32[]{:S(2)}, u32[]{:S(2)}) collective-permute-start(bf16[4,512,128]{2,1,0:T(8,128)(2,1)S(1)} %all_to_all.32), channel_id=1, source_target_pairs={{0,64},{64,0},{1,65},{65,1},{2,66},{66,2},{3,67},{67,3},{4,68},{68... | collective-permute-start | bytes 1572872 | tf_op jit(solution)/shard_map/ppermute | solution.py:70
  110.8 1.2 collective-permute-done.1
  112.6 1.0 copy.118
  113.6 6.9 %all-to-all-start.4 = ((bf16[2,64,4,512]{3,2,0,1:T(4,128)(2,1)}), bf16[2,64,4,512]{3,2,0,1:T(4,128)(2,1)S(1)}, u32[]{:S(2)}, u32[]{:S(2)}) async-start(bf16[2,64,4,512]{3,2,0,1:T(4,128)(2,1)} %copy.118), calls=%async_computation.4 | async-start | bytes 1048576 | tf_op jit(solution)/shard_map/all_to_all | solution.py:82
  121.1 1.2 scatter_custom_fusion
  123.0 29.5 %all-to-all-done.4 = bf16[2,64,4,512]{3,2,0,1:T(4,128)(2,1)S(1)} async-done(((bf16[2,64,4,512]{3,2,0,1:T(4,128)(2,1)}), bf16[2,64,4,512]{3,2,0,1:T(4,128)(2,1)S(1)}, u32[]{:S(2)}, u32[]{:S(2)}) %all-to-all-start.4) | async-done | bytes 524320 | tf_op jit(solution)/shard_map/all_to_all | solution.py:82
  154.0 21.6 %all_to_all.33 = f32[64,1,512]{2,1,0:T(1,128)S(1)} all-to-all(f32[64,1,512]{2,1,0:T(1,128)S(1)} %copy.120), channel_id=1, replica_groups=mesh['ry'=4,'rc'=2,'expert'=64] {'expert'}, dimensions={0} | all-to-all | bytes 262144 | tf_op jit(solution)/shard_map/all_to_all | solution.py:109
  (69 shorter events, 12.0 us)
Async XLA Ops:
  1.6 9.8 %all-to-all-start = ((f32[8,1,128]{2,1,0:T(1,128)}), f32[8,1,128]{2,1,0:T(1,128)S(1)}, u32[]{:S(2)}, u32[]{:S(2)}) async-start(f32[8,1,128]{2,1,0:T(1,128)} %broadcast_in_dim.67), calls=%async_computation | async-start | bytes 8192 | tf_op jit(solution)/shard_map/all_to_all | solution.py:37
  7.0 4.4 %copy-start.1 = (bf16[128,512]{1,0:T(8,128)(2,1)S(1)}, bf16[128,512]{1,0:T(8,128)(2,1)}, u32[]{:S(2)}) copy-start(bf16[128,512]{1,0:T(8,128)(2,1)} %param.8) | copy-start | bytes 393220
  7.0 4.4 %copy-start.6 = (f32[512]{0:T(512)S(1)}, f32[512]{0:T(512)}, u32[]{:S(2)}) copy-start(f32[512]{0:T(512)} %param.9) | copy-start | bytes 6148
  10.1 1.3 copy-start.2
  12.9 51.0 %all-to-all-start.1 = ((bf16[2,64,4,512]{3,2,0,1:T(4,128)(2,1)}), bf16[2,64,4,512]{3,2,0,1:T(4,128)(2,1)}, u32[]{:S(2)}, u32[]{:S(2)}) async-start(bf16[2,64,4,512]{3,2,0,1:T(4,128)(2,1)} %copy.111), calls=%async_computation.1 | async-start | bytes 1048576 | tf_op jit(solution)/shard_map/all_to_all | solution.py:47
  69.3 5.6 %collective-permute-start = (f32[4,512,128]{2,1,0:T(8,128)}, f32[4,512,128]{2,1,0:T(8,128)}, u32[]{:S(2)}, u32[]{:S(2)}) collective-permute-start(f32[4,512,128]{2,1,0:T(8,128)} %bitcast.11), channel_id=1, source_target_pairs={{0,64},{64,0},{1,65},{65,1},{2,66},{66,2},{3,67},{67,3},{4,68},{68... | collective-permute-start | bytes 3145736 | tf_op jit(solution)/shard_map/ppermute | solution.py:64
  96.2 14.0 %copy-start = (bf16[2,1024,512]{2,1,0:T(8,128)(2,1)S(1)}, bf16[2,1024,512]{2,1,0:T(8,128)(2,1)}, u32[]{:S(2)}) copy-start(bf16[2,1024,512]{2,1,0:T(8,128)(2,1)} %param.15) | copy-start | bytes 6291460
  108.2 3.8 %collective-permute-start.1 = (bf16[4,512,128]{2,1,0:T(8,128)(2,1)S(1)}, bf16[4,512,128]{2,1,0:T(8,128)(2,1)S(1)}, u32[]{:S(2)}, u32[]{:S(2)}) collective-permute-start(bf16[4,512,128]{2,1,0:T(8,128)(2,1)S(1)} %all_to_all.32), channel_id=1, source_target_pairs={{0,64},{64,0},{1,65},{65,1},{2,66},{66,2},{3,67},{67,3},{4,68},{68... | collective-permute-start | bytes 1572872 | tf_op jit(solution)/shard_map/ppermute | solution.py:70
  112.4 8.1 %copy-start.5 = (f32[128,8]{0,1:T(8,128)S(1)}, f32[128,8]{0,1:T(8,128)}, u32[]{:S(2)}) copy-start(f32[128,8]{0,1:T(8,128)} %param.10) | copy-start | bytes 12292
  112.5 8.2 %copy-start.4 = (s32[128]{0:T(128)S(1)}, s32[128]{0:T(128)}, u32[]{:S(2)}) copy-start(s32[128]{0:T(128)} %param.13) | copy-start | bytes 1540
  112.5 8.6 %copy-start.7 = (s32[128]{0:T(128)S(1)}, s32[128]{0:T(128)}, u32[]{:S(2)}) copy-start(s32[128]{0:T(128)} %param.11) | copy-start | bytes 1540
  112.5 9.8 %copy-start.3 = (s32[128,8]{1,0:T(8,128)S(1)}, s32[128,8]{1,0:T(8,128)}, u32[]{:S(2)}) copy-start(s32[128,8]{1,0:T(8,128)} %copy-done.2) | copy-start | bytes 12292
  113.6 38.9 %all-to-all-start.4 = ((bf16[2,64,4,512]{3,2,0,1:T(4,128)(2,1)}), bf16[2,64,4,512]{3,2,0,1:T(4,128)(2,1)S(1)}, u32[]{:S(2)}, u32[]{:S(2)}) async-start(bf16[2,64,4,512]{3,2,0,1:T(4,128)(2,1)} %copy.118), calls=%async_computation.4 | async-start | bytes 1048576 | tf_op jit(solution)/shard_map/all_to_all | solution.py:82

commit v14 on v10

--- a/solution.py
+++ b/solution.py
@@ -42,8 +42,13 @@
     pick = jnp.sum(
         (slot_of[None, :, :] == slot_ids[:, None, None]).astype(jnp.float32), axis=2
     ).astype(jnp.bfloat16)
+    pick = jnp.transpose(
+        pick.reshape(local_experts, owner_count, capacity, row_count), (1, 0, 2, 3)
+    ).reshape(slot_total, row_count)
     outbound = jnp.dot(pick, normed, preferred_element_type=jnp.float32).astype(jnp.bfloat16)
-    outbound = outbound.reshape(local_experts, owner_count, capacity, feat_width)
+    outbound = jnp.transpose(
+        outbound.reshape(owner_count, local_experts, capacity, feat_width), (1, 0, 2, 3)
+    )
     received = lax.all_to_all(outbound, "expert", split_axis=1, concat_axis=1, tiled=True)
     item_count = received.shape[2]
     rows_here = owner_count * item_count
@@ -71,12 +76,12 @@
     down_other = lax.dynamic_index_in_dim(down_q, 1 - core, axis=1, keepdims=False)
     act_half = act_half.reshape(chips, local_experts, rows_here, quarter)
     act_other = act_other.reshape(chips, local_experts, rows_here, quarter)
+    act_half = act_half.reshape(chips, local_experts, owner_count, item_count, quarter)
+    act_other = act_other.reshape(chips, local_experts, owner_count, item_count, quarter)
     expert_out = jnp.einsum(
-        "qerj,eqjd->erd", act_half, down_mine, preferred_element_type=jnp.float32
-    ) + jnp.einsum("qerj,eqjd->erd", act_other, down_other, preferred_element_type=jnp.float32)
-    expert_out = expert_out.astype(jnp.bfloat16).reshape(
-        local_experts, owner_count, item_count, feat_width
-    )
+        "qeocj,eqjd->oecd", act_half, down_mine, preferred_element_type=jnp.float32
+    ) + jnp.einsum("qeocj,eqjd->oecd", act_other, down_other, preferred_element_type=jnp.float32)
+    expert_out = jnp.transpose(expert_out.astype(jnp.bfloat16), (1, 0, 2, 3))
     returned = lax.all_to_all(expert_out, "expert", split_axis=1, concat_axis=1, tiled=True)
     flat_back = returned.reshape(slot_total, feat_width)
     combine = jnp.sum(

time: 170 us -> 172 us (1.012)
  transfers between devices with their start and end apart: 5 -> 5, of which waited for: 5 -> 5; matrix products, arithmetic and copies ran while one was open for 5% -> 4% of each run, Pallas kernels for 0% -> 0%
where the time goes in v14:
time: 172 us; the launch traced here: 171 us
  waiting for transfers between devices  66.1 us (38%)
  blocking collectives  52.2 us (30%)
  starting transfers between devices  34 us (20%)
  local copies, waits for them, and re-layouts  8.59 us (5%)
  other arithmetic  5.81 us (3%)
  matrix products  3.92 us (2%)
    all_to_all x1, waiting for transfers between devices, per_device(): lax.all_to_all(outbound, 'expert', split_axis=1, concat_axis=1, tiled=True)  32.1 us
    all_to_all x1, waiting for transfers between devices, per_device(): lax.all_to_all(expert_out, 'expert', split_axis=1, concat_axis=1, tiled=T...  29.7 us
    all_to_all x1, blocking collectives, per_device(): lax.all_to_all(leaving, 'expert', split_axis=0, concat_axis=0, tiled=True)  21.6 us
    all_to_all x1, blocking collectives, per_device(): lax.all_to_all(half_sum, 'ry', split_axis=0, concat_axis=0, tiled=True)  19.5 us
    all_to_all x1, starting transfers between devices, per_device(): lax.all_to_all(outbound, 'expert', split_axis=1, concat_axis=1, tiled=True)  18.8 us
    all_to_all x1, blocking collectives, per_device(): lax.all_to_all(act_tile, 'ry', split_axis=0, concat_axis=0, tiled=True)  11 us
    all_to_all x1, starting transfers between devices, per_device(): lax.all_to_all(expert_out, 'expert', split_axis=1, concat_axis=1, tiled=T...  6.91 us
    all_to_all x1, starting transfers between devices, per_device(): lax.all_to_all(spread, ('ry', 'rc'), 0, 0, tiled=True)  4.47 us
  transfers between devices with their start and end apart: 5, of which 5 were waited for; matrix products, arithmetic and copies ran while one was open for 4% of the time, Pallas kernels for 0%

profile of v14, /device:TPU:6, one launch (start us, length us, event | category | flops | bytes accessed | tf_op | source)
XLA Modules:
  0.0 171.0 jit_solution(9645358996631794730)
XLA Ops:
  0.0 1.2 fusion.12
  1.8 4.5 %all-to-all-start = ((f32[8,1,128]{2,1,0:T(1,128)}), f32[8,1,128]{2,1,0:T(1,128)S(1)}, u32[]{:S(2)}, u32[]{:S(2)}) async-start(f32[8,1,128]{2,1,0:T(1,128)} %broadcast_in_dim.67), calls=%async_computation | async-start | bytes 8192 | tf_op jit(solution)/shard_map/all_to_all | solution.py:37
  6.2 0.8 copy.92
  7.2 0.7 broadcast_subtract_fusion
  7.9 0.7 broadcast_compare_fusion
  10.3 0.9 convert_reduce_fusion
  11.9 0.9 reshape.160
  12.9 18.8 %all-to-all-start.1 = ((bf16[2,64,4,512]{3,2,0,1:T(4,128)(2,1)}), bf16[2,64,4,512]{3,2,0,1:T(4,128)(2,1)S(1)}, u32[]{:S(2)}, u32[]{:S(2)}) async-start(bf16[2,64,4,512]{3,2,0,1:T(4,128)(2,1)} %bitcast.8), calls=%async_computation.1 | async-start | bytes 1048576 | tf_op jit(solution)/shard_map/all_to_all | solution.py:52
  31.7 32.1 %all-to-all-done.1 = bf16[2,64,4,512]{3,2,0,1:T(4,128)(2,1)S(1)} async-done(((bf16[2,64,4,512]{3,2,0,1:T(4,128)(2,1)}), bf16[2,64,4,512]{3,2,0,1:T(4,128)(2,1)S(1)}, u32[]{:S(2)}, u32[]{:S(2)}) %all-to-all-start.1) | async-done | bytes 524320 | tf_op jit(solution)/shard_map/all_to_all | solution.py:52
  64.1 2.3 %fusion.37 = f32[2,256,1024]{2,1,0:T(8,128)S(1)} fusion(bf16[2,256,512]{2,1,0:T(8,128)(2,1)S(1)} %reshape.161, bf16[2,512,1024]{2,1,0:T(8,128)(2,1)} %param.14), kind=kOutput, calls=%fused_computation.75 | convolution fusion | flops 536870912 | bytes 4718592 | tf_op jit(solution)/shard_map/erd,edh->erh/dot_general | solution.py:56
  67.4 1.9 %collective-permute-start = (f32[4,512,128]{2,1,0:T(8,128)S(1)}, f32[4,512,128]{2,1,0:T(8,128)S(1)}, u32[]{:S(2)}, u32[]{:S(2)}) collective-permute-start(f32[4,512,128]{2,1,0:T(8,128)S(1)} %bitcast.71), channel_id=1, source_target_pairs={{0,64},{64,0},{1,65},{65,1},{2,66},{66,2},{3,67},{67,3},{4,68},{68... | collective-permute-start | bytes 3145736 | tf_op jit(solution)/shard_map/ppermute | solution.py:67
  69.3 2.6 %collective-permute-done = f32[4,512,128]{2,1,0:T(8,128)S(1)} collective-permute-done((f32[4,512,128]{2,1,0:T(8,128)S(1)}, f32[4,512,128]{2,1,0:T(8,128)S(1)}, u32[]{:S(2)}, u32[]{:S(2)}) %collective-permute-start) | collective-permute-done | bytes 1048608 | tf_op jit(solution)/shard_map/ppermute | solution.py:67
  72.0 19.5 %all_to_all.31 = f32[4,512,128]{2,1,0:T(8,128)S(1)} all-to-all(f32[4,512,128]{2,1,0:T(8,128)S(1)} %fusion.4), channel_id=1, replica_groups=mesh['ry'=4,'rc'=2,'expert'=64] {'ry'}, dimensions={0} | all-to-all | bytes 2097152 | tf_op jit(solution)/shard_map/all_to_all | solution.py:68
  91.8 11.0 %all_to_all.32 = bf16[4,512,128]{2,1,0:T(8,128)(2,1)S(1)} all-to-all(bf16[4,512,128]{2,1,0:T(8,128)(2,1)S(1)} %broadcast_in_dim.68), channel_id=1, replica_groups=mesh['ry'=4,'rc'=2,'expert'=64] {'ry'}, dimensions={0} | all-to-all | bytes 1048576 | tf_op jit(solution)/shard_map/all_to_all | solution.py:72
  102.8 1.9 %collective-permute-start.1 = (bf16[4,512,128]{2,1,0:T(8,128)(2,1)S(1)}, bf16[4,512,128]{2,1,0:T(8,128)(2,1)S(1)}, u32[]{:S(2)}, u32[]{:S(2)}) collective-permute-start(bf16[4,512,128]{2,1,0:T(8,128)(2,1)S(1)} %all_to_all.32), channel_id=1, source_target_pairs={{0,64},{64,0},{1,65},{65,1},{2,66},{66,2},{3,67},{67,3},{4,68},{68... | collective-permute-start | bytes 1572872 | tf_op jit(solution)/shard_map/ppermute | solution.py:73
  105.2 1.4 collective-permute-done.1
  107.1 1.2 copy.112
  108.3 6.9 %all-to-all-start.4 = ((bf16[2,64,4,512]{3,2,0,1:T(4,128)(2,1)}), bf16[2,64,4,512]{3,2,0,1:T(4,128)(2,1)S(1)}, u32[]{:S(2)}, u32[]{:S(2)}) async-start(bf16[2,64,4,512]{3,2,0,1:T(4,128)(2,1)} %copy.112), calls=%async_computation.4 | async-start | bytes 1048576 | tf_op jit(solution)/shard_map/all_to_all | solution.py:85
  115.8 1.0 scatter_custom_fusion
  116.8 0.7 select_reduce_fusion
  117.5 29.7 %all-to-all-done.4 = bf16[2,64,4,512]{3,2,0,1:T(4,128)(2,1)S(1)} async-done(((bf16[2,64,4,512]{3,2,0,1:T(4,128)(2,1)}), bf16[2,64,4,512]{3,2,0,1:T(4,128)(2,1)S(1)}, u32[]{:S(2)}, u32[]{:S(2)}) %all-to-all-start.4) | async-done | bytes 524320 | tf_op jit(solution)/shard_map/all_to_all | solution.py:85
  147.9 0.7 gather_fusion
  148.7 21.6 %all_to_all.33 = f32[64,1,512]{2,1,0:T(1,128)S(1)} all-to-all(f32[64,1,512]{2,1,0:T(1,128)S(1)} %copy.114), channel_id=1, replica_groups=mesh['ry'=4,'rc'=2,'expert'=64] {'expert'}, dimensions={0} | all-to-all | bytes 262144 | tf_op jit(solution)/shard_map/all_to_all | solution.py:112
  170.3 0.7 copy.135
  (63 shorter events, 7.0 us)
Async XLA Ops:
  0.0 104.7 %copy-start = (bf16[2,1024,512]{2,1,0:T(8,128)(2,1)S(1)}, bf16[2,1024,512]{2,1,0:T(8,128)(2,1)}, u32[]{:S(2)}) copy-start(bf16[2,1024,512]{2,1,0:T(8,128)(2,1)} %param.15) | copy-start | bytes 6291460
  1.8 9.8 %all-to-all-start = ((f32[8,1,128]{2,1,0:T(1,128)}), f32[8,1,128]{2,1,0:T(1,128)S(1)}, u32[]{:S(2)}, u32[]{:S(2)}) async-start(f32[8,1,128]{2,1,0:T(1,128)} %broadcast_in_dim.67), calls=%async_computation | async-start | bytes 8192 | tf_op jit(solution)/shard_map/all_to_all | solution.py:37
  8.8 2.8 %copy-start.1 = (bf16[128,512]{1,0:T(8,128)(2,1)S(1)}, bf16[128,512]{1,0:T(8,128)(2,1)}, u32[]{:S(2)}) copy-start(bf16[128,512]{1,0:T(8,128)(2,1)} %param.8) | copy-start | bytes 393220
  8.8 2.8 %copy-start.6 = (f32[512]{0:T(512)S(1)}, f32[512]{0:T(512)}, u32[]{:S(2)}) copy-start(f32[512]{0:T(512)} %param.9) | copy-start | bytes 6148
  10.2 21.4 %copy-start.2 = (s32[128,8]{1,0:T(8,128)}, s32[128,8]{1,0:T(8,128)S(1)}, u32[]{:S(2)}) copy-start(s32[128,8]{1,0:T(8,128)S(1)} %fusion.25) | copy-start | bytes 12292
  12.9 51.0 %all-to-all-start.1 = ((bf16[2,64,4,512]{3,2,0,1:T(4,128)(2,1)}), bf16[2,64,4,512]{3,2,0,1:T(4,128)(2,1)S(1)}, u32[]{:S(2)}, u32[]{:S(2)}) async-start(bf16[2,64,4,512]{3,2,0,1:T(4,128)(2,1)} %bitcast.8), calls=%async_computation.1 | async-start | bytes 1048576 | tf_op jit(solution)/shard_map/all_to_all | solution.py:52
  67.4 4.6 %collective-permute-start = (f32[4,512,128]{2,1,0:T(8,128)S(1)}, f32[4,512,128]{2,1,0:T(8,128)S(1)}, u32[]{:S(2)}, u32[]{:S(2)}) collective-permute-start(f32[4,512,128]{2,1,0:T(8,128)S(1)} %bitcast.71), channel_id=1, source_target_pairs={{0,64},{64,0},{1,65},{65,1},{2,66},{66,2},{3,67},{67,3},{4,68},{68... | collective-permute-start | bytes 3145736 | tf_op jit(solution)/shard_map/ppermute | solution.py:67
  102.8 3.8 %collective-permute-start.1 = (bf16[4,512,128]{2,1,0:T(8,128)(2,1)S(1)}, bf16[4,512,128]{2,1,0:T(8,128)(2,1)S(1)}, u32[]{:S(2)}, u32[]{:S(2)}) collective-permute-start(bf16[4,512,128]{2,1,0:T(8,128)(2,1)S(1)} %all_to_all.32), channel_id=1, source_target_pairs={{0,64},{64,0},{1,65},{65,1},{2,66},{66,2},{3,67},{67,3},{4,68},{68... | collective-permute-start | bytes 1572872 | tf_op jit(solution)/shard_map/ppermute | solution.py:73
  106.6 8.6 %copy-start.5 = (f32[128,8]{0,1:T(8,128)S(1)}, f32[128,8]{0,1:T(8,128)}, u32[]{:S(2)}) copy-start(f32[128,8]{0,1:T(8,128)} %param.10) | copy-start | bytes 12292
  106.6 8.7 %copy-start.4 = (s32[128]{0:T(128)S(1)}, s32[128]{0:T(128)}, u32[]{:S(2)}) copy-start(s32[128]{0:T(128)} %param.13) | copy-start | bytes 1540
  106.6 9.1 %copy-start.7 = (s32[128]{0:T(128)S(1)}, s32[128]{0:T(128)}, u32[]{:S(2)}) copy-start(s32[128]{0:T(128)} %param.11) | copy-start | bytes 1540
  106.6 10.2 %copy-start.3 = (s32[128,8]{1,0:T(8,128)S(1)}, s32[128,8]{1,0:T(8,128)}, u32[]{:S(2)}) copy-start(s32[128,8]{1,0:T(8,128)} %copy-done.2) | copy-start | bytes 12292
  108.3 38.9 %all-to-all-start.4 = ((bf16[2,64,4,512]{3,2,0,1:T(4,128)(2,1)}), bf16[2,64,4,512]{3,2,0,1:T(4,128)(2,1)S(1)}, u32[]{:S(2)}, u32[]{:S(2)}) async-start(bf16[2,64,4,512]{3,2,0,1:T(4,128)(2,1)} %copy.112), calls=%async_computation.4 | async-start | bytes 1048576 | tf_op jit(solution)/shard_map/all_to_all | solution.py:85
